TPU v7x, 128 devices: a whole 4x4x4 slice. The times are simulated.
128 devices in a mesh: req: 4 (over y), head: 32 (over x, z, core).
Axes of the slice: x: 4, y: 4, z: 4, core: 2. Of those that a mesh axis runs over, the one named last changes fastest.
Arguments:
- hidden_in: bfloat16 [8192, 2048], P(('req', 'head')), may hold values from -6 to 6
- queries: bfloat16 [8192, 2048], P(('req', 'head')), may hold values from -160 to 160
- keys_values: bfloat16 [8192, 1024], P(('req', 'head')), may hold values from -10 to 10
- request_of_row: int32 [8192], P('req'), may hold values from 0 to 7, as said below
- page_route: int32 [4, 32, 4], P('req', 'head'), may hold values from 0 to 3, each once within a row
- expert_ids: int32 [8192, 6], P(('req', 'head')), may hold values from 0 to 31, all different within a row; in each aligned block of 64 rows (0 to 63, 64 to 127, ...) at most 14 rows name the same one
- expert_weights: float32 [8192, 6], P(('req', 'head')), may hold values from 0.05 to 0.5
- norm_gain: float32 [2048], replicated, may hold values from 0.25 to 1.75
- shared_gate_up: bfloat16 [2048, 2, 1408], replicated, may hold values from -0.125 to 0.125
- shared_down: bfloat16 [1408, 2048], replicated, may hold values from -0.15625 to 0.15625
- expert_gate_up: bfloat16 [32, 2, 1408, 2048], P('head', None, 'req'), may hold values from -0.125 to 0.125
- expert_down: bfloat16 [32, 1408, 2048], P('head', 'req'), may hold values from -0.15625 to 0.15625
Outputs:
- layer_out: bfloat16 [8192, 2048], P(('req', 'head'))
Inputs may be any that keep to these rules, and one draw needn't show every extreme that they name: `request_of_row`: each group of 2048 rows g holds two requests, ids 2 g then 2 g + 1, each a whole number of pages of 16 rows and at least 128 rows long. `page_route`: for every device, the groups receiving its pages form a permutation of all groups. `expert_ids`: each row names 6 different experts; among the rows of one device no expert is named more than 14 times, and some device names some expert exactly 14 times.
All inputs are finite; a program needn't handle non-finite values.
Results may differ from a plain program's by a relative error of at most 0.006.
Values may be sent and summed in bfloat16 or wider, within the bound.
No kernel may reach another device: no remote copies, remote signals or barrier semaphores. Data moves between devices by JAX's collectives and lax.ppermute only.
A program may use at most 192 MiB of HBM per device.

v0:
```python
import jax
import jax.numpy as jnp
from jax import lax
from jax.sharding import PartitionSpec as P

QUERY_HEADS = 16
KEY_VALUE_HEADS = 4
HEAD_SIZE = 128
EXPERTS = 32
TOP = 6
CAP = 14


negative_large = -1e30


def silu_mul(gate_value, upward):
    return gate_value / (1.0 + jnp.exp(-gate_value)) * upward


def expand_rows(arrived_block, gate_up):
    both_parts = jnp.einsum(
        "rhjcd,jkfd->rhjckf", arrived_block, gate_up, preferred_element_type=jnp.float32
    )
    return silu_mul(both_parts[..., 0, :], both_parts[..., 1, :]).astype(jnp.bfloat16)


def project_down(hidden, down_matrix):
    return jnp.einsum("rhjcf,jfd->rhjcd", hidden, down_matrix, preferred_element_type=jnp.float32)


def body(
    hidden_in,
    queries,
    keys_values,
    request_of_row,
    page_route,
    expert_ids,
    expert_weights,
    norm_gain,
    shared_gate_up,
    shared_down,
    expert_gate_up,
    expert_down,
):
    groups = lax.axis_size("req")
    columns = lax.axis_size("head")
    token_rows = hidden_in.shape[0]
    model_width = hidden_in.shape[1]
    page_rows = token_rows // groups
    group_ids = jnp.arange(groups, dtype=jnp.int32)
    page_dest = page_route.reshape(groups)
    matches = (page_dest[None, :] == group_ids[:, None]).astype(jnp.int32)
    dest_order = jnp.sum(matches * group_ids[None, :], axis=1)

    def by_dest(array_in):
        return jnp.take(array_in.reshape(groups, page_rows, array_in.shape[1]), dest_order, axis=0)

    moved_rows = (
        lax.all_to_all(by_dest(hidden_in), "req", split_axis=0, concat_axis=0, tiled=True),
        lax.all_to_all(by_dest(queries), "req", split_axis=0, concat_axis=0, tiled=True),
        lax.all_to_all(by_dest(keys_values), "req", split_axis=0, concat_axis=0, tiled=True),
    )
    resid = moved_rows[0].reshape(token_rows, model_width)
    rows_of_queries = moved_rows[1].reshape(token_rows, QUERY_HEADS * HEAD_SIZE)
    key_value_rows = moved_rows[2].reshape(token_rows, 2 * KEY_VALUE_HEADS * HEAD_SIZE)
    group_fraction = QUERY_HEADS // KEY_VALUE_HEADS
    key_value_width = KEY_VALUE_HEADS * HEAD_SIZE
    score_scale = HEAD_SIZE ** (-0.5)
    query_start = lax.axis_index("head") * token_rows
    segment_query = lax.dynamic_slice_in_dim(request_of_row, query_start, token_rows)
    position_query = query_start + jnp.arange(token_rows, dtype=jnp.int32)
    query_fourfold = rows_of_queries.reshape(token_rows, KEY_VALUE_HEADS, group_fraction, HEAD_SIZE)
    start_state = (
        jnp.full((KEY_VALUE_HEADS, group_fraction, token_rows), negative_large, jnp.float32),
        jnp.zeros((KEY_VALUE_HEADS, group_fraction, token_rows), jnp.float32),
        jnp.zeros((KEY_VALUE_HEADS, group_fraction, token_rows, HEAD_SIZE), jnp.float32),
    )
    kv_piece = lax.all_gather(key_value_rows, "head", axis=0, tiled=True)
    piece_rows = kv_piece.shape[0]
    rows_per_block = 512

    def one_block(block_index, carried_block):
        offset = block_index * rows_per_block
        current_block = lax.dynamic_slice_in_dim(kv_piece, offset, rows_per_block)
        block_keys = current_block[:, :key_value_width].reshape(
            rows_per_block, KEY_VALUE_HEADS, HEAD_SIZE
        )
        block_values = current_block[:, key_value_width:].reshape(
            rows_per_block, KEY_VALUE_HEADS, HEAD_SIZE
        )
        segment_key = lax.dynamic_slice_in_dim(request_of_row, offset, rows_per_block)
        position_key = offset + jnp.arange(rows_per_block, dtype=jnp.int32)
        allowed = (segment_query[:, None] == segment_key[None, :]) & (
            position_key[None, :] <= position_query[:, None]
        )
        running_max, running_sum, accumulated = carried_block
        score = (
            jnp.einsum(
                "tgqd,sgd->gqts", query_fourfold, block_keys, preferred_element_type=jnp.float32
            )
            * score_scale
        )
        masked = jnp.where(allowed, score, negative_large)
        new_max = jnp.maximum(running_max, jnp.max(masked, axis=-1))
        weights = jnp.where(allowed, jnp.exp(masked - new_max[..., None]), 0.0)
        factor = jnp.exp(running_max - new_max)
        running_sum = running_sum * factor + jnp.sum(weights, axis=-1)
        accumulated = accumulated * factor[..., None] + jnp.einsum(
            "gqts,sgd->gqtd",
            weights.astype(jnp.bfloat16),
            block_values,
            preferred_element_type=jnp.float32,
        )
        return (new_max, running_sum, accumulated)

    running_max, running_sum, accumulated = lax.fori_loop(
        0, piece_rows // rows_per_block, one_block, start_state
    )
    context = jnp.transpose(accumulated / running_sum[..., None], (2, 0, 1, 3)).reshape(
        token_rows, QUERY_HEADS * HEAD_SIZE
    )
    mixed_rows = resid.astype(jnp.float32) + context
    mean_square = jnp.mean(mixed_rows * mixed_rows, axis=1, keepdims=True)
    normed = (mixed_rows * lax.rsqrt(mean_square + 1e-06) * norm_gain).astype(jnp.bfloat16)
    pair_expert = expert_ids.reshape(-1)
    hit_table = (pair_expert[:, None] == jnp.arange(EXPERTS, dtype=jnp.int32)[None, :]).astype(
        jnp.int32
    )
    ranks = jnp.sum((jnp.cumsum(hit_table, axis=0) - 1) * hit_table, axis=1)
    slot_of = pair_expert * CAP + ranks
    slots_all = EXPERTS * CAP
    placing = jnp.arange(slots_all, dtype=jnp.int32)[:, None] == slot_of[None, :]
    placing = jnp.any(placing.reshape(slots_all, token_rows, TOP), axis=2).astype(jnp.bfloat16)
    outgoing = jnp.dot(placing, normed, preferred_element_type=jnp.float32).astype(jnp.bfloat16)
    local_experts = expert_gate_up.shape[0]
    outgoing = outgoing.reshape(columns, local_experts * CAP, model_width)
    shared_both = jnp.dot(
        normed, shared_gate_up.reshape(model_width, -1), preferred_element_type=jnp.float32
    ).reshape(token_rows, 2, -1)
    shared_hidden = silu_mul(shared_both[:, 0], shared_both[:, 1]).astype(jnp.bfloat16)
    shared_out = jnp.dot(shared_hidden, shared_down, preferred_element_type=jnp.float32)
    copies = jnp.broadcast_to(outgoing[None], (groups,) + outgoing.shape).reshape(
        groups * columns, local_experts * CAP, model_width
    )
    arrived = lax.all_to_all(copies, ("req", "head"), split_axis=0, concat_axis=0, tiled=True)
    arrived = arrived.reshape(groups, columns, local_experts, CAP, model_width)

    def per_group(arrived_group):
        hidden = expand_rows(arrived_group[None], expert_gate_up)
        return project_down(hidden, expert_down)[0].astype(jnp.bfloat16)

    partial_out = lax.map(per_group, arrived)
    returned = lax.all_to_all(
        partial_out.reshape(groups * columns, local_experts * CAP, model_width),
        ("req", "head"),
        split_axis=0,
        concat_axis=0,
        tiled=True,
    )
    summed = jnp.sum(returned.reshape(groups, slots_all, model_width).astype(jnp.float32), axis=0)
    pair_rows = jnp.take(summed, slot_of, axis=0).reshape(token_rows, TOP, model_width)
    routed = jnp.sum(pair_rows * expert_weights[:, :, None], axis=1)
    return (mixed_rows + shared_out + routed).astype(jnp.bfloat16)


def solution(mesh):
    return jax.shard_map(
        body,
        mesh=mesh,
        in_specs=(
            P(("req", "head"), None),
            P(("req", "head"), None),
            P(("req", "head"), None),
            P("req"),
            P("req", "head", None),
            P(("req", "head"), None),
            P(("req", "head"), None),
            P(),
            P(),
            P(),
            P("head", None, "req", None),
            P("head", "req", None),
        ),
        out_specs=P(("req", "head"), None),
        check_vma=False,
    )
```

profile of v0, /device:TPU:53, one launch (start us, length us, event | category | flops | bytes accessed | tf_op | source)
XLA Modules:
  0.0 414.8 jit_solution(3095983030153056360)
XLA Ops:
  8.9 6.5 %all_to_all.25 = bf16[4,16,1024]{2,1,0:T(8,128)(2,1)} all-to-all(bf16[4,16,1024]{2,1,0:T(8,128)(2,1)S(1)} %broadcast_select_fusion.2), channel_id=1, replica_groups=mesh['req'=4,'head'=32] {'req'}, dimensions={0} | all-to-all | bytes 262144 | tf_op jit(solution)/shard_map/all_to_all | solution.py:62
  18.5 5.8 %all-to-all-start.2 = ((bf16[4,16,2048]{2,1,0:T(8,128)(2,1)}), bf16[4,16,2048]{2,1,0:T(8,128)(2,1)S(1)}, u32[]{:S(2)}, u32[]{:S(2)}) async-start(bf16[4,16,2048]{2,1,0:T(8,128)(2,1)} %get-tuple-element.333), calls=%async_computation.2 | async-start | bytes 524288 | tf_op jit(solution)/shard_map/all_to_all | solution.py:61
  27.2 6.1 %all-to-all-start = ((bf16[4,16,2048]{2,1,0:T(8,128)(2,1)}), bf16[4,16,2048]{2,1,0:T(8,128)(2,1)S(1)}, u32[]{:S(2)}, u32[]{:S(2)}) async-start(bf16[4,16,2048]{2,1,0:T(8,128)(2,1)} %get-tuple-element.334), calls=%async_computation | async-start | bytes 524288 | tf_op jit(solution)/shard_map/all_to_all | solution.py:60
  36.8 27.1 %all-gather.2.cloned.1.call-done = bf16[2048,1024]{1,0:T(8,128)(2,1)} async-done(((bf16[64,1024]{1,0:T(8,128)(2,1)}), bf16[2048,1024]{1,0:T(8,128)(2,1)}) %all-gather.2.cloned.1.call-update) | async-done | bytes 4194320 | tf_op jit(solution)/shard_map/all_gather | solution.py:79
  63.9 18.9 %while.29 = (s32[]{:T(128)}, f32[4,4,64]{2,1,0:T(4,128)S(1)}, f32[4,4,64]{2,1,0:T(4,128)S(1)}, f32[4,4,64,128]{3,2,1,0:T(8,128)S(1)}, s32[64]{0:T(128)S(1)}, /*i...) while((s32[]{:T(128)}, f32[4,4,64]{2,1,0:T(4,128)S(1)}, ...), condition=%wide.region_4.6_spmd.clone, body=%wide.region_1.5_spmd.clone.sunk | while | flops 275748416 | bytes 13052903 | solution.py:117
  83.6 2.2 multiply_reduce_fusion.1
  88.9 2.5 broadcast_in_dim.109
  91.4 4.3 %broadcast_in_dim.110 = bf16[4,32,14,2048]{3,2,1,0:T(8,128)(2,1)} broadcast(bf16[32,14,2048]{2,1,0:T(8,128)(2,1)S(1)} %broadcast_in_dim.109), dimensions={1,2,3} | broadcast | bytes 9175040 | tf_op jit(solution)/shard_map/broadcast_in_dim | solution.py:143
  95.7 9.9 %all-to-all-start.3 = ((bf16[128,14,2048]{2,1,0:T(8,128)(2,1)}), bf16[128,14,2048]{2,1,0:T(8,128)(2,1)}, u32[]{:S(2)}, u32[]{:S(2)}) async-start(bf16[128,14,2048]{2,1,0:T(8,128)(2,1)} %bitcast.149), calls=%async_computation.3 | async-start | bytes 16777216 | tf_op jit(solution)/shard_map/all_to_all | solution.py:146
  105.6 104.5 %all-to-all-done.3 = bf16[128,14,2048]{2,1,0:T(8,128)(2,1)} async-done(((bf16[128,14,2048]{2,1,0:T(8,128)(2,1)}), bf16[128,14,2048]{2,1,0:T(8,128)(2,1)}, u32[]{:S(2)}, u32[]{:S(2)}) %all-to-all-start.3) | async-done | bytes 7340064 | tf_op jit(solution)/shard_map/all_to_all | solution.py:146
  210.1 10.6 %copy.95 = bf16[4,32,1,14,2048]{4,1,3,2,0:T(8,128)(2,1)} copy(bf16[4,32,1,14,2048]{4,3,1,0,2:T(8,128)(2,1)} %bitcast.32) | data formatting | bytes 14680064 | tf_op jit(solution)/shard_map/while | solution.py:153
  220.8 25.5 %while.28 = (s32[]{:T(128)}, bf16[4,32,1,14,2048]{4,1,0,3,2:T(8,128)(2,1)}, bf16[4,32,1,14,2048]{4,1,3,2,0:T(8,128)(2,1)}, bf16[1,2,352,2048]{3,2,1,0:T(8,128)(2...) while((s32[]{:T(128)}, bf16[4,32,1,14,2048]{4,1,0,3,2:T(8,128)(2,1)}, ...), condition=%wide.region_11.13_spmd, body=%wide.region_10.12_spmd.sunk | while | flops 1939474432 | bytes 10518613 | solution.py:153
  220.8 4.0 fusion.77
  224.8 2.4 fusion.78
  227.2 4.0 fusion.77
  231.2 2.4 fusion.78
  233.6 4.0 fusion.77
  237.6 2.4 fusion.78
  239.9 4.0 fusion.77
  243.9 2.4 fusion.78
  246.3 10.4 %copy.97 = bf16[128,14,2048]{2,1,0:T(8,128)(2,1)} copy(bf16[128,14,2048]{2,0,1:T(8,128)(2,1)} %bitcast.152) | data formatting | bytes 14680064 | tf_op jit(solution)/shard_map/reshape | solution.py:155
  256.8 8.5 %all-to-all-start.4 = ((bf16[128,14,2048]{2,1,0:T(8,128)(2,1)}), bf16[128,14,2048]{2,1,0:T(8,128)(2,1)}, u32[]{:S(2)}, u32[]{:S(2)}) async-start(bf16[128,14,2048]{2,1,0:T(8,128)(2,1)} %copy.97), calls=%async_computation.4 | async-start | bytes 16777216 | tf_op jit(solution)/shard_map/all_to_all | solution.py:154
  265.8 11.3 %copy.115 = bf16[256,8,2,1408]{3,1,2,0:T(8,128)(2,1)} copy(bf16[256,8,2,1408]{3,2,1,0:T(2,128)(2,1)} %bitcast.151) | data formatting | bytes 23068672
  277.0 15.1 %copy.88 = bf16[2816,2048]{1,0:T(8,128)(2,1)} copy(bf16[2816,2048]{0,1:T(8,128)(2,1)} %bitcast.148) | data formatting | bytes 23068672 | tf_op jit(solution)/shard_map/dot_general | solution.py:138
  292.6 8.7 %fusion.51 = f32[64,2,1408]{2,0,1:T(8,128)} fusion(bf16[64,2048,1]{1,0,2:T(8,128)(2,1)S(1)} %reshape.281, bf16[2,1408,2048]{2,1,0:T(8,128)(2,1)} %bitcast.147), kind=kOutput, calls=%fused_computation.90 | convolution fusion | flops 738197504 | bytes 12517376 | tf_op jit(solution)/shard_map/dot_general | solution.py:138
  301.3 68.5 %all-to-all-done.4 = bf16[128,14,2048]{2,1,0:T(8,128)(2,1)} async-done(((bf16[128,14,2048]{2,1,0:T(8,128)(2,1)}), bf16[128,14,2048]{2,1,0:T(8,128)(2,1)}, u32[]{:S(2)}, u32[]{:S(2)}) %all-to-all-start.4) | async-done | bytes 7340064 | tf_op jit(solution)/shard_map/all_to_all | solution.py:154
  369.8 11.7 %reshape.235 = f32[4,448,2048]{2,1,0:T(8,128)} reshape(bf16[128,14,2048]{2,1,0:T(8,128)(2,1)} %all-to-all-done.4) | data formatting | bytes 22020096 | tf_op jit(solution)/shard_map/convert_element_type | solution.py:161
  381.5 9.0 %reduce_sum.69 = f32[448,2048]{1,0:T(8,128)} reduce(f32[4,448,2048]{2,1,0:T(8,128)} %reshape.235, f32[]{:T(128)} %constant.123.clone.1), dimensions={0}, to_apply=%region_12.14 | reduce | flops 2752512 | bytes 18350084 | tf_op jit(solution)/shard_map/reduce_sum | solution.py:161
  390.5 6.4 %gather_fusion.1 = f32[384,2048]{1,0:T(8,128)S(1)} fusion(f32[448,2048]{1,0:T(8,128)} %reduce_sum.69, s32[1024]{0:T(1024)S(1)} %pad_clamp_fusion), kind=kCustom, calls=%fused_computation.3 | custom fusion | bytes 6292992 | tf_op jit(solution)/shard_map/jit(_take)/gather | solution.py:162
  396.9 2.1 gather.15
  399.1 4.4 %multiply_reduce_fusion = f32[64,2048]{1,0:T(8,128)S(1)} fusion(f32[64,6,2048]{2,1,0:T(8,128)} %gather.15, f32[64,6]{1,0:T(8,128)S(1)} %copy.99, pred[64,6]{1,0:T(8,128)(4,1)S(1)} %copy.93), kind=kLoop, calls=%fused_computation.41 | loop fusion | flops 2228224 | bytes 3671936 | tf_op jit(solution)/shard_map/reduce_sum | solution.py:163
  403.5 4.5 %fusion.32 = bf16[64,2048]{1,0:T(8,128)(2,1)} fusion(f32[64,2048]{1,0:T(8,128)S(1)} %multiply_reduce_fusion, f32[64,2048]{1,0:T(8,128)S(1)} %copy-done.3, bf16[1408,2048]{1,0:T(8,128)(2,1)} %param.27, f32[64,2,1408]{2,0,1:T(8,128)S(1)} %copy-done.4), kind=kOutput, calls=%fused_computation.45 | convolution fusion | flops 369942528 | bytes 7798784 | tf_op jit(solution)/shard_map/dot_general | solution.py:142
  (121 shorter events, 35.0 us)
Async XLA Ops:
  6.5 9.0 %copy-start = (bf16[64,2048]{1,0:T(8,128)(2,1)S(1)}, bf16[64,2048]{1,0:T(8,128)(2,1)}, u32[]{:S(2)}) copy-start(bf16[64,2048]{1,0:T(8,128)(2,1)} %param.19) | copy-start | bytes 786436
  6.5 17.8 %copy-start.6 = (s32[64,6]{0,1:T(8,128)S(1)}, s32[64,6]{0,1:T(8,128)}, u32[]{:S(2)}) copy-start(s32[64,6]{0,1:T(8,128)} %param.23) | copy-start | bytes 4612
  6.5 57.3 %all-gather.2.cloned.1.call-start = ((), (), s32[]{:S(2)}) async-start(), calls=%async_computation.5 | async-start | bytes 4325376 | tf_op jit(solution)/shard_map/all_gather | solution.py:79
  18.5 8.7 %all-to-all-start.2 = ((bf16[4,16,2048]{2,1,0:T(8,128)(2,1)}), bf16[4,16,2048]{2,1,0:T(8,128)(2,1)S(1)}, u32[]{:S(2)}, u32[]{:S(2)}) async-start(bf16[4,16,2048]{2,1,0:T(8,128)(2,1)} %get-tuple-element.333), calls=%async_computation.2 | async-start | bytes 524288 | tf_op jit(solution)/shard_map/all_to_all | solution.py:61
  27.2 9.2 %all-to-all-start = ((bf16[4,16,2048]{2,1,0:T(8,128)(2,1)}), bf16[4,16,2048]{2,1,0:T(8,128)(2,1)S(1)}, u32[]{:S(2)}, u32[]{:S(2)}) async-start(bf16[4,16,2048]{2,1,0:T(8,128)(2,1)} %get-tuple-element.334), calls=%async_computation | async-start | bytes 524288 | tf_op jit(solution)/shard_map/all_to_all | solution.py:60
  82.8 0.8 copy-start.5
  82.8 4.1 copy-start.7
  86.1 0.8 copy-start.2
  95.7 114.4 %all-to-all-start.3 = ((bf16[128,14,2048]{2,1,0:T(8,128)(2,1)}), bf16[128,14,2048]{2,1,0:T(8,128)(2,1)}, u32[]{:S(2)}, u32[]{:S(2)}) async-start(bf16[128,14,2048]{2,1,0:T(8,128)(2,1)} %bitcast.149), calls=%async_computation.3 | async-start | bytes 16777216 | tf_op jit(solution)/shard_map/all_to_all | solution.py:146
  210.1 10.6 %copy-start.9 = (bf16[1,352,2048]{2,1,0:T(8,128)(2,1)S(1)}, bf16[1,352,2048]{2,1,0:T(8,128)(2,1)}, u32[]{:S(2)}) copy-start(bf16[1,352,2048]{2,1,0:T(8,128)(2,1)} %param.29) | copy-start | bytes 4325380
  256.8 8.8 %copy-start.8 = (f32[64,6]{0,1:T(8,128)S(1)}, f32[64,6]{0,1:T(8,128)}, u32[]{:S(2)}) copy-start(f32[64,6]{0,1:T(8,128)} %param.24) | copy-start | bytes 4612
  256.8 113.1 %all-to-all-start.4 = ((bf16[128,14,2048]{2,1,0:T(8,128)(2,1)}), bf16[128,14,2048]{2,1,0:T(8,128)(2,1)}, u32[]{:S(2)}, u32[]{:S(2)}) async-start(bf16[128,14,2048]{2,1,0:T(8,128)(2,1)} %copy.97), calls=%async_computation.4 | async-start | bytes 16777216 | tf_op jit(solution)/shard_map/all_to_all | solution.py:154
  399.1 4.4 %copy-start.3 = (f32[64,2048]{1,0:T(8,128)S(1)}, f32[64,2048]{1,0:T(8,128)}, u32[]{:S(2)}) copy-start(f32[64,2048]{1,0:T(8,128)} %copy-done.2) | copy-start | bytes 1572868
  399.1 4.5 %copy-start.4 = (f32[64,2,1408]{2,0,1:T(8,128)S(1)}, f32[64,2,1408]{2,0,1:T(8,128)}, u32[]{:S(2)}) copy-start(f32[64,2,1408]{2,0,1:T(8,128)} %fusion.51) | copy-start | bytes 2162692
  399.1 8.9 %copy-start.1 = (bf16[64,2048]{1,0:T(8,128)(2,1)S(1)}, bf16[64,2048]{1,0:T(8,128)(2,1)}, u32[]{:S(2)}) copy-start(bf16[64,2048]{1,0:T(8,128)(2,1)} %param.19) | copy-start | bytes 786436
Sparse Core Ops, SparseCore 0:
  15.6 48.2 all-gather.1
where the time goes:
time: 417 us; the launch traced here: 415 us
  waiting for transfers between devices  203 us (49%)
  local copies, waits for them, and re-layouts  92.5 us (22%)
  matrix products  46.1 us (11%)
  starting transfers between devices  30.3 us (7%)
  other arithmetic  22.3 us (5%)
  between operations  13.7 us (3%)
  blocking collectives  6.54 us (2%)
    all_to_all x1, waiting for transfers between devices, body(): lax.all_to_all(copies, ('req', 'head'), split_axis=0, concat_axis=0, tile...  105 us
    all_to_all x1, waiting for transfers between devices, body(): lax.all_to_all(partial_out.reshape(groups * columns, local_experts * CAP,...  68.5 us
    all_gather x1, waiting for transfers between devices, body(): kv_piece = lax.all_gather(key_value_rows, 'head', axis=0, tiled=True)  27.1 us
    dot_general x4, matrix products, expand_rows(): jnp.einsum('rhjcd,jkfd->rhjckf', arrived_block, gate_up, preferred_elemen...  16 us
    dot_general x1, local copies, waits for them, and re-layouts, body(): jnp.dot(normed, shared_gate_up.reshape(model_width, -1), preferred_elemen...  15.1 us
    unnamed x24, local copies, waits for them, and re-layouts  13 us
    convert_element_type x1, local copies, waits for them, and re-layouts, body(): returned.reshape(groups, slots_all, model_width).astype(jnp.float32)  11.7 us
    while x1, local copies, waits for them, and re-layouts, body(): partial_out = lax.map(per_group, arrived)  10.6 us
  transfers between devices with their start and end apart: 5, of which 5 were waited for; matrix products, arithmetic and copies ran while one was open for 10% of the time, Pallas kernels for 0%

commit v1 on v0

--- a/solution.py
+++ b/solution.py
@@ -16,17 +16,6 @@
 
 def silu_mul(gate_value, upward):
     return gate_value / (1.0 + jnp.exp(-gate_value)) * upward
-
-
-def expand_rows(arrived_block, gate_up):
-    both_parts = jnp.einsum(
-        "rhjcd,jkfd->rhjckf", arrived_block, gate_up, preferred_element_type=jnp.float32
-    )
-    return silu_mul(both_parts[..., 0, :], both_parts[..., 1, :]).astype(jnp.bfloat16)
-
-
-def project_down(hidden, down_matrix):
-    return jnp.einsum("rhjcf,jfd->rhjcd", hidden, down_matrix, preferred_element_type=jnp.float32)
 
 
 def body(
@@ -56,14 +45,13 @@
     def by_dest(array_in):
         return jnp.take(array_in.reshape(groups, page_rows, array_in.shape[1]), dest_order, axis=0)
 
-    moved_rows = (
-        lax.all_to_all(by_dest(hidden_in), "req", split_axis=0, concat_axis=0, tiled=True),
-        lax.all_to_all(by_dest(queries), "req", split_axis=0, concat_axis=0, tiled=True),
-        lax.all_to_all(by_dest(keys_values), "req", split_axis=0, concat_axis=0, tiled=True),
-    )
-    resid = moved_rows[0].reshape(token_rows, model_width)
-    rows_of_queries = moved_rows[1].reshape(token_rows, QUERY_HEADS * HEAD_SIZE)
-    key_value_rows = moved_rows[2].reshape(token_rows, 2 * KEY_VALUE_HEADS * HEAD_SIZE)
+    widths = (hidden_in.shape[1], queries.shape[1], keys_values.shape[1])
+    packed = jnp.concatenate((hidden_in, queries, keys_values), axis=1)
+    moved = lax.all_to_all(by_dest(packed), "req", split_axis=0, concat_axis=0, tiled=True)
+    moved = moved.reshape(token_rows, sum(widths))
+    resid = moved[:, : widths[0]]
+    rows_of_queries = moved[:, widths[0] : widths[0] + widths[1]]
+    key_value_rows = moved[:, widths[0] + widths[1] :]
     group_fraction = QUERY_HEADS // KEY_VALUE_HEADS
     key_value_width = KEY_VALUE_HEADS * HEAD_SIZE
     score_scale = HEAD_SIZE ** (-0.5)
@@ -140,27 +128,27 @@
     ).reshape(token_rows, 2, -1)
     shared_hidden = silu_mul(shared_both[:, 0], shared_both[:, 1]).astype(jnp.bfloat16)
     shared_out = jnp.dot(shared_hidden, shared_down, preferred_element_type=jnp.float32)
-    copies = jnp.broadcast_to(outgoing[None], (groups,) + outgoing.shape).reshape(
-        groups * columns, local_experts * CAP, model_width
+    at_expert = lax.all_to_all(outgoing, "head", split_axis=0, concat_axis=0, tiled=True)
+    gathered = lax.all_gather(at_expert, "req", axis=0, tiled=True)
+    expert_rows = gathered.reshape(-1, model_width)
+    both_parts = jnp.einsum(
+        "nd,kfd->nkf", expert_rows, expert_gate_up[0], preferred_element_type=jnp.float32
     )
-    arrived = lax.all_to_all(copies, ("req", "head"), split_axis=0, concat_axis=0, tiled=True)
-    arrived = arrived.reshape(groups, columns, local_experts, CAP, model_width)
-
-    def per_group(arrived_group):
-        hidden = expand_rows(arrived_group[None], expert_gate_up)
-        return project_down(hidden, expert_down)[0].astype(jnp.bfloat16)
-
-    partial_out = lax.map(per_group, arrived)
+    hidden = silu_mul(both_parts[:, 0], both_parts[:, 1]).astype(jnp.bfloat16)
+    part_out = jnp.dot(hidden, expert_down[0], preferred_element_type=jnp.float32).astype(
+        jnp.bfloat16
+    )
+    part_sum = lax.psum_scatter(part_out, "req", scatter_dimension=0, tiled=True)
     returned = lax.all_to_all(
-        partial_out.reshape(groups * columns, local_experts * CAP, model_width),
-        ("req", "head"),
+        part_sum.reshape(columns, local_experts * CAP, model_width),
+        "head",
         split_axis=0,
         concat_axis=0,
         tiled=True,
     )
-    summed = jnp.sum(returned.reshape(groups, slots_all, model_width).astype(jnp.float32), axis=0)
+    summed = returned.reshape(slots_all, model_width)
     pair_rows = jnp.take(summed, slot_of, axis=0).reshape(token_rows, TOP, model_width)
-    routed = jnp.sum(pair_rows * expert_weights[:, :, None], axis=1)
+    routed = jnp.sum(pair_rows.astype(jnp.float32) * expert_weights[:, :, None], axis=1)
     return (mixed_rows + shared_out + routed).astype(jnp.bfloat16)
 
 

time: 417 us -> 422 us (1.012)
  blocking collectives: 6.54 us -> 44.3 us
  waiting for transfers between devices: 203 us -> 171 us
  starting transfers between devices: 30.3 us -> 8.27 us
  local copies, waits for them, and re-layouts: 92.5 us -> 113 us
  matrix products: 46.1 us -> 40.1 us
    all_to_all x4 -> x1, waiting for transfers between devices: 176 us -> 0.01 us  [body(): lax.all_to_all(part_sum.reshape(columns, local_experts * CAP, model_width...]
    all_gather x0 -> x1, waiting for transfers between devices: none -> 73.6 us  [body(): gathered = lax.all_gather(at_expert, 'req', axis=0, tiled=True)]
    reduce_scatter x0 -> x1, waiting for transfers between devices: none -> 72.5 us  [body(): lax.psum_scatter(part_out, 'req', scatter_dimension=0, tiled=True)]
    all_to_all x1 -> x2, blocking collectives: 6.54 us -> 44.3 us  [the longest x1 32.9 us: body(): lax.all_to_all(outgoing, 'head', split_axis=0, concat_axis=0, tiled=True)]
    all_to_all x4 -> x1, starting transfers between devices: 30.3 us -> 8.01 us  [body(): lax.all_to_all(part_sum.reshape(columns, local_experts * CAP, model_width...]
    convert_element_type x3 -> x0, local copies, waits for them, and re-layouts: 12.3 us -> none  [the longest x1 11.7 us: body(): returned.reshape(groups, slots_all, model_width).astype(jnp.float32)]
    reshape x1 -> x5, local copies, waits for them, and re-layouts: 10.4 us -> 22.1 us  [the longest x1 10.5 us: body(): expert_rows = gathered.reshape(-1, model_width)]
    dot_general x8 -> x2, matrix products: 25.5 us -> 14.8 us  [the longest x1 8.6 us: body(): jnp.einsum('nd,kfd->nkf', expert_rows, expert_gate_up[0], preferred_eleme...]
  transfers between devices with their start and end apart: 5 -> 4, of which waited for: 5 -> 3; matrix products, arithmetic and copies ran while one was open for 10% -> 14% of each run, Pallas kernels for 0% -> 0%
where the time goes in v1:
time: 422 us; the launch traced here: 416 us
  waiting for transfers between devices  171 us (41%)
  local copies, waits for them, and re-layouts  113 us (27%)
  blocking collectives  44.3 us (10%)
  matrix products  40.1 us (10%)
  other arithmetic  25 us (6%)
  between operations  13.3 us (3%)
  starting transfers between devices  8.27 us (2%)
    all_gather x1, waiting for transfers between devices, body(): gathered = lax.all_gather(at_expert, 'req', axis=0, tiled=True)  73.6 us
    reduce_scatter x1, waiting for transfers between devices, body(): lax.psum_scatter(part_out, 'req', scatter_dimension=0, tiled=True)  72.5 us
    all_to_all x1, blocking collectives, body(): lax.all_to_all(outgoing, 'head', split_axis=0, concat_axis=0, tiled=True)  32.9 us
    all_gather x1, waiting for transfers between devices, body(): kv_piece = lax.all_gather(key_value_rows, 'head', axis=0, tiled=True)  25.3 us
    while x36, local copies, waits for them, and re-layouts  15.5 us
    unnamed x30, local copies, waits for them, and re-layouts  15.2 us
    dot_general x1, local copies, waits for them, and re-layouts, body(): jnp.dot(normed, shared_gate_up.reshape(model_width, -1), preferred_elemen...  15.2 us
    all_to_all x1, blocking collectives, body(): lax.all_to_all(by_dest(packed), 'req', split_axis=0, concat_axis=0, tiled...  11.4 us
  transfers between devices with their start and end apart: 4, of which 3 were waited for; matrix products, arithmetic and copies ran while one was open for 14% of the time, Pallas kernels for 0%

profile of v1, /device:TPU:53, one launch (start us, length us, event | category | flops | bytes accessed | tf_op | source)
XLA Modules:
  0.0 416.1 jit_solution(10034668112566596704)
XLA Ops:
  7.5 2.0 pad_maximum_fusion
  11.3 11.4 %all_to_all.15 = bf16[4,16,5120]{2,1,0:T(8,128)(2,1)S(1)} all-to-all(bf16[4,16,5120]{2,1,0:T(8,128)(2,1)S(1)} %broadcast_select_fusion), channel_id=1, replica_groups=mesh['req'=4,'head'=32] {'req'}, dimensions={0} | all-to-all | bytes 1310720 | tf_op jit(solution)/shard_map/all_to_all | solution.py:50
  29.1 2.6 reduce-window.6
  46.4 25.3 %all-gather.3.cloned.1.call-done = bf16[2048,1024]{1,0:T(8,128)(2,1)} async-done(((bf16[64,1024]{1,0:T(8,128)(2,1)}), bf16[2048,1024]{1,0:T(8,128)(2,1)}) %all-gather.3.cloned.1.call-update) | async-done | bytes 4194320 | tf_op jit(solution)/shard_map/all_gather | solution.py:67
  71.7 43.0 %while.18 = (s32[]{:T(128)}, f32[4,4,64]{2,1,0:T(4,128)S(1)}, f32[4,4,64]{2,1,0:T(4,128)S(1)}, f32[4,4,64,128]{3,2,1,0:T(8,128)}, s32[64]{0:T(128)}, /*index=5*/...) while((s32[]{:T(128)}, f32[4,4,64]{2,1,0:T(4,128)S(1)}, ...), condition=%wide.region_4.5_spmd.clone, body=%wide.region_1.4_spmd.clone.sunk | while | flops 275748416 | bytes 19344444 | solution.py:105
  73.2 2.1 fusion.59
  75.3 2.1 copy.86
  83.9 2.1 fusion.59
  86.0 2.1 copy.86
  94.7 2.1 fusion.59
  96.8 2.1 copy.86
  105.4 2.1 fusion.59
  107.5 2.1 copy.86
  123.2 3.6 reshape.171
  126.8 32.9 %all_to_all.16 = bf16[32,14,2048]{2,1,0:T(8,128)(2,1)S(1)} all-to-all(bf16[32,14,2048]{2,1,0:T(8,128)(2,1)} %reshape.171), channel_id=1, replica_groups=mesh['req'=4,'head'=32] {'head'}, dimensions={0} | all-to-all | bytes 3670016 | tf_op jit(solution)/shard_map/all_to_all | solution.py:131
  159.8 2.3 copy.68
  162.3 73.6 %all-gather.5.cloned.1.call-done = bf16[128,14,2048]{2,0,1:T(8,128)(2,1)} async-done(((bf16[32,14,2048]{2,0,1:T(8,128)(2,1)}), bf16[128,14,2048]{2,0,1:T(8,128)(2,1)}) %all-gather.5.cloned.1.call-update) | async-done | bytes 7340048 | tf_op jit(solution)/shard_map/all_gather | solution.py:132
  235.9 10.4 %copy.69 = bf16[128,14,2048]{2,1,0:T(8,128)(2,1)} copy(bf16[128,14,2048]{2,0,1:T(8,128)(2,1)} %all-gather.5.cloned.1.call-done) | data formatting | bytes 14680064 | tf_op jit(solution)/shard_map/all_gather | solution.py:132
  246.3 10.5 %reshape.196 = bf16[1792,2048,1]{1,0,2:T(8,128)(2,1)} reshape(bf16[128,14,2048]{2,1,0:T(8,128)(2,1)} %copy.69) | data formatting | bytes 14680064 | tf_op jit(solution)/shard_map/reshape | solution.py:133
  256.8 8.6 %fusion.14 = f32[1792,2,352]{0,2,1:T(8,128)S(1)} fusion(bf16[1792,2048,1]{1,0,2:T(8,128)(2,1)} %reshape.196, bf16[1,2,352,2048]{3,2,1,0:T(8,128)(2,1)S(1)} %copy-done), kind=kOutput, calls=%fused_computation.28 | convolution fusion | flops 5167382528 | bytes 15269888 | tf_op jit(solution)/shard_map/nd,kfd->nkf/dot_general | solution.py:134
  265.4 6.2 %convolution_convert_fusion = bf16[1792,2048]{1,0:T(8,128)(2,1)} fusion(bf16[1,352,2048]{2,1,0:T(8,128)(2,1)S(1)} %copy-done.15, f32[1792,2,352]{0,2,1:T(8,128)S(1)} %fusion.14), kind=kOutput, calls=%fused_computation.25 | convolution fusion | flops 2590515200 | bytes 13828096 | tf_op jit(solution)/shard_map/dot_general | solution.py:138
  271.6 72.5 %reduce-scatter.2.cloned.1.call-done = bf16[448,2048]{1,0:T(8,128)(2,1)} async-done(((bf16[1792,2048]{1,0:T(8,128)(2,1)}), bf16[448,2048]{1,0:T(8,128)(2,1)}) %reduce-scatter.2.cloned.1.call-update) | async-done | bytes 1835024 | tf_op jit(solution)/shard_map/reduce_scatter | solution.py:141
  344.2 3.6 reshape.173
  347.8 8.0 %all-to-all-start.2 = ((bf16[32,14,2048]{2,1,0:T(8,128)(2,1)}), bf16[32,14,2048]{2,1,0:T(8,128)(2,1)}, u32[]{:S(2)}, u32[]{:S(2)}) async-start(bf16[32,14,2048]{2,1,0:T(8,128)(2,1)} %reshape.173), calls=%async_computation.3 | async-start | bytes 4194304 | tf_op jit(solution)/shard_map/all_to_all | solution.py:142
  356.3 11.3 %copy.82 = bf16[256,8,2,1408]{3,1,2,0:T(8,128)(2,1)} copy(bf16[256,8,2,1408]{3,2,1,0:T(2,128)(2,1)} %bitcast.103) | data formatting | bytes 23068672
  367.5 15.2 %copy.62 = bf16[2816,2048]{1,0:T(8,128)(2,1)} copy(bf16[2816,2048]{0,1:T(8,128)(2,1)} %bitcast.101) | data formatting | bytes 23068672 | tf_op jit(solution)/shard_map/dot_general | solution.py:126
  382.8 8.7 %fusion.25 = f32[64,2,1408]{2,0,1:T(8,128)} fusion(bf16[2,1408,2048]{2,1,0:T(8,128)(2,1)} %bitcast.100, bf16[64,2048]{1,0:T(8,128)(2,1)S(1)} %copy-done.6), kind=kOutput, calls=%fused_computation.49 | convolution fusion | flops 738197504 | bytes 12517376 | tf_op jit(solution)/shard_map/dot_general | solution.py:126
  391.5 2.5 reshape.174
  394.1 3.1 gather_fusion.1
  397.2 3.7 gather.12
  400.9 4.2 %multiply_reduce_fusion = f32[64,2048]{1,0:T(8,128)S(1)} fusion(f32[64,6]{1,0:T(8,128)S(1)} %copy.71, bf16[64,6,2048]{2,1,0:T(8,128)(2,1)} %gather.12, pred[64,6]{1,0:T(8,128)(4,1)S(1)} %copy.67), kind=kLoop, calls=%fused_computation.26 | loop fusion | flops 3014656 | bytes 2099072 | tf_op jit(solution)/shard_map/reduce_sum | solution.py:151
  405.1 4.5 %fusion.18 = bf16[64,2048]{1,0:T(8,128)(2,1)} fusion(f32[64,2048]{1,0:T(8,128)S(1)} %multiply_reduce_fusion, bf16[1408,2048]{1,0:T(8,128)(2,1)} %param.23, f32[64,2,1408]{2,0,1:T(8,128)S(1)} %copy-done.4, f32[64,2048]{1,0:T(8,128)S(1)} %reshape.167, bf16[64,5120]{1,0:T(8,128)(2,1)} %bitcast.108), kind=kOutput, calls=%fused_computation.34 | convolution fusion | flops 370204672 | bytes 8060928 | tf_op jit(solution)/shard_map/dot_general | solution.py:130
  (140 shorter events, 59.2 us)
Async XLA Ops:
  6.5 250.3 %copy-start = (bf16[1,2,352,2048]{3,2,1,0:T(8,128)(2,1)S(1)}, bf16[1,2,352,2048]{3,2,1,0:T(8,128)(2,1)}, u32[]{:S(2)}) copy-start(bf16[1,2,352,2048]{3,2,1,0:T(8,128)(2,1)} %param.24) | copy-start | bytes 8650756
  6.5 65.2 %all-gather.3.cloned.1.call-start = ((), (), s32[]{:S(2)}) async-start(), calls=%async_computation.4 | async-start | bytes 4325376 | tf_op jit(solution)/shard_map/all_gather | solution.py:67
  22.7 49.1 %copy-start.3 = (bf16[4,16,5120]{2,1,0:T(8,128)(2,1)}, bf16[4,16,5120]{2,1,0:T(8,128)(2,1)S(1)}, u32[]{:S(2)}) copy-start(bf16[4,16,5120]{2,1,0:T(8,128)(2,1)S(1)} %all_to_all.15) | copy-start | bytes 1966084
  23.4 212.5 %all-gather.5.cloned.1.call-start = ((), (), s32[]{:S(2)}) async-start(), calls=%async_computation.5 | async-start | bytes 9175040 | tf_op jit(solution)/shard_map/all_gather | solution.py:132
  78.4 2.5 copy-start.2
  78.4 2.5 copy-start.7
  81.7 0.8 copy-start.8
  89.1 2.5 copy-start.2
  89.1 2.5 copy-start.7
  92.4 0.8 copy-start.8
  99.8 2.5 copy-start.2
  99.9 2.5 copy-start.7
  103.2 0.8 copy-start.8
  110.6 2.5 copy-start.2
  110.6 2.5 copy-start.7
  113.9 0.8 copy-start.8
  114.7 4.8 %copy-start.12 = (f32[2048]{0:T(1024)S(1)}, f32[2048]{0:T(1024)}, u32[]{:S(2)}) copy-start(f32[2048]{0:T(1024)} %param.21) | copy-start | bytes 24580
  116.0 5.3 %copy-start.9 = (pred[448,64]{0,1:T(8,128)(4,1)S(1)}, pred[448,64]{0,1:T(8,128)(4,1)}, u32[]{:S(2)}) copy-start(pred[448,64]{0,1:T(8,128)(4,1)} %fusion.22) | copy-start | bytes 86020
  120.6 0.7 copy-start.5
  162.1 182.1 %reduce-scatter.2.cloned.1.call-start = ((), (), s32[]{:S(2)}) async-start(), calls=%async_computation.6 | async-start | bytes 9175040 | tf_op jit(solution)/shard_map/reduce_scatter | solution.py:141
  256.8 8.6 %copy-start.15 = (bf16[1,352,2048]{2,1,0:T(8,128)(2,1)S(1)}, bf16[1,352,2048]{2,1,0:T(8,128)(2,1)}, u32[]{:S(2)}) copy-start(bf16[1,352,2048]{2,1,0:T(8,128)(2,1)} %param.25) | copy-start | bytes 4325380
  347.8 8.0 %copy-start.10 = (s32[64,6]{0,1:T(8,128)S(1)}, s32[64,6]{0,1:T(8,128)}, u32[]{:S(2)}) copy-start(s32[64,6]{0,1:T(8,128)} %param.19) | copy-start | bytes 4612
  347.8 8.3 %copy-start.13 = (f32[64,6]{0,1:T(8,128)S(1)}, f32[64,6]{0,1:T(8,128)}, u32[]{:S(2)}) copy-start(f32[64,6]{0,1:T(8,128)} %param.20) | copy-start | bytes 4612
  347.8 8.4 %copy-start.14 = (pred[64,6]{0,1:T(8,128)(4,1)S(1)}, pred[64,6]{0,1:T(8,128)(4,1)}, u32[]{:S(2)}) copy-start(pred[64,6]{0,1:T(8,128)(4,1)} %get-tuple-element.260) | copy-start | bytes 1156
  347.8 43.7 %all-to-all-start.2 = ((bf16[32,14,2048]{2,1,0:T(8,128)(2,1)}), bf16[32,14,2048]{2,1,0:T(8,128)(2,1)}, u32[]{:S(2)}, u32[]{:S(2)}) async-start(bf16[32,14,2048]{2,1,0:T(8,128)(2,1)} %reshape.173), calls=%async_computation.3 | async-start | bytes 4194304 | tf_op jit(solution)/shard_map/all_to_all | solution.py:142
  367.5 15.2 %copy-start.11 = (s32[384]{0:T(512)S(1)}, s32[384]{0:T(512)}, u32[]{:S(2)}) copy-start(s32[384]{0:T(512)} %fusion.30) | copy-start | bytes 4612
  367.5 15.2 %copy-start.6 = (bf16[64,2048]{1,0:T(8,128)(2,1)S(1)}, bf16[64,2048]{1,0:T(8,128)(2,1)}, u32[]{:S(2)}) copy-start(bf16[64,2048]{1,0:T(8,128)(2,1)} %copy-done.5) | copy-start | bytes 786436
  400.9 4.2 %copy-start.4 = (f32[64,2,1408]{2,0,1:T(8,128)S(1)}, f32[64,2,1408]{2,0,1:T(8,128)}, u32[]{:S(2)}) copy-start(f32[64,2,1408]{2,0,1:T(8,128)} %fusion.25) | copy-start | bytes 2162692
  400.9 8.7 %copy-start.1 = (bf16[1,2,352,2048]{3,2,1,0:T(8,128)(2,1)S(1)}, bf16[1,2,352,2048]{3,2,1,0:T(8,128)(2,1)}, u32[]{:S(2)}) copy-start(bf16[1,2,352,2048]{3,2,1,0:T(8,128)(2,1)} %param.24) | copy-start | bytes 8650756
Sparse Core Ops, SparseCore 0:
  23.5 48.1 all-gather.2
  162.2 73.6 all-gather.4
  271.7 72.3 reduce-scatter.1

commit v2 on v1

v2 whole, which is shorter than its diff:
```python
import functools

import jax
import jax.numpy as jnp
from jax import lax
from jax.experimental import pallas as pl
from jax.experimental.pallas import tpu as pltpu
from jax.sharding import PartitionSpec as P

QUERY_HEADS = 16
KEY_VALUE_HEADS = 4
HEAD_SIZE = 128
EXPERTS = 32
TOP = 6
CAP = 14
SLOT = 16


negative_large = -1e30


def silu_mul(gate_value, upward):
    return gate_value / (1.0 + jnp.exp(-gate_value)) * upward


def attn_kernel(q_ref, kv_ref, segq_ref, segk_ref, posq_ref, posk_ref, out_ref, *, heads, kv_heads, size):
    allowed = (segq_ref[...] == segk_ref[...]) & (posk_ref[...] <= posq_ref[...])
    frac = heads // kv_heads
    width = kv_heads * size
    for g in range(kv_heads):
        keys = kv_ref[:, g * size:(g + 1) * size]
        values = kv_ref[:, width + g * size: width + (g + 1) * size]
        for j in range(frac):
            h = g * frac + j
            qh = q_ref[:, h * size:(h + 1) * size]
            score = lax.dot_general(qh, keys, (((1,), (1,)), ((), ())), preferred_element_type=jnp.float32) * (size ** -0.5)
            masked = jnp.where(allowed, score, -1e30)
            top = jnp.max(masked, axis=1, keepdims=True)
            weights = jnp.where(allowed, jnp.exp(masked - top), 0.0)
            total = jnp.sum(weights, axis=1, keepdims=True)
            ctx = jnp.dot(weights.astype(jnp.bfloat16), values, preferred_element_type=jnp.float32)
            out_ref[:, h * size:(h + 1) * size] = ctx / total

def attention(q, kv, segq, segk, posq, posk):
    rows = q.shape[0]
    vmem = pl.BlockSpec(memory_space=pltpu.VMEM)
    return pl.pallas_call(
        functools.partial(attn_kernel, heads=16, kv_heads=4, size=128),
        out_shape=jax.ShapeDtypeStruct((rows, q.shape[1]), jnp.float32),
        in_specs=[vmem] * 6, out_specs=vmem,
    )(q, kv, segq.reshape(rows, 1), segk.reshape(1, -1), posq.reshape(rows, 1), posk.reshape(1, -1))


def body(
    hidden_in,
    queries,
    keys_values,
    request_of_row,
    page_route,
    expert_ids,
    expert_weights,
    norm_gain,
    shared_gate_up,
    shared_down,
    expert_gate_up,
    expert_down,
):
    groups = lax.axis_size("req")
    columns = lax.axis_size("head")
    token_rows = hidden_in.shape[0]
    model_width = hidden_in.shape[1]
    page_rows = token_rows // groups
    group_ids = jnp.arange(groups, dtype=jnp.int32)
    page_dest = page_route.reshape(groups)
    matches = (page_dest[None, :] == group_ids[:, None]).astype(jnp.int32)
    dest_order = jnp.sum(matches * group_ids[None, :], axis=1)

    def by_dest(array_in):
        return jnp.take(array_in.reshape(groups, page_rows, array_in.shape[1]), dest_order, axis=0)

    widths = (hidden_in.shape[1], queries.shape[1], keys_values.shape[1])
    packed = jnp.concatenate((hidden_in, queries, keys_values), axis=1)
    moved = lax.all_to_all(by_dest(packed), "req", split_axis=0, concat_axis=0, tiled=True)
    moved = moved.reshape(token_rows, sum(widths))
    resid = moved[:, : widths[0]]
    rows_of_queries = moved[:, widths[0] : widths[0] + widths[1]]
    key_value_rows = moved[:, widths[0] + widths[1] :]
    query_start = lax.axis_index("head") * token_rows
    segment_query = lax.dynamic_slice_in_dim(request_of_row, query_start, token_rows)
    position_query = query_start + jnp.arange(token_rows, dtype=jnp.int32)
    kv_piece = lax.all_gather(key_value_rows, "head", axis=0, tiled=True)
    position_key = jnp.arange(kv_piece.shape[0], dtype=jnp.int32)
    context = attention(
        rows_of_queries, kv_piece, segment_query, request_of_row, position_query, position_key
    )
    mixed_rows = resid.astype(jnp.float32) + context
    mean_square = jnp.mean(mixed_rows * mixed_rows, axis=1, keepdims=True)
    normed = (mixed_rows * lax.rsqrt(mean_square + 1e-06) * norm_gain).astype(jnp.bfloat16)
    pair_expert = expert_ids.reshape(-1)
    hit_table = (pair_expert[:, None] == jnp.arange(EXPERTS, dtype=jnp.int32)[None, :]).astype(
        jnp.int32
    )
    ranks = jnp.sum((jnp.cumsum(hit_table, axis=0) - 1) * hit_table, axis=1)
    slot_of = pair_expert * SLOT + ranks
    slots_all = EXPERTS * SLOT
    placing = jnp.arange(slots_all, dtype=jnp.int32)[:, None] == slot_of[None, :]
    placing = jnp.any(placing.reshape(slots_all, token_rows, TOP), axis=2).astype(jnp.bfloat16)
    outgoing = jnp.dot(placing, normed, preferred_element_type=jnp.float32).astype(jnp.bfloat16)
    local_experts = expert_gate_up.shape[0]
    outgoing = outgoing.reshape(columns, local_experts * SLOT, model_width)
    shared_both = jnp.einsum(
        "td,dkf->tkf", normed, shared_gate_up, preferred_element_type=jnp.float32
    )
    shared_hidden = silu_mul(shared_both[:, 0], shared_both[:, 1]).astype(jnp.bfloat16)
    shared_out = jnp.dot(shared_hidden, shared_down, preferred_element_type=jnp.float32)
    at_expert = lax.all_to_all(outgoing, "head", split_axis=0, concat_axis=0, tiled=True)
    gathered = lax.all_gather(at_expert, "req", axis=0, tiled=True)
    expert_rows = gathered.reshape(-1, model_width)
    both_parts = jnp.einsum(
        "nd,kfd->nkf", expert_rows, expert_gate_up[0], preferred_element_type=jnp.float32
    )
    hidden = silu_mul(both_parts[:, 0], both_parts[:, 1]).astype(jnp.bfloat16)
    part_out = jnp.dot(hidden, expert_down[0], preferred_element_type=jnp.float32).astype(
        jnp.bfloat16
    )
    part_sum = lax.psum_scatter(part_out, "req", scatter_dimension=0, tiled=True)
    returned = lax.all_to_all(
        part_sum.reshape(columns, local_experts * SLOT, model_width),
        "head",
        split_axis=0,
        concat_axis=0,
        tiled=True,
    )
    summed = returned.reshape(slots_all, model_width)
    pair_rows = jnp.take(summed, slot_of, axis=0).reshape(token_rows, TOP, model_width)
    routed = jnp.sum(pair_rows.astype(jnp.float32) * expert_weights[:, :, None], axis=1)
    return (mixed_rows + shared_out + routed).astype(jnp.bfloat16)


def solution(mesh):
    return jax.shard_map(
        body,
        mesh=mesh,
        in_specs=(
            P(("req", "head"), None),
            P(("req", "head"), None),
            P(("req", "head"), None),
            P("req"),
            P("req", "head", None),
            P(("req", "head"), None),
            P(("req", "head"), None),
            P(),
            P(),
            P(),
            P("head", None, "req", None),
            P("head", "req", None),
        ),
        out_specs=P(("req", "head"), None),
        check_vma=False,
    )
```

time: 422 us -> 366 us (0.87)
  local copies, waits for them, and re-layouts: 113 us -> 22.1 us
  waiting for transfers between devices: 171 us -> 216 us
  matrix products: 40.1 us -> 28.8 us
  Pallas kernels: 0 us -> 11.2 us
  other arithmetic: 25 us -> 15.7 us
    reshape x6 -> x2, local copies, waits for them, and re-layouts: 23.4 us -> 1.47 us  [attention(): segq.reshape(rows, 1)]
    all_to_all x1, waiting for transfers between devices: 0.01 us -> 17.9 us  [body(): lax.all_to_all(part_sum.reshape(columns, local_experts * SLOT, model_widt...]
    while x36 -> x0, local copies, waits for them, and re-layouts: 15.5 us -> none
    dot_general x1 -> x0, local copies, waits for them, and re-layouts: 15.2 us -> none  [body(): jnp.dot(normed, shared_gate_up.reshape(model_width, -1), preferred_elemen...]
    unnamed x30 -> x24, local copies, waits for them, and re-layouts: 15.2 us -> 1.55 us
    dot_general x9 -> x1, matrix products: 18.9 us -> 7.26 us  [body(): jnp.einsum('td,dkf->tkf', normed, shared_gate_up, preferred_element_type=...]
    pallas_call x0 -> x1, Pallas kernels: none -> 11.2 us  [attention(): pl.pallas_call(functools.partial(attn_kernel, heads=16, kv_heads=4, size=...]
    all_gather x1 -> x0, local copies, waits for them, and re-layouts: 10.4 us -> none  [body(): gathered = lax.all_gather(at_expert, 'req', axis=0, tiled=True)]
  transfers between devices with their start and end apart: 4 -> 4, of which waited for: 3 -> 4; matrix products, arithmetic and copies ran while one was open for 14% -> 6% of each run, Pallas kernels for 0% -> 0%
where the time goes in v2:
time: 366 us; the launch traced here: 359 us
  waiting for transfers between devices  216 us (59%)
  blocking collectives  44.2 us (12%)
  matrix products  28.8 us (8%)
  local copies, waits for them, and re-layouts  22.1 us (6%)
  other arithmetic  15.7 us (4%)
  between operations  13.3 us (4%)
  Pallas kernels  11.2 us (3%)
  starting transfers between devices  8.16 us (2%)
    all_gather x1, waiting for transfers between devices, body(): gathered = lax.all_gather(at_expert, 'req', axis=0, tiled=True)  82.5 us
    reduce_scatter x1, waiting for transfers between devices, body(): lax.psum_scatter(part_out, 'req', scatter_dimension=0, tiled=True)  80.5 us
    all_gather x1, waiting for transfers between devices, body(): kv_piece = lax.all_gather(key_value_rows, 'head', axis=0, tiled=True)  34.8 us
    all_to_all x1, blocking collectives, body(): lax.all_to_all(outgoing, 'head', split_axis=0, concat_axis=0, tiled=True)  32.8 us
    all_to_all x1, waiting for transfers between devices, body(): lax.all_to_all(part_sum.reshape(columns, local_experts * SLOT, model_widt...  17.9 us
    all_to_all x1, blocking collectives, body(): lax.all_to_all(by_dest(packed), 'req', split_axis=0, concat_axis=0, tiled...  11.4 us
    pallas_call x1, Pallas kernels, attention(): pl.pallas_call(functools.partial(attn_kernel, heads=16, kv_heads=4, size=...  11.2 us
    gather x2, local copies, waits for them, and re-layouts, body(): jnp.take(summed, slot_of, axis=0).reshape(token_rows, TOP, model_width)  10.7 us
  transfers between devices with their start and end apart: 4, of which 4 were waited for; matrix products, arithmetic and copies ran while one was open for 6% of the time, Pallas kernels for 0%

profile of v2, /device:TPU:53, one launch (start us, length us, event | category | flops | bytes accessed | tf_op | source)
XLA Modules:
  0.0 359.2 jit_solution(15800062243642600386)
XLA Ops:
  6.5 0.9 select_reduce_fusion
  7.5 2.0 pad_maximum_fusion
  9.5 1.7 gather_fusion
  11.3 11.4 %all_to_all.15 = bf16[4,16,5120]{2,1,0:T(8,128)(2,1)S(1)} all-to-all(bf16[4,16,5120]{2,1,0:T(8,128)(2,1)S(1)} %broadcast_select_fusion), channel_id=1, replica_groups=mesh['req'=4,'head'=32] {'req'}, dimensions={0} | all-to-all | bytes 1310720 | tf_op jit(solution)/shard_map/all_to_all | solution.py:83
  23.5 0.7 copy.42
  24.2 0.9 eq.59
  25.1 0.9 reshape.148
  26.0 0.8 dynamic-slice_bitcast_fusion
  28.1 2.6 reduce-window.6
  30.7 1.0 slice_reduce_fusion
  31.7 0.9 fusion.17
  32.6 0.8 reduce_sum.46
  33.4 0.8 copy.45
  35.4 0.8 fusion.10
  36.2 0.7 slice.41.q_ref
  36.9 34.8 %all-gather.3.cloned.1.call-done.kv_ref = bf16[2048,1024]{1,0:T(8,128)(2,1)} async-done(((bf16[64,1024]{1,0:T(8,128)(2,1)}), bf16[2048,1024]{1,0:T(8,128)(2,1)}) %all-gather.3.cloned.1.call-update) | async-done | bytes 4194320 | tf_op jit(solution)/shard_map/all_gather | solution.py:91
  72.3 11.2 %shard_map.118 = f32[64,2048]{1,0:T(8,128)} custom-call(bf16[64,2048]{1,0:T(8,128)(2,1)} %slice.41.q_ref, bf16[2048,1024]{1,0:T(8,128)(2,1)} %all-gather.3.cloned.1.call-done.kv_ref, s32[64,1]{1,0:T(8,128)} %copy.40.segq_ref, s32[1,2048]{1,0:T(1,128)} %bitcast.68, s32[64,1]{1,0:T(8,128)} %iota_add_fusion.posq_ref, s32[1,2048]{1,0:T(1,128)} %iota.31.posk_ref), custom_call_target="tpu_custom_call" | custom-call | tf_op jit(solution)/shard_map/pallas_call | solution.py:47
  83.5 1.2 multiply_reduce_fusion.1
  84.8 1.2 multiply_convert_fusion
  86.7 1.5 convolution_convert_fusion.1
  88.2 32.8 %all_to_all.16 = bf16[32,16,2048]{2,1,0:T(8,128)(2,1)} all-to-all(bf16[32,16,2048]{2,1,0:T(8,128)(2,1)S(1)} %bitcast.60), channel_id=1, replica_groups=mesh['req'=4,'head'=32] {'head'}, dimensions={0} | all-to-all | bytes 4194304 | tf_op jit(solution)/shard_map/all_to_all | solution.py:116
  121.3 82.5 %all-gather.5.cloned.1.call-done = bf16[128,16,2048]{2,1,0:T(8,128)(2,1)} async-done(((bf16[32,16,2048]{2,1,0:T(8,128)(2,1)}), bf16[128,16,2048]{2,1,0:T(8,128)(2,1)}) %all-gather.5.cloned.1.call-update) | async-done | bytes 8388624 | tf_op jit(solution)/shard_map/all_gather | solution.py:117
  203.7 8.7 %fusion.3 = f32[2048,2,352]{0,2,1:T(8,128)S(1)} fusion(bf16[2048,2048,1]{1,0,2:T(8,128)(2,1)} %bitcast.70, bf16[1,2,352,2048]{3,2,1,0:T(8,128)(2,1)S(1)} %copy-done), kind=kOutput, calls=%fused_computation.9 | convolution fusion | flops 5905580032 | bytes 17039360 | tf_op jit(solution)/shard_map/nd,kfd->nkf/dot_general | solution.py:119
  212.4 6.9 %convolution_convert_fusion = bf16[2048,2048]{1,0:T(8,128)(2,1)} fusion(bf16[1,352,2048]{2,1,0:T(8,128)(2,1)S(1)} %copy-done.10, f32[2048,2,352]{0,2,1:T(8,128)S(1)} %fusion.3), kind=kOutput, calls=%fused_computation.4 | convolution fusion | flops 2960588800 | bytes 15597568 | tf_op jit(solution)/shard_map/dot_general | solution.py:123
  219.3 80.5 %reduce-scatter.2.cloned.1.call-done = bf16[512,2048]{1,0:T(8,128)(2,1)} async-done(((bf16[2048,2048]{1,0:T(8,128)(2,1)}), bf16[512,2048]{1,0:T(8,128)(2,1)}) %reduce-scatter.2.cloned.1.call-update) | async-done | bytes 2097168 | tf_op jit(solution)/shard_map/reduce_scatter | solution.py:126
  299.8 7.9 %all-to-all-start.2 = ((bf16[32,16,2048]{2,1,0:T(8,128)(2,1)}), bf16[32,16,2048]{2,1,0:T(8,128)(2,1)}, u32[]{:S(2)}, u32[]{:S(2)}) async-start(bf16[32,16,2048]{2,1,0:T(8,128)(2,1)} %bitcast.67), calls=%async_computation.3 | async-start | bytes 4194304 | tf_op jit(solution)/shard_map/all_to_all | solution.py:127
  308.2 7.3 %fusion = f32[64,2,1408]{2,0,1:T(8,128)} fusion(bf16[2048,2,1408]{2,1,0:T(2,128)(2,1)} %param.20, bf16[64,2048]{1,0:T(8,128)(2,1)S(1)} %copy-done.4), kind=kOutput, calls=%fused_computation.2 | convolution fusion | flops 738197504 | bytes 12517376 | tf_op jit(solution)/shard_map/td,dkf->tkf/dot_general | solution.py:111
  315.5 17.9 %all-to-all-done.2 = bf16[32,16,2048]{2,1,0:T(8,128)(2,1)} async-done(((bf16[32,16,2048]{2,1,0:T(8,128)(2,1)}), bf16[32,16,2048]{2,1,0:T(8,128)(2,1)}, u32[]{:S(2)}, u32[]{:S(2)}) %all-to-all-start.2) | async-done | bytes 2097184 | tf_op jit(solution)/shard_map/all_to_all | solution.py:127
  333.4 6.9 %gather_fusion.1 = bf16[384,2048]{1,0:T(8,128)(2,1)} fusion(bf16[512,2048]{1,0:T(8,128)(2,1)} %bitcast.18, s32[1024]{0:T(1024)S(1)} %pad_clamp_fusion), kind=kCustom, calls=%fused_computation.1 | custom fusion | bytes 3147264 | tf_op jit(solution)/shard_map/jit(_take)/gather | solution.py:135
  340.3 3.8 %gather.12 = bf16[64,6,2048]{2,1,0:T(8,128)(2,1)} reshape(bf16[384,2048]{1,0:T(8,128)(2,1)} %gather_fusion.1) | data formatting | bytes 3145728 | tf_op jit(solution)/shard_map/jit(_take)/gather | solution.py:135
  344.1 4.1 %multiply_reduce_fusion = f32[64,2048]{1,0:T(8,128)S(1)} fusion(f32[64,6]{1,0:T(8,128)S(1)} %copy.48, bf16[64,6,2048]{2,1,0:T(8,128)(2,1)} %gather.12, pred[64,6]{1,0:T(8,128)(4,1)S(1)} %copy.46), kind=kLoop, calls=%fused_computation.5 | loop fusion | flops 3014656 | bytes 2099072 | tf_op jit(solution)/shard_map/reduce_sum | solution.py:136
  348.2 4.5 %fusion.6 = bf16[64,2048]{1,0:T(8,128)(2,1)} fusion(f32[64,2048]{1,0:T(8,128)S(1)} %multiply_reduce_fusion, bf16[1408,2048]{1,0:T(8,128)(2,1)} %param.21, f32[64,2,1408]{2,0,1:T(8,128)S(1)} %copy-done.5, f32[64,2048]{1,0:T(8,128)S(1)} %copy-done.1, bf16[64,5120]{1,0:T(8,128)(2,1)} %bitcast.65), kind=kOutput, calls=%fused_computation.13 | convolution fusion | flops 370204672 | bytes 8060928 | tf_op jit(solution)/shard_map/dot_general | solution.py:115
  (47 shorter events, 5.6 us)
Async XLA Ops:
  6.5 197.2 %copy-start = (bf16[1,2,352,2048]{3,2,1,0:T(8,128)(2,1)S(1)}, bf16[1,2,352,2048]{3,2,1,0:T(8,128)(2,1)}, u32[]{:S(2)}) copy-start(bf16[1,2,352,2048]{3,2,1,0:T(8,128)(2,1)} %param.22) | copy-start | bytes 8650756
  6.5 16.9 %copy-start.6 = (s32[64,6]{0,1:T(8,128)S(1)}, s32[64,6]{0,1:T(8,128)}, u32[]{:S(2)}) copy-start(s32[64,6]{0,1:T(8,128)} %param.17) | copy-start | bytes 4612
  6.5 65.2 %all-gather.3.cloned.1.call-start = ((), (), s32[]{:S(2)}) async-start(), calls=%async_computation.4 | async-start | bytes 4325376 | tf_op jit(solution)/shard_map/all_gather | solution.py:91
  22.7 62.1 %copy-start.2 = (bf16[4,16,5120]{2,1,0:T(8,128)(2,1)}, bf16[4,16,5120]{2,1,0:T(8,128)(2,1)S(1)}, u32[]{:S(2)}) copy-start(bf16[4,16,5120]{2,1,0:T(8,128)(2,1)S(1)} %all_to_all.15) | copy-start | bytes 1966084
  23.4 180.3 %all-gather.5.cloned.1.call-start = ((), (), s32[]{:S(2)}) async-start(), calls=%async_computation.5 | async-start | bytes 10485760 | tf_op jit(solution)/shard_map/all_gather | solution.py:117
  72.3 12.4 %copy-start.7 = (f32[2048]{0:T(1024)S(1)}, f32[2048]{0:T(1024)}, u32[]{:S(2)}) copy-start(f32[2048]{0:T(1024)} %param.19) | copy-start | bytes 24580
  85.9 0.7 copy-start.3
  121.0 178.8 %reduce-scatter.2.cloned.1.call-start = ((), (), s32[]{:S(2)}) async-start(), calls=%async_computation.6 | async-start | bytes 10485760 | tf_op jit(solution)/shard_map/reduce_scatter | solution.py:126
  203.7 8.7 %copy-start.10 = (bf16[1,352,2048]{2,1,0:T(8,128)(2,1)S(1)}, bf16[1,352,2048]{2,1,0:T(8,128)(2,1)}, u32[]{:S(2)}) copy-start(bf16[1,352,2048]{2,1,0:T(8,128)(2,1)} %param.23) | copy-start | bytes 4325380
  219.3 88.7 %copy-start.9 = (pred[64,6]{0,1:T(8,128)(4,1)S(1)}, pred[64,6]{0,1:T(8,128)(4,1)}, u32[]{:S(2)}) copy-start(pred[64,6]{0,1:T(8,128)(4,1)} %get-tuple-element.5) | copy-start | bytes 1156
  219.3 88.8 %copy-start.8 = (f32[64,6]{0,1:T(8,128)S(1)}, f32[64,6]{0,1:T(8,128)}, u32[]{:S(2)}) copy-start(f32[64,6]{0,1:T(8,128)} %param.18) | copy-start | bytes 4612
  219.3 88.9 %copy-start.4 = (bf16[64,2048]{1,0:T(8,128)(2,1)S(1)}, bf16[64,2048]{1,0:T(8,128)(2,1)}, u32[]{:S(2)}) copy-start(bf16[64,2048]{1,0:T(8,128)(2,1)} %copy-done.3) | copy-start | bytes 786436
  299.8 33.6 %all-to-all-start.2 = ((bf16[32,16,2048]{2,1,0:T(8,128)(2,1)}), bf16[32,16,2048]{2,1,0:T(8,128)(2,1)}, u32[]{:S(2)}, u32[]{:S(2)}) async-start(bf16[32,16,2048]{2,1,0:T(8,128)(2,1)} %bitcast.67), calls=%async_computation.3 | async-start | bytes 4194304 | tf_op jit(solution)/shard_map/all_to_all | solution.py:127
  340.3 7.9 %copy-start.1 = (f32[64,2048]{1,0:T(8,128)S(1)}, f32[64,2048]{1,0:T(8,128)}, u32[]{:S(2)}) copy-start(f32[64,2048]{1,0:T(8,128)} %shard_map.118) | copy-start | bytes 1572868
  344.1 4.1 %copy-start.5 = (f32[64,2,1408]{2,0,1:T(8,128)S(1)}, f32[64,2,1408]{2,0,1:T(8,128)}, u32[]{:S(2)}) copy-start(f32[64,2,1408]{2,0,1:T(8,128)} %fusion) | copy-start | bytes 2162692
Sparse Core Ops, SparseCore 0:
  23.5 48.1 all-gather.2
  121.1 82.5 all-gather.4
  219.4 80.3 reduce-scatter.1

commit v3 on v2

--- a/solution.py
+++ b/solution.py
@@ -78,17 +78,18 @@
     def by_dest(array_in):
         return jnp.take(array_in.reshape(groups, page_rows, array_in.shape[1]), dest_order, axis=0)
 
-    widths = (hidden_in.shape[1], queries.shape[1], keys_values.shape[1])
-    packed = jnp.concatenate((hidden_in, queries, keys_values), axis=1)
+    moved_kv = lax.all_to_all(by_dest(keys_values), "req", split_axis=0, concat_axis=0, tiled=True)
+    key_value_rows = moved_kv.reshape(token_rows, keys_values.shape[1])
+    kv_piece = lax.all_gather(key_value_rows, "head", axis=0, tiled=True)
+    widths = (hidden_in.shape[1], queries.shape[1])
+    packed = jnp.concatenate((hidden_in, queries), axis=1)
     moved = lax.all_to_all(by_dest(packed), "req", split_axis=0, concat_axis=0, tiled=True)
     moved = moved.reshape(token_rows, sum(widths))
     resid = moved[:, : widths[0]]
-    rows_of_queries = moved[:, widths[0] : widths[0] + widths[1]]
-    key_value_rows = moved[:, widths[0] + widths[1] :]
+    rows_of_queries = moved[:, widths[0] :]
     query_start = lax.axis_index("head") * token_rows
     segment_query = lax.dynamic_slice_in_dim(request_of_row, query_start, token_rows)
     position_query = query_start + jnp.arange(token_rows, dtype=jnp.int32)
-    kv_piece = lax.all_gather(key_value_rows, "head", axis=0, tiled=True)
     position_key = jnp.arange(kv_piece.shape[0], dtype=jnp.int32)
     context = attention(
         rows_of_queries, kv_piece, segment_query, request_of_row, position_query, position_key
@@ -113,9 +114,11 @@
     )
     shared_hidden = silu_mul(shared_both[:, 0], shared_both[:, 1]).astype(jnp.bfloat16)
     shared_out = jnp.dot(shared_hidden, shared_down, preferred_element_type=jnp.float32)
-    at_expert = lax.all_to_all(outgoing, "head", split_axis=0, concat_axis=0, tiled=True)
-    gathered = lax.all_gather(at_expert, "req", axis=0, tiled=True)
-    expert_rows = gathered.reshape(-1, model_width)
+    copies = jnp.broadcast_to(outgoing[None], (groups,) + outgoing.shape).reshape(
+        groups * columns, local_experts * SLOT, model_width
+    )
+    arrived = lax.all_to_all(copies, ("req", "head"), split_axis=0, concat_axis=0, tiled=True)
+    expert_rows = arrived.reshape(-1, model_width)
     both_parts = jnp.einsum(
         "nd,kfd->nkf", expert_rows, expert_gate_up[0], preferred_element_type=jnp.float32
     )
@@ -123,17 +126,19 @@
     part_out = jnp.dot(hidden, expert_down[0], preferred_element_type=jnp.float32).astype(
         jnp.bfloat16
     )
-    part_sum = lax.psum_scatter(part_out, "req", scatter_dimension=0, tiled=True)
     returned = lax.all_to_all(
-        part_sum.reshape(columns, local_experts * SLOT, model_width),
-        "head",
+        part_out.reshape(groups * columns, local_experts * SLOT, model_width),
+        ("req", "head"),
         split_axis=0,
         concat_axis=0,
         tiled=True,
     )
-    summed = returned.reshape(slots_all, model_width)
-    pair_rows = jnp.take(summed, slot_of, axis=0).reshape(token_rows, TOP, model_width)
-    routed = jnp.sum(pair_rows.astype(jnp.float32) * expert_weights[:, :, None], axis=1)
+    returned = returned.reshape(groups, slots_all, model_width)
+    pair_sum = jnp.take(returned[0], slot_of, axis=0).astype(jnp.float32)
+    for part in range(1, groups):
+        pair_sum = pair_sum + jnp.take(returned[part], slot_of, axis=0).astype(jnp.float32)
+    pair_sum = pair_sum.reshape(token_rows, TOP, model_width)
+    routed = jnp.sum(pair_sum * expert_weights[:, :, None], axis=1)
     return (mixed_rows + shared_out + routed).astype(jnp.bfloat16)
 
 

time: 366 us -> 370 us (1.011); the launches traced: 359 us -> 369 us
  waiting for transfers between devices: 216 us -> 131 us
  blocking collectives: 44.2 us -> 112 us
  local copies, waits for them, and re-layouts: 22.1 us -> 41.8 us
  starting transfers between devices: 8.16 us -> 16.4 us
    all_gather x1 -> x0, waiting for transfers between devices: 82.5 us -> none  [body(): gathered = lax.all_gather(at_expert, 'req', axis=0, tiled=True)]
    reduce_scatter x1 -> x0, waiting for transfers between devices: 80.5 us -> none  [body(): lax.psum_scatter(part_out, 'req', scatter_dimension=0, tiled=True)]
    all_to_all x1 -> x2, waiting for transfers between devices: 17.9 us -> 97.5 us  [the longest x1 97.2 us: body(): lax.all_to_all(part_out.reshape(groups * columns, local_experts * SLOT, m...]
    all_to_all x2, blocking collectives: 44.2 us -> 112 us  [the longest x1 105 us: body(): lax.all_to_all(copies, ('req', 'head'), split_axis=0, concat_axis=0, tile...]
    gather x2 -> x4, local copies, waits for them, and re-layouts: 10.7 us -> 23.9 us  [the longest x3 17 us: body(): jnp.take(returned[part], slot_of, axis=0).astype(jnp.float32)]
    all_to_all x1 -> x2, starting transfers between devices: 7.89 us -> 16.4 us  [the longest x1 10.5 us: body(): lax.all_to_all(part_out.reshape(groups * columns, local_experts * SLOT, m...]
    add x0 -> x2, other arithmetic: none -> 6.08 us  [the longest x1 6.07 us: body(): pair_sum + jnp.take(returned[part], slot_of, axis=0).astype(jnp.float32)]
    slice x3, local copies, waits for them, and re-layouts: 2.42 us -> 6.61 us  [the longest x1 5.66 us: body(): pair_sum = jnp.take(returned[0], slot_of, axis=0).astype(jnp.float32)]
  transfers between devices with their start and end apart: 4 -> 3, of which waited for: 4 -> 3; matrix products, arithmetic and copies ran while one was open for 6% -> 4% of each run, Pallas kernels for 0% -> 0%
where the time goes in v3:
time: 370 us; the launch traced here: 369 us
  waiting for transfers between devices  131 us (35%)
  blocking collectives  112 us (30%)
  local copies, waits for them, and re-layouts  41.8 us (11%)
  matrix products  25.6 us (7%)
  other arithmetic  18.2 us (5%)
  starting transfers between devices  16.4 us (4%)
  between operations  13.6 us (4%)
  Pallas kernels  11.2 us (3%)
    all_to_all x1, blocking collectives, body(): lax.all_to_all(copies, ('req', 'head'), split_axis=0, concat_axis=0, tile...  105 us
    all_to_all x1, waiting for transfers between devices, body(): lax.all_to_all(part_out.reshape(groups * columns, local_experts * SLOT, m...  97.2 us
    all_gather x1, waiting for transfers between devices, body(): kv_piece = lax.all_gather(key_value_rows, 'head', axis=0, tiled=True)  33 us
    gather x3, local copies, waits for them, and re-layouts, body(): jnp.take(returned[part], slot_of, axis=0).astype(jnp.float32)  17 us
    pallas_call x1, Pallas kernels, attention(): pl.pallas_call(functools.partial(attn_kernel, heads=16, kv_heads=4, size=...  11.2 us
    all_to_all x1, starting transfers between devices, body(): lax.all_to_all(part_out.reshape(groups * columns, local_experts * SLOT, m...  10.5 us
  transfers between devices with their start and end apart: 3, of which 3 were waited for; matrix products, arithmetic and copies ran while one was open for 4% of the time, Pallas kernels for 0%

profile of v3, /device:TPU:53, one launch (start us, length us, event | category | flops | bytes accessed | tf_op | source)
XLA Modules:
  0.0 368.9 jit_solution(6828987820358664425)
XLA Ops:
  6.5 0.9 select_reduce_fusion
  7.5 1.5 gather_fusion.1
  9.1 6.5 %all_to_all.20 = bf16[4,16,1024]{2,1,0:T(8,128)(2,1)} all-to-all(bf16[4,16,1024]{2,1,0:T(8,128)(2,1)S(1)} %broadcast_select_fusion.1), channel_id=1, replica_groups=mesh['req'=4,'head'=32] {'req'}, dimensions={0} | all-to-all | bytes 262144 | tf_op jit(solution)/shard_map/all_to_all | solution.py:81
  15.6 1.1 pad_maximum_fusion
  16.7 1.4 gather_fusion
  18.1 1.9 broadcast_select_fusion
  20.0 5.9 %all-to-all-start = ((bf16[4,16,4096]{2,1,0:T(8,128)(2,1)}), bf16[4,16,4096]{2,1,0:T(8,128)(2,1)S(1)}, u32[]{:S(2)}, u32[]{:S(2)}) async-start(bf16[4,16,4096]{2,1,0:T(8,128)(2,1)} %broadcast_select_fusion), calls=%async_computation | async-start | bytes 1048576 | tf_op jit(solution)/shard_map/all_to_all | solution.py:86
  26.3 0.9 reduce-window.6
  28.1 0.8 dynamic-slice_bitcast_fusion
  28.9 0.7 copy.34.segq_ref
  30.4 0.7 slice.65.q_ref
  31.1 33.0 %all-gather.2.cloned.1.call-done.kv_ref = bf16[2048,1024]{1,0:T(8,128)(2,1)} async-done(((bf16[64,1024]{1,0:T(8,128)(2,1)}), bf16[2048,1024]{1,0:T(8,128)(2,1)}) %all-gather.2.cloned.1.call-update) | async-done | bytes 4194320 | tf_op jit(solution)/shard_map/all_gather | solution.py:83
  64.7 11.2 %shard_map.118 = f32[64,2048]{1,0:T(8,128)} custom-call(bf16[64,2048]{1,0:T(8,128)(2,1)} %slice.65.q_ref, bf16[2048,1024]{1,0:T(8,128)(2,1)} %all-gather.2.cloned.1.call-done.kv_ref, s32[64,1]{1,0:T(8,128)} %copy.34.segq_ref, s32[1,2048]{1,0:T(1,128)} %bitcast.81, s32[64,1]{1,0:T(8,128)} %iota_add_fusion.posq_ref, s32[1,2048]{1,0:T(1,128)} %iota.31.posk_ref), custom_call_target="tpu_custom_call" | custom-call | tf_op jit(solution)/shard_map/pallas_call | solution.py:47
  75.9 1.2 multiply_reduce_fusion.1
  77.1 1.2 multiply_convert_fusion
  78.3 0.8 convolution_convert_fusion.1
  79.0 1.1 broadcast_in_dim.49
  80.1 105.0 %all_to_all.21 = bf16[128,16,2048]{2,1,0:T(8,128)(2,1)S(1)} all-to-all(bf16[128,16,2048]{2,1,0:T(8,128)(2,1)S(1)} %bitcast.70), channel_id=1, replica_groups=mesh['req'=4,'head'=32] {'req','head'}, dimensions={0} | all-to-all | bytes 16777216 | tf_op jit(solution)/shard_map/all_to_all | solution.py:120
  185.1 6.3 %fusion.3 = f32[2048,2,352]{0,2,1:T(8,128)S(1)} fusion(bf16[2048,2048,1]{1,0,2:T(8,128)(2,1)S(1)} %bitcast.73, bf16[1,2,352,2048]{3,2,1,0:T(8,128)(2,1)S(1)} %copy-done), kind=kOutput, calls=%fused_computation.14 | convolution fusion | flops 5905580032 | bytes 17039360 | tf_op jit(solution)/shard_map/nd,kfd->nkf/dot_general | solution.py:122
  191.4 6.9 %convolution_convert_fusion = bf16[2048,2048]{1,0:T(8,128)(2,1)} fusion(bf16[1,352,2048]{2,1,0:T(8,128)(2,1)S(1)} %copy-done.9, f32[2048,2,352]{0,2,1:T(8,128)S(1)} %fusion.3), kind=kOutput, calls=%fused_computation.8 | convolution fusion | flops 2960588800 | bytes 15597568 | tf_op jit(solution)/shard_map/dot_general | solution.py:126
  198.3 10.5 %all-to-all-start.3 = ((bf16[128,16,2048]{2,1,0:T(8,128)(2,1)}), bf16[128,16,2048]{2,1,0:T(8,128)(2,1)}, u32[]{:S(2)}, u32[]{:S(2)}) async-start(bf16[128,16,2048]{2,1,0:T(8,128)(2,1)} %bitcast.72), calls=%async_computation.3 | async-start | bytes 16777216 | tf_op jit(solution)/shard_map/all_to_all | solution.py:129
  209.0 7.3 %fusion = f32[64,2,1408]{2,0,1:T(8,128)} fusion(bf16[2048,2,1408]{2,1,0:T(2,128)(2,1)} %param.22, bf16[64,2048]{1,0:T(8,128)(2,1)S(1)} %copy-done.4), kind=kOutput, calls=%fused_computation.6 | convolution fusion | flops 738197504 | bytes 12517376 | tf_op jit(solution)/shard_map/td,dkf->tkf/dot_general | solution.py:112
  216.2 97.2 %all-to-all-done.3 = bf16[128,16,2048]{2,1,0:T(8,128)(2,1)} async-done(((bf16[128,16,2048]{2,1,0:T(8,128)(2,1)}), bf16[128,16,2048]{2,1,0:T(8,128)(2,1)}, u32[]{:S(2)}, u32[]{:S(2)}) %all-to-all-start.3) | async-done | bytes 8388640 | tf_op jit(solution)/shard_map/all_to_all | solution.py:129
  313.4 5.7 %fusion.22 = (bf16[32,16,2048]{2,1,0:T(8,128)(2,1)}, bf16[32,16,2048]{2,1,0:T(8,128)(2,1)S(1)}, bf16[32,16,2048]{2,1,0:T(8,128)(2,1)}, bf16[32,16,2048]{2,1,0:T(8,128)(2,1)}) fusion(bf16[128,16,2048]{2,1,0:T(8,128)(2,1)} %all-to-all-done.3), kind=kLoop, calls=%fused_computation.59 | loop fusion | bytes 16777216 | tf_op jit(solution)/shard_map/slice | solution.py:137
  319.1 6.9 %gather_fusion.2 = bf16[384,2048]{1,0:T(8,128)(2,1)} fusion(bf16[512,2048]{1,0:T(8,128)(2,1)} %bitcast.69, s32[1024]{0:T(1024)S(1)} %pad_clamp_fusion), kind=kCustom, calls=%fused_computation.clone | custom fusion | bytes 3147264 | tf_op jit(solution)/shard_map/jit(_take)/gather | solution.py:137
  326.0 6.9 %gather_fusion.3 = bf16[384,2048]{1,0:T(8,128)(2,1)} fusion(bf16[512,2048]{1,0:T(8,128)(2,1)} %bitcast.68, s32[1024]{0:T(1024)S(1)} %pad_clamp_fusion), kind=kCustom, calls=%fused_computation.1.clone | custom fusion | bytes 3147264 | tf_op jit(solution)/shard_map/jit(_take)/gather | solution.py:139
  332.9 6.9 %gather_fusion.4 = bf16[384,2048]{1,0:T(8,128)(2,1)} fusion(bf16[512,2048]{1,0:T(8,128)(2,1)} %bitcast.67, s32[1024]{0:T(1024)S(1)} %pad_clamp_fusion), kind=kCustom, calls=%fused_computation.2.clone | custom fusion | bytes 3147264 | tf_op jit(solution)/shard_map/jit(_take)/gather | solution.py:139
  339.8 3.2 gather_fusion.5
  343.0 6.1 %convert_add_fusion = f32[384,2048]{1,0:T(8,128)} fusion(bf16[384,2048]{1,0:T(8,128)(2,1)} %gather_fusion.5, bf16[384,2048]{1,0:T(8,128)(2,1)} %gather_fusion.4, bf16[384,2048]{1,0:T(8,128)(2,1)} %gather_fusion.3, bf16[384,2048]{1,0:T(8,128)(2,1)} %gather_fusion.2, pred[384]{0:T(512)(128)(4,1)S(1)} %get-tuple-element.6), kind=kLoop, calls=%fused_computation.10 | loop fusion | flops 8650752 | bytes 9437568 | tf_op jit(solution)/shard_map/add | solution.py:139
  349.1 4.6 %reshape.131 = f32[64,6,2048]{2,1,0:T(8,128)} reshape(f32[384,2048]{1,0:T(8,128)} %convert_add_fusion) | data formatting | bytes 6291456 | tf_op jit(solution)/shard_map/reshape | solution.py:140
  353.7 3.9 %multiply_reduce_fusion = f32[64,2048]{1,0:T(8,128)S(1)} fusion(f32[64,6,2048]{2,1,0:T(8,128)} %reshape.131, f32[64,6]{1,0:T(8,128)S(1)} %copy.40), kind=kLoop, calls=%fused_computation.9 | loop fusion | flops 1441792 | bytes 3671552 | tf_op jit(solution)/shard_map/reduce_sum | solution.py:141
  357.6 4.5 %fusion.6 = bf16[64,2048]{1,0:T(8,128)(2,1)} fusion(f32[64,2048]{1,0:T(8,128)S(1)} %multiply_reduce_fusion, bf16[1408,2048]{1,0:T(8,128)(2,1)} %param.23, f32[64,2,1408]{2,0,1:T(8,128)S(1)} %copy-done.5, f32[64,2048]{1,0:T(8,128)S(1)} %copy-done.2, bf16[64,4096]{1,0:T(8,128)(2,1)S(1)} %bitcast.77), kind=kOutput, calls=%fused_computation.18 | convolution fusion | flops 370204672 | bytes 8060928 | tf_op jit(solution)/shard_map/dot_general | solution.py:116
  (44 shorter events, 3.0 us)
Async XLA Ops:
  6.5 178.6 %copy-start = (bf16[1,2,352,2048]{3,2,1,0:T(8,128)(2,1)S(1)}, bf16[1,2,352,2048]{3,2,1,0:T(8,128)(2,1)}, u32[]{:S(2)}) copy-start(bf16[1,2,352,2048]{3,2,1,0:T(8,128)(2,1)} %param.24) | copy-start | bytes 8650756
  6.5 19.4 %copy-start.6 = (s32[64,6]{0,1:T(8,128)S(1)}, s32[64,6]{0,1:T(8,128)}, u32[]{:S(2)}) copy-start(s32[64,6]{0,1:T(8,128)} %param.19) | copy-start | bytes 4612
  6.5 57.5 %all-gather.2.cloned.1.call-start = ((), (), s32[]{:S(2)}) async-start(), calls=%async_computation.4 | async-start | bytes 4325376 | tf_op jit(solution)/shard_map/all_gather | solution.py:83
  20.0 10.4 %all-to-all-start = ((bf16[4,16,4096]{2,1,0:T(8,128)(2,1)}), bf16[4,16,4096]{2,1,0:T(8,128)(2,1)S(1)}, u32[]{:S(2)}, u32[]{:S(2)}) async-start(bf16[4,16,4096]{2,1,0:T(8,128)(2,1)} %broadcast_select_fusion), calls=%async_computation | async-start | bytes 1048576 | tf_op jit(solution)/shard_map/all_to_all | solution.py:86
  64.7 12.4 %copy-start.7 = (f32[2048]{0:T(1024)S(1)}, f32[2048]{0:T(1024)}, u32[]{:S(2)}) copy-start(f32[2048]{0:T(1024)} %param.21) | copy-start | bytes 24580
  78.3 1.9 copy-start.3
  185.1 6.3 %copy-start.9 = (bf16[1,352,2048]{2,1,0:T(8,128)(2,1)S(1)}, bf16[1,352,2048]{2,1,0:T(8,128)(2,1)}, u32[]{:S(2)}) copy-start(bf16[1,352,2048]{2,1,0:T(8,128)(2,1)} %param.25) | copy-start | bytes 4325380
  198.3 10.6 %copy-start.8 = (f32[64,6]{0,1:T(8,128)S(1)}, f32[64,6]{0,1:T(8,128)}, u32[]{:S(2)}) copy-start(f32[64,6]{0,1:T(8,128)} %param.20) | copy-start | bytes 4612
  198.3 10.7 %copy-start.4 = (bf16[64,2048]{1,0:T(8,128)(2,1)S(1)}, bf16[64,2048]{1,0:T(8,128)(2,1)}, u32[]{:S(2)}) copy-start(bf16[64,2048]{1,0:T(8,128)(2,1)} %copy-done.3) | copy-start | bytes 786436
  198.3 115.1 %all-to-all-start.3 = ((bf16[128,16,2048]{2,1,0:T(8,128)(2,1)}), bf16[128,16,2048]{2,1,0:T(8,128)(2,1)}, u32[]{:S(2)}, u32[]{:S(2)}) async-start(bf16[128,16,2048]{2,1,0:T(8,128)(2,1)} %bitcast.72), calls=%async_computation.3 | async-start | bytes 16777216 | tf_op jit(solution)/shard_map/all_to_all | solution.py:129
  353.7 3.9 %copy-start.2 = (f32[64,2048]{1,0:T(8,128)S(1)}, f32[64,2048]{1,0:T(8,128)}, u32[]{:S(2)}) copy-start(f32[64,2048]{1,0:T(8,128)} %shard_map.118) | copy-start | bytes 1572868
  353.7 3.9 %copy-start.5 = (f32[64,2,1408]{2,0,1:T(8,128)S(1)}, f32[64,2,1408]{2,0,1:T(8,128)}, u32[]{:S(2)}) copy-start(f32[64,2,1408]{2,0,1:T(8,128)} %fusion) | copy-start | bytes 2162692
  353.7 8.4 %copy-start.1 = (bf16[1,2,352,2048]{3,2,1,0:T(8,128)(2,1)S(1)}, bf16[1,2,352,2048]{3,2,1,0:T(8,128)(2,1)}, u32[]{:S(2)}) copy-start(bf16[1,2,352,2048]{3,2,1,0:T(8,128)(2,1)} %param.24) | copy-start | bytes 8650756
Sparse Core Ops, SparseCore 0:
  15.7 48.2 all-gather.1

commit v4 on v3

--- a/solution.py
+++ b/solution.py
@@ -133,10 +133,10 @@
         concat_axis=0,
         tiled=True,
     )
-    returned = returned.reshape(groups, slots_all, model_width)
-    pair_sum = jnp.take(returned[0], slot_of, axis=0).astype(jnp.float32)
-    for part in range(1, groups):
-        pair_sum = pair_sum + jnp.take(returned[part], slot_of, axis=0).astype(jnp.float32)
+    returned = returned.reshape(groups * slots_all, model_width)
+    picking = slot_of[:, None] == jnp.arange(slots_all, dtype=jnp.int32)[None, :]
+    picking = jnp.tile(picking, (1, groups)).astype(jnp.bfloat16)
+    pair_sum = jnp.dot(picking, returned, preferred_element_type=jnp.float32)
     pair_sum = pair_sum.reshape(token_rows, TOP, model_width)
     routed = jnp.sum(pair_sum * expert_weights[:, :, None], axis=1)
     return (mixed_rows + shared_out + routed).astype(jnp.bfloat16)

time: 370 us -> 333 us (0.900)
  local copies, waits for them, and re-layouts: 41.8 us -> 10.9 us
  other arithmetic: 18.2 us -> 9.1 us
  matrix products: 25.6 us -> 33.5 us
  waiting for transfers between devices: 131 us -> 126 us
    gather x4 -> x0, local copies, waits for them, and re-layouts: 23.9 us -> none  [the longest x3 17 us: body(): jnp.take(returned[part], slot_of, axis=0).astype(jnp.float32)]
    dot_general x0 -> x1, matrix products: none -> 7.85 us  [body(): pair_sum = jnp.dot(picking, returned, preferred_element_type=jnp.float32)]
    add x1 -> x0, other arithmetic: 6.07 us -> none  [body(): pair_sum + jnp.take(returned[part], slot_of, axis=0).astype(jnp.float32)]
    slice x2 -> x1, local copies, waits for them, and re-layouts: 5.88 us -> 0.23 us  [the longest x1 5.66 us: body(): pair_sum = jnp.take(returned[0], slot_of, axis=0).astype(jnp.float32)]
    reshape x1, local copies, waits for them, and re-layouts: 4.59 us -> 0.14 us  [body(): pair_expert = expert_ids.reshape(-1)]
    reduce_sum x1 -> x0, other arithmetic: 3.9 us -> none  [body(): routed = jnp.sum(pair_sum * expert_weights[:, :, None], axis=1)]
  transfers between devices with their start and end apart: 3 -> 3, of which waited for: 3 -> 2; matrix products, arithmetic and copies ran while one was open for 4% -> 6% of each run, Pallas kernels for 0% -> 0%
where the time goes in v4:
time: 333 us
  waiting for transfers between devices  126 us (38%)
  blocking collectives  112 us (34%)
  matrix products  33.5 us (10%)
  starting transfers between devices  16.4 us (5%)
  between operations  13.6 us (4%)
  Pallas kernels  11.2 us (3%)
  local copies, waits for them, and re-layouts  10.9 us (3%)
  other arithmetic  9.1 us (3%)
    all_to_all x1, blocking collectives, body(): lax.all_to_all(copies, ('req', 'head'), split_axis=0, concat_axis=0, tile...  105 us
    all_to_all x1, waiting for transfers between devices, body(): lax.all_to_all(part_out.reshape(groups * columns, local_experts * SLOT, m...  94.3 us
    all_gather x1, waiting for transfers between devices, body(): kv_piece = lax.all_gather(key_value_rows, 'head', axis=0, tiled=True)  31.9 us
    pallas_call x1, Pallas kernels, attention(): pl.pallas_call(functools.partial(attn_kernel, heads=16, kv_heads=4, size=...  11.2 us
    all_to_all x1, starting transfers between devices, body(): lax.all_to_all(part_out.reshape(groups * columns, local_experts * SLOT, m...  10.6 us
    dot_general x1, matrix products, body(): pair_sum = jnp.dot(picking, returned, preferred_element_type=jnp.float32)  7.85 us
    dot_general x1, matrix products, body(): jnp.einsum('td,dkf->tkf', normed, shared_gate_up, preferred_element_type=...  7.29 us
    dot_general x1, matrix products, body(): jnp.dot(hidden, expert_down[0], preferred_element_type=jnp.float32)  6.87 us
  transfers between devices with their start and end apart: 3, of which 2 were waited for; matrix products, arithmetic and copies ran while one was open for 6% of the time, Pallas kernels for 0%

profile of v4, /device:TPU:53, one launch (start us, length us, event | category | flops | bytes accessed | tf_op | source)
XLA Modules:
  0.0 332.6 jit_solution(10732483978458139779)
XLA Ops:
  6.5 0.9 select_reduce_fusion
  7.5 1.5 gather_fusion.1
  9.1 6.5 %all_to_all.20 = bf16[4,16,1024]{2,1,0:T(8,128)(2,1)} all-to-all(bf16[4,16,1024]{2,1,0:T(8,128)(2,1)S(1)} %broadcast_select_fusion.1), channel_id=1, replica_groups=mesh['req'=4,'head'=32] {'req'}, dimensions={0} | all-to-all | bytes 262144 | tf_op jit(solution)/shard_map/all_to_all | solution.py:81
  15.6 1.1 pad_maximum_fusion
  16.7 1.4 gather_fusion
  18.1 1.9 broadcast_select_fusion
  20.0 5.9 %all-to-all-start = ((bf16[4,16,4096]{2,1,0:T(8,128)(2,1)}), bf16[4,16,4096]{2,1,0:T(8,128)(2,1)S(1)}, u32[]{:S(2)}, u32[]{:S(2)}) async-start(bf16[4,16,4096]{2,1,0:T(8,128)(2,1)} %broadcast_select_fusion), calls=%async_computation | async-start | bytes 1048576 | tf_op jit(solution)/shard_map/all_to_all | solution.py:86
  25.9 0.8 copy.35
  27.0 0.9 reduce-window.6
  27.8 0.2 slice_reduce_fusion
  28.1 0.6 iota_add_fusion.posq_ref
  28.8 0.8 dynamic-slice_bitcast_fusion
  29.6 0.7 copy.33.segq_ref
  30.5 0.7 multiply_add_fusion
  31.4 0.7 slice.37.q_ref
  32.1 31.9 %all-gather.2.cloned.1.call-done.kv_ref = bf16[2048,1024]{1,0:T(8,128)(2,1)} async-done(((bf16[64,1024]{1,0:T(8,128)(2,1)}), bf16[2048,1024]{1,0:T(8,128)(2,1)}) %all-gather.2.cloned.1.call-update) | async-done | bytes 4194320 | tf_op jit(solution)/shard_map/all_gather | solution.py:83
  64.0 0.6 iota.39.posk_ref
  64.6 11.2 %shard_map.118 = f32[64,2048]{1,0:T(8,128)} custom-call(bf16[64,2048]{1,0:T(8,128)(2,1)} %slice.37.q_ref, bf16[2048,1024]{1,0:T(8,128)(2,1)} %all-gather.2.cloned.1.call-done.kv_ref, s32[64,1]{1,0:T(8,128)} %copy.33.segq_ref, s32[1,2048]{1,0:T(1,128)} %bitcast.77, s32[64,1]{1,0:T(8,128)} %iota_add_fusion.posq_ref, s32[1,2048]{1,0:T(1,128)} %iota.39.posk_ref), custom_call_target="tpu_custom_call" | custom-call | tf_op jit(solution)/shard_map/pallas_call | solution.py:47
  75.8 1.2 multiply_reduce_fusion.1
  77.0 1.2 multiply_convert_fusion
  78.2 0.8 convolution_convert_fusion.1
  79.0 1.1 broadcast_in_dim.42
  80.1 105.0 %all_to_all.21 = bf16[128,16,2048]{2,1,0:T(8,128)(2,1)S(1)} all-to-all(bf16[128,16,2048]{2,1,0:T(8,128)(2,1)S(1)} %bitcast.66), channel_id=1, replica_groups=mesh['req'=4,'head'=32] {'req','head'}, dimensions={0} | all-to-all | bytes 16777216 | tf_op jit(solution)/shard_map/all_to_all | solution.py:120
  185.1 6.3 %fusion.5 = f32[2048,2,352]{0,2,1:T(8,128)S(1)} fusion(bf16[2048,2048,1]{1,0,2:T(8,128)(2,1)S(1)} %bitcast.69, bf16[1,2,352,2048]{3,2,1,0:T(8,128)(2,1)S(1)} %copy-done), kind=kOutput, calls=%fused_computation.11 | convolution fusion | flops 5905580032 | bytes 17039360 | tf_op jit(solution)/shard_map/nd,kfd->nkf/dot_general | solution.py:122
  191.3 6.9 %convolution_convert_fusion = bf16[2048,2048]{1,0:T(8,128)(2,1)} fusion(bf16[1,352,2048]{2,1,0:T(8,128)(2,1)S(1)} %copy-done.7, f32[2048,2,352]{0,2,1:T(8,128)S(1)} %fusion.5), kind=kOutput, calls=%fused_computation.4 | convolution fusion | flops 2960588800 | bytes 15597568 | tf_op jit(solution)/shard_map/dot_general | solution.py:126
  198.2 10.6 %all-to-all-start.3 = ((bf16[128,16,2048]{2,1,0:T(8,128)(2,1)}), bf16[128,16,2048]{2,1,0:T(8,128)(2,1)}, u32[]{:S(2)}, u32[]{:S(2)}) async-start(bf16[128,16,2048]{2,1,0:T(8,128)(2,1)} %bitcast.68), calls=%async_computation.3 | async-start | bytes 16777216 | tf_op jit(solution)/shard_map/all_to_all | solution.py:129
  209.0 0.7 tile.2
  209.7 2.0 dot_general.22
  211.7 7.3 %fusion = f32[64,2,1408]{2,0,1:T(8,128)} fusion(bf16[2048,2,1408]{2,1,0:T(2,128)(2,1)} %param.20, bf16[64,2048]{1,0:T(8,128)(2,1)S(1)} %copy-done.4), kind=kOutput, calls=%fused_computation.2 | convolution fusion | flops 738197504 | bytes 12517376 | tf_op jit(solution)/shard_map/td,dkf->tkf/dot_general | solution.py:112
  219.0 94.3 %all-to-all-done.3 = bf16[128,16,2048]{2,1,0:T(8,128)(2,1)} async-done(((bf16[128,16,2048]{2,1,0:T(8,128)(2,1)}), bf16[128,16,2048]{2,1,0:T(8,128)(2,1)}, u32[]{:S(2)}, u32[]{:S(2)}) %all-to-all-start.3) | async-done | bytes 8388640 | tf_op jit(solution)/shard_map/all_to_all | solution.py:129
  313.3 7.8 %multiply_reduce_fusion = f32[64,2048]{1,0:T(8,128)S(1)} fusion(f32[64,6]{0,1:T(8,128)S(1)} %copy-done.8, bf16[2048,2048,1]{1,0,2:T(8,128)(2,1)} %bitcast.22, pred[64,6,2048]{2,1,0:T(8,128)(4,1)} %dot_general.22), kind=kOutput, calls=%fused_computation.5 | convolution fusion | flops 3222667264 | bytes 9700864 | tf_op jit(solution)/shard_map/dot_general | solution.py:139
  321.2 4.5 %fusion.8 = bf16[64,2048]{1,0:T(8,128)(2,1)} fusion(f32[64,2048]{1,0:T(8,128)S(1)} %multiply_reduce_fusion, bf16[1408,2048]{1,0:T(8,128)(2,1)} %param.21, f32[64,2,1408]{2,0,1:T(8,128)S(1)} %copy-done.5, f32[64,2048]{1,0:T(8,128)S(1)} %copy-done.2, bf16[64,4096]{1,0:T(8,128)(2,1)S(1)} %bitcast.73), kind=kOutput, calls=%fused_computation.15 | convolution fusion | flops 370204672 | bytes 8060928 | tf_op jit(solution)/shard_map/dot_general | solution.py:116
  (36 shorter events, 1.1 us)
Async XLA Ops:
  6.5 178.5 %copy-start = (bf16[1,2,352,2048]{3,2,1,0:T(8,128)(2,1)S(1)}, bf16[1,2,352,2048]{3,2,1,0:T(8,128)(2,1)}, u32[]{:S(2)}) copy-start(bf16[1,2,352,2048]{3,2,1,0:T(8,128)(2,1)} %param.22) | copy-start | bytes 8650756
  6.5 57.5 %all-gather.2.cloned.1.call-start = ((), (), s32[]{:S(2)}) async-start(), calls=%async_computation.4 | async-start | bytes 4325376 | tf_op jit(solution)/shard_map/all_gather | solution.py:83
  9.0 68.0 %copy-start.6 = (f32[2048]{0:T(1024)S(1)}, f32[2048]{0:T(1024)}, u32[]{:S(2)}) copy-start(f32[2048]{0:T(1024)} %param.19) | copy-start | bytes 24580
  20.0 11.4 %all-to-all-start = ((bf16[4,16,4096]{2,1,0:T(8,128)(2,1)}), bf16[4,16,4096]{2,1,0:T(8,128)(2,1)S(1)}, u32[]{:S(2)}, u32[]{:S(2)}) async-start(bf16[4,16,4096]{2,1,0:T(8,128)(2,1)} %broadcast_select_fusion), calls=%async_computation | async-start | bytes 1048576 | tf_op jit(solution)/shard_map/all_to_all | solution.py:86
  78.2 0.8 copy-start.3
  185.1 6.3 %copy-start.7 = (bf16[1,352,2048]{2,1,0:T(8,128)(2,1)S(1)}, bf16[1,352,2048]{2,1,0:T(8,128)(2,1)}, u32[]{:S(2)}) copy-start(bf16[1,352,2048]{2,1,0:T(8,128)(2,1)} %param.23) | copy-start | bytes 4325380
  198.2 13.5 %copy-start.4 = (bf16[64,2048]{1,0:T(8,128)(2,1)S(1)}, bf16[64,2048]{1,0:T(8,128)(2,1)}, u32[]{:S(2)}) copy-start(bf16[64,2048]{1,0:T(8,128)(2,1)} %copy-done.3) | copy-start | bytes 786436
  198.2 115.1 %all-to-all-start.3 = ((bf16[128,16,2048]{2,1,0:T(8,128)(2,1)}), bf16[128,16,2048]{2,1,0:T(8,128)(2,1)}, u32[]{:S(2)}, u32[]{:S(2)}) async-start(bf16[128,16,2048]{2,1,0:T(8,128)(2,1)} %bitcast.68), calls=%async_computation.3 | async-start | bytes 16777216 | tf_op jit(solution)/shard_map/all_to_all | solution.py:129
  211.7 101.6 %copy-start.8 = (f32[64,6]{0,1:T(8,128)S(1)}, f32[64,6]{0,1:T(8,128)}, u32[]{:S(2)}) copy-start(f32[64,6]{0,1:T(8,128)} %param.18) | copy-start | bytes 4612
  313.3 7.9 %copy-start.2 = (f32[64,2048]{1,0:T(8,128)S(1)}, f32[64,2048]{1,0:T(8,128)}, u32[]{:S(2)}) copy-start(f32[64,2048]{1,0:T(8,128)} %shard_map.118) | copy-start | bytes 1572868
  313.3 7.9 %copy-start.5 = (f32[64,2,1408]{2,0,1:T(8,128)S(1)}, f32[64,2,1408]{2,0,1:T(8,128)}, u32[]{:S(2)}) copy-start(f32[64,2,1408]{2,0,1:T(8,128)} %fusion) | copy-start | bytes 2162692
  313.3 12.4 %copy-start.1 = (bf16[1,2,352,2048]{3,2,1,0:T(8,128)(2,1)S(1)}, bf16[1,2,352,2048]{3,2,1,0:T(8,128)(2,1)}, u32[]{:S(2)}) copy-start(bf16[1,2,352,2048]{3,2,1,0:T(8,128)(2,1)} %param.22) | copy-start | bytes 8650756
Sparse Core Ops, SparseCore 0:
  15.7 48.2 all-gather.1

commit v5 on v4

--- a/solution.py
+++ b/solution.py
@@ -78,9 +78,12 @@
     def by_dest(array_in):
         return jnp.take(array_in.reshape(groups, page_rows, array_in.shape[1]), dest_order, axis=0)
 
-    moved_kv = lax.all_to_all(by_dest(keys_values), "req", split_axis=0, concat_axis=0, tiled=True)
-    key_value_rows = moved_kv.reshape(token_rows, keys_values.shape[1])
-    kv_piece = lax.all_gather(key_value_rows, "head", axis=0, tiled=True)
+    kv_pages = by_dest(keys_values)
+    kv_copies = jnp.broadcast_to(
+        kv_pages[:, None], (groups, columns) + kv_pages.shape[1:]
+    ).reshape((groups * columns,) + kv_pages.shape[1:])
+    kv_piece = lax.all_to_all(kv_copies, ("req", "head"), split_axis=0, concat_axis=0, tiled=True)
+    kv_piece = kv_piece.reshape(-1, keys_values.shape[1])
     widths = (hidden_in.shape[1], queries.shape[1])
     packed = jnp.concatenate((hidden_in, queries), axis=1)
     moved = lax.all_to_all(by_dest(packed), "req", split_axis=0, concat_axis=0, tiled=True)
@@ -90,9 +93,17 @@
     query_start = lax.axis_index("head") * token_rows
     segment_query = lax.dynamic_slice_in_dim(request_of_row, query_start, token_rows)
     position_query = query_start + jnp.arange(token_rows, dtype=jnp.int32)
-    position_key = jnp.arange(kv_piece.shape[0], dtype=jnp.int32)
+    position_key = (
+        jnp.arange(kv_piece.shape[0], dtype=jnp.int32)
+        .reshape(columns, groups, page_rows)
+        .transpose(1, 0, 2)
+        .reshape(-1)
+    )
+    segment_key = (
+        request_of_row.reshape(columns, groups, page_rows).transpose(1, 0, 2).reshape(-1)
+    )
     context = attention(
-        rows_of_queries, kv_piece, segment_query, request_of_row, position_query, position_key
+        rows_of_queries, kv_piece, segment_query, segment_key, position_query, position_key
     )
     mixed_rows = resid.astype(jnp.float32) + context
     mean_square = jnp.mean(mixed_rows * mixed_rows, axis=1, keepdims=True)

time: 333 us -> 340 us (1.021)
  waiting for transfers between devices: 126 us -> 140 us
  between operations: 13.6 us -> 0.23 us
  starting transfers between devices: 16.4 us -> 27.4 us
  blocking collectives: 112 us -> 104 us
    all_to_all x0 -> x1, waiting for transfers between devices: none -> 41.5 us  [body(): lax.all_to_all(kv_copies, ('req', 'head'), split_axis=0, concat_axis=0, t...]
    all_gather x1 -> x0, waiting for transfers between devices: 31.9 us -> none  [body(): kv_piece = lax.all_gather(key_value_rows, 'head', axis=0, tiled=True)]
    all_to_all x0 -> x1, starting transfers between devices: none -> 12.6 us  [body(): lax.all_to_all(kv_copies, ('req', 'head'), split_axis=0, concat_axis=0, t...]
    all_to_all x1 -> x0, blocking collectives: 6.54 us -> none  [body(): lax.all_to_all(by_dest(keys_values), 'req', split_axis=0, concat_axis=0,...]
    all_to_all x1, waiting for transfers between devices: 0.01 us -> 3.74 us  [body(): lax.all_to_all(by_dest(packed), 'req', split_axis=0, concat_axis=0, tiled...]
  transfers between devices with their start and end apart: 3 -> 3, of which waited for: 2 -> 3; matrix products, arithmetic and copies ran while one was open for 6% -> 6% of each run, Pallas kernels for 0% -> 0%
where the time goes in v5:
time: 340 us; the launch traced here: 339 us
  waiting for transfers between devices  140 us (41%)
  blocking collectives  104 us (31%)
  matrix products  33.5 us (10%)
  starting transfers between devices  27.4 us (8%)
  local copies, waits for them, and re-layouts  13.3 us (4%)
  Pallas kernels  11.2 us (3%)
  other arithmetic  10 us (3%)
    all_to_all x1, blocking collectives, body(): lax.all_to_all(copies, ('req', 'head'), split_axis=0, concat_axis=0, tile...  104 us
    all_to_all x1, waiting for transfers between devices, body(): lax.all_to_all(part_out.reshape(groups * columns, local_experts * SLOT, m...  94.3 us
    all_to_all x1, waiting for transfers between devices, body(): lax.all_to_all(kv_copies, ('req', 'head'), split_axis=0, concat_axis=0, t...  41.5 us
    all_to_all x1, starting transfers between devices, body(): lax.all_to_all(kv_copies, ('req', 'head'), split_axis=0, concat_axis=0, t...  12.6 us
    pallas_call x1, Pallas kernels, attention(): pl.pallas_call(functools.partial(attn_kernel, heads=16, kv_heads=4, size=...  11.2 us
    all_to_all x1, starting transfers between devices, body(): lax.all_to_all(part_out.reshape(groups * columns, local_experts * SLOT, m...  10.5 us
    dot_general x1, matrix products, body(): pair_sum = jnp.dot(picking, returned, preferred_element_type=jnp.float32)  7.85 us
    dot_general x1, matrix products, body(): jnp.einsum('td,dkf->tkf', normed, shared_gate_up, preferred_element_type=...  7.29 us
  transfers between devices with their start and end apart: 3, of which 3 were waited for; matrix products, arithmetic and copies ran while one was open for 6% of the time, Pallas kernels for 0%

profile of v5, /device:TPU:53, one launch (start us, length us, event | category | flops | bytes accessed | tf_op | source)
XLA Modules:
  0.0 339.4 jit_solution(10692836886421021912)
XLA Ops:
  0.0 0.9 select_reduce_fusion
  1.0 1.1 pad_maximum_fusion
  2.0 1.4 gather_fusion
  3.4 1.9 broadcast_select_fusion
  5.3 4.2 %all-to-all-start = ((bf16[4,16,4096]{2,1,0:T(8,128)(2,1)}), bf16[4,16,4096]{2,1,0:T(8,128)(2,1)S(1)}, u32[]{:S(2)}, u32[]{:S(2)}) async-start(bf16[4,16,4096]{2,1,0:T(8,128)(2,1)} %broadcast_select_fusion), calls=%async_computation | async-start | bytes 1048576 | tf_op jit(solution)/shard_map/all_to_all | solution.py:89
  9.6 1.2 gather_fusion.1
  10.8 1.0 broadcast_select_fusion.1
  11.8 3.7 %all-to-all-done = bf16[4,16,4096]{2,1,0:T(8,128)(2,1)S(1)} async-done(((bf16[4,16,4096]{2,1,0:T(8,128)(2,1)}), bf16[4,16,4096]{2,1,0:T(8,128)(2,1)S(1)}, u32[]{:S(2)}, u32[]{:S(2)}) %all-to-all-start) | async-done | bytes 524320 | tf_op jit(solution)/shard_map/all_to_all | solution.py:89
  15.5 2.5 broadcast_in_dim.47
  18.0 12.6 %all-to-all-start.1 = ((bf16[128,16,1024]{2,1,0:T(8,128)(2,1)}), bf16[128,16,1024]{2,1,0:T(8,128)(2,1)}, u32[]{:S(2)}, u32[]{:S(2)}) async-start(bf16[128,16,1024]{2,1,0:T(8,128)(2,1)} %bitcast.68), calls=%async_computation.1 | async-start | bytes 8388608 | tf_op jit(solution)/shard_map/all_to_all | solution.py:85
  30.8 0.7 eq.76
  31.8 0.7 copy.36.segq_ref
  32.5 0.7 reshape_reshape.4.segk_ref
  33.2 0.7 reshape.219.posk_ref
  34.6 0.9 reduce-window.6
  36.9 0.7 slice.37.q_ref
  37.6 41.5 %all-to-all-done.1 = bf16[128,16,1024]{2,1,0:T(8,128)(2,1)} async-done(((bf16[128,16,1024]{2,1,0:T(8,128)(2,1)}), bf16[128,16,1024]{2,1,0:T(8,128)(2,1)}, u32[]{:S(2)}, u32[]{:S(2)}) %all-to-all-start.1) | async-done | bytes 4194336 | tf_op jit(solution)/shard_map/all_to_all | solution.py:85
  79.0 11.2 %shard_map.118 = f32[64,2048]{1,0:T(8,128)} custom-call(bf16[64,2048]{1,0:T(8,128)(2,1)} %slice.37.q_ref, bf16[2048,1024]{1,0:T(8,128)(2,1)} %bitcast.7.kv_ref, s32[64,1]{1,0:T(8,128)} %copy.36.segq_ref, s32[1,2048]{1,0:T(1,128)} %reshape_reshape.4.segk_ref, s32[64,1]{1,0:T(8,128)} %iota_add_fusion.posq_ref, s32[1,2048]{1,0:T(1,128)} %reshape.219.posk_ref), custom_call_target="tpu_custom_call" | custom-call | tf_op jit(solution)/shard_map/pallas_call | solution.py:47
  90.2 1.2 multiply_reduce_fusion.1
  91.4 1.2 multiply_convert_fusion
  92.6 0.8 convolution_convert_fusion.1
  93.4 1.1 broadcast_in_dim.49
  94.5 104.3 %all_to_all.20 = bf16[128,16,2048]{2,1,0:T(8,128)(2,1)S(1)} all-to-all(bf16[128,16,2048]{2,1,0:T(8,128)(2,1)S(1)} %bitcast.67), channel_id=1, replica_groups=mesh['req'=4,'head'=32] {'req','head'}, dimensions={0} | all-to-all | bytes 16777216 | tf_op jit(solution)/shard_map/all_to_all | solution.py:131
  198.8 6.3 %fusion.5 = f32[2048,2,352]{0,2,1:T(8,128)S(1)} fusion(bf16[2048,2048,1]{1,0,2:T(8,128)(2,1)S(1)} %bitcast.71, bf16[1,2,352,2048]{3,2,1,0:T(8,128)(2,1)S(1)} %copy-done), kind=kOutput, calls=%fused_computation.11 | convolution fusion | flops 5905580032 | bytes 17039360 | tf_op jit(solution)/shard_map/nd,kfd->nkf/dot_general | solution.py:133
  205.1 6.9 %convolution_convert_fusion = bf16[2048,2048]{1,0:T(8,128)(2,1)} fusion(bf16[1,352,2048]{2,1,0:T(8,128)(2,1)S(1)} %copy-done.10, f32[2048,2,352]{0,2,1:T(8,128)S(1)} %fusion.5), kind=kOutput, calls=%fused_computation.4 | convolution fusion | flops 2960588800 | bytes 15597568 | tf_op jit(solution)/shard_map/dot_general | solution.py:137
  211.9 10.5 %all-to-all-start.3 = ((bf16[128,16,2048]{2,1,0:T(8,128)(2,1)}), bf16[128,16,2048]{2,1,0:T(8,128)(2,1)}, u32[]{:S(2)}, u32[]{:S(2)}) async-start(bf16[128,16,2048]{2,1,0:T(8,128)(2,1)} %bitcast.70), calls=%async_computation.3 | async-start | bytes 16777216 | tf_op jit(solution)/shard_map/all_to_all | solution.py:140
  222.7 0.7 tile.2
  223.4 2.0 dot_general.22
  225.4 7.3 %fusion = f32[64,2,1408]{2,0,1:T(8,128)} fusion(bf16[2048,2,1408]{2,1,0:T(2,128)(2,1)} %param.20, bf16[64,2048]{1,0:T(8,128)(2,1)S(1)} %copy-done.4), kind=kOutput, calls=%fused_computation.2 | convolution fusion | flops 738197504 | bytes 12517376 | tf_op jit(solution)/shard_map/td,dkf->tkf/dot_general | solution.py:123
  232.7 94.3 %all-to-all-done.3 = bf16[128,16,2048]{2,1,0:T(8,128)(2,1)} async-done(((bf16[128,16,2048]{2,1,0:T(8,128)(2,1)}), bf16[128,16,2048]{2,1,0:T(8,128)(2,1)}, u32[]{:S(2)}, u32[]{:S(2)}) %all-to-all-start.3) | async-done | bytes 8388640 | tf_op jit(solution)/shard_map/all_to_all | solution.py:140
  327.0 7.8 %multiply_reduce_fusion = f32[64,2048]{1,0:T(8,128)S(1)} fusion(f32[64,6]{0,1:T(8,128)S(1)} %copy-done.11, bf16[2048,2048,1]{1,0,2:T(8,128)(2,1)} %bitcast.23, pred[64,6,2048]{2,1,0:T(8,128)(4,1)} %dot_general.22), kind=kOutput, calls=%fused_computation.5 | convolution fusion | flops 3222667264 | bytes 9700864 | tf_op jit(solution)/shard_map/dot_general | solution.py:150
  334.9 4.5 %fusion.8 = bf16[64,2048]{1,0:T(8,128)(2,1)} fusion(f32[64,2048]{1,0:T(8,128)S(1)} %multiply_reduce_fusion, bf16[1408,2048]{1,0:T(8,128)(2,1)} %param.21, f32[64,2,1408]{2,0,1:T(8,128)S(1)} %copy-done.5, f32[64,2048]{1,0:T(8,128)S(1)} %copy-done.2, bf16[64,4096]{1,0:T(8,128)(2,1)S(1)} %bitcast.75), kind=kOutput, calls=%fused_computation.15 | convolution fusion | flops 370204672 | bytes 8060928 | tf_op jit(solution)/shard_map/dot_general | solution.py:127
  (45 shorter events, 2.7 us)
Async XLA Ops:
  0.0 198.8 %copy-start = (bf16[1,2,352,2048]{3,2,1,0:T(8,128)(2,1)S(1)}, bf16[1,2,352,2048]{3,2,1,0:T(8,128)(2,1)}, u32[]{:S(2)}) copy-start(bf16[1,2,352,2048]{3,2,1,0:T(8,128)(2,1)} %param.22) | copy-start | bytes 8650756
  0.0 9.6 %copy-start.6 = (bf16[64,1024]{1,0:T(8,128)(2,1)S(1)}, bf16[64,1024]{1,0:T(8,128)(2,1)}, u32[]{:S(2)}) copy-start(bf16[64,1024]{1,0:T(8,128)(2,1)} %param.14) | copy-start | bytes 393220
  5.3 10.2 %all-to-all-start = ((bf16[4,16,4096]{2,1,0:T(8,128)(2,1)}), bf16[4,16,4096]{2,1,0:T(8,128)(2,1)S(1)}, u32[]{:S(2)}, u32[]{:S(2)}) async-start(bf16[4,16,4096]{2,1,0:T(8,128)(2,1)} %broadcast_select_fusion), calls=%async_computation | async-start | bytes 1048576 | tf_op jit(solution)/shard_map/all_to_all | solution.py:89
  18.0 12.6 %copy-start.7 = (s32[64,6]{0,1:T(8,128)S(1)}, s32[64,6]{0,1:T(8,128)}, u32[]{:S(2)}) copy-start(s32[64,6]{0,1:T(8,128)} %param.17) | copy-start | bytes 4612
  18.0 13.6 %copy-start.9 = (s32[2048]{0:T(1024)S(1)}, s32[2048]{0:T(1024)}, u32[]{:S(2)}) copy-start(s32[2048]{0:T(1024)} %param.15) | copy-start | bytes 24580
  18.0 61.0 %all-to-all-start.1 = ((bf16[128,16,1024]{2,1,0:T(8,128)(2,1)}), bf16[128,16,1024]{2,1,0:T(8,128)(2,1)}, u32[]{:S(2)}, u32[]{:S(2)}) async-start(bf16[128,16,1024]{2,1,0:T(8,128)(2,1)} %bitcast.68), calls=%async_computation.1 | async-start | bytes 8388608 | tf_op jit(solution)/shard_map/all_to_all | solution.py:85
  30.6 60.8 %copy-start.8 = (f32[2048]{0:T(1024)S(1)}, f32[2048]{0:T(1024)}, u32[]{:S(2)}) copy-start(f32[2048]{0:T(1024)} %param.19) | copy-start | bytes 24580
  92.6 1.9 copy-start.3
  198.8 6.3 %copy-start.10 = (bf16[1,352,2048]{2,1,0:T(8,128)(2,1)S(1)}, bf16[1,352,2048]{2,1,0:T(8,128)(2,1)}, u32[]{:S(2)}) copy-start(bf16[1,352,2048]{2,1,0:T(8,128)(2,1)} %param.23) | copy-start | bytes 4325380
  211.9 13.5 %copy-start.4 = (bf16[64,2048]{1,0:T(8,128)(2,1)S(1)}, bf16[64,2048]{1,0:T(8,128)(2,1)}, u32[]{:S(2)}) copy-start(bf16[64,2048]{1,0:T(8,128)(2,1)} %copy-done.3) | copy-start | bytes 786436
  211.9 115.1 %all-to-all-start.3 = ((bf16[128,16,2048]{2,1,0:T(8,128)(2,1)}), bf16[128,16,2048]{2,1,0:T(8,128)(2,1)}, u32[]{:S(2)}, u32[]{:S(2)}) async-start(bf16[128,16,2048]{2,1,0:T(8,128)(2,1)} %bitcast.70), calls=%async_computation.3 | async-start | bytes 16777216 | tf_op jit(solution)/shard_map/all_to_all | solution.py:140
  225.4 101.6 %copy-start.11 = (f32[64,6]{0,1:T(8,128)S(1)}, f32[64,6]{0,1:T(8,128)}, u32[]{:S(2)}) copy-start(f32[64,6]{0,1:T(8,128)} %param.18) | copy-start | bytes 4612
  327.0 7.9 %copy-start.2 = (f32[64,2048]{1,0:T(8,128)S(1)}, f32[64,2048]{1,0:T(8,128)}, u32[]{:S(2)}) copy-start(f32[64,2048]{1,0:T(8,128)} %shard_map.118) | copy-start | bytes 1572868
  327.0 7.9 %copy-start.5 = (f32[64,2,1408]{2,0,1:T(8,128)S(1)}, f32[64,2,1408]{2,0,1:T(8,128)}, u32[]{:S(2)}) copy-start(f32[64,2,1408]{2,0,1:T(8,128)} %fusion) | copy-start | bytes 2162692
  327.0 12.4 %copy-start.1 = (bf16[1,2,352,2048]{3,2,1,0:T(8,128)(2,1)S(1)}, bf16[1,2,352,2048]{3,2,1,0:T(8,128)(2,1)}, u32[]{:S(2)}) copy-start(bf16[1,2,352,2048]{3,2,1,0:T(8,128)(2,1)} %param.22) | copy-start | bytes 8650756

commit v6 on v4

--- a/solution.py
+++ b/solution.py
@@ -7,16 +7,10 @@
 from jax.experimental.pallas import tpu as pltpu
 from jax.sharding import PartitionSpec as P
 
-QUERY_HEADS = 16
-KEY_VALUE_HEADS = 4
-HEAD_SIZE = 128
+
 EXPERTS = 32
 TOP = 6
-CAP = 14
 SLOT = 16
-
-
-negative_large = -1e30
 
 
 def silu_mul(gate_value, upward):
@@ -41,6 +35,7 @@
             ctx = jnp.dot(weights.astype(jnp.bfloat16), values, preferred_element_type=jnp.float32)
             out_ref[:, h * size:(h + 1) * size] = ctx / total
 
+
 def attention(q, kv, segq, segk, posq, posk):
     rows = q.shape[0]
     vmem = pl.BlockSpec(memory_space=pltpu.VMEM)
@@ -51,7 +46,7 @@
     )(q, kv, segq.reshape(rows, 1), segk.reshape(1, -1), posq.reshape(rows, 1), posk.reshape(1, -1))
 
 
-def body(
+def layer(
     hidden_in,
     queries,
     keys_values,
@@ -74,6 +69,12 @@
     page_dest = page_route.reshape(groups)
     matches = (page_dest[None, :] == group_ids[:, None]).astype(jnp.int32)
     dest_order = jnp.sum(matches * group_ids[None, :], axis=1)
+
+    down_parts = [expert_down[0]]
+    for shift in range(1, groups):
+        down_parts.append(
+            lax.ppermute(expert_down[0], "req", [(i, (i + shift) % groups) for i in range(groups)])
+        )
 
     def by_dest(array_in):
         return jnp.take(array_in.reshape(groups, page_rows, array_in.shape[1]), dest_order, axis=0)
@@ -123,19 +124,25 @@
         "nd,kfd->nkf", expert_rows, expert_gate_up[0], preferred_element_type=jnp.float32
     )
     hidden = silu_mul(both_parts[:, 0], both_parts[:, 1]).astype(jnp.bfloat16)
-    part_out = jnp.dot(hidden, expert_down[0], preferred_element_type=jnp.float32).astype(
-        jnp.bfloat16
-    )
+    hidden = hidden.reshape(groups, columns * local_experts * SLOT, hidden.shape[-1])
+    hidden_parts = lax.all_to_all(hidden, "req", split_axis=0, concat_axis=0, tiled=True)
+    out_rows = None
+    for shift in range(groups):
+        part_index = (lax.axis_index("req") - shift) % groups
+        hidden_part = lax.dynamic_index_in_dim(hidden_parts, part_index, 0, keepdims=False)
+        product = jnp.dot(hidden_part, down_parts[shift], preferred_element_type=jnp.float32)
+        out_rows = product if out_rows is None else out_rows + product
     returned = lax.all_to_all(
-        part_out.reshape(groups * columns, local_experts * SLOT, model_width),
-        ("req", "head"),
+        out_rows.astype(jnp.bfloat16).reshape(columns, local_experts * SLOT, model_width),
+        "head",
         split_axis=0,
         concat_axis=0,
         tiled=True,
     )
-    returned = returned.reshape(groups * slots_all, model_width)
-    picking = slot_of[:, None] == jnp.arange(slots_all, dtype=jnp.int32)[None, :]
-    picking = jnp.tile(picking, (1, groups)).astype(jnp.bfloat16)
+    returned = returned.reshape(slots_all, model_width)
+    picking = (slot_of[:, None] == jnp.arange(slots_all, dtype=jnp.int32)[None, :]).astype(
+        jnp.bfloat16
+    )
     pair_sum = jnp.dot(picking, returned, preferred_element_type=jnp.float32)
     pair_sum = pair_sum.reshape(token_rows, TOP, model_width)
     routed = jnp.sum(pair_sum * expert_weights[:, :, None], axis=1)
@@ -144,7 +151,7 @@
 
 def solution(mesh):
     return jax.shard_map(
-        body,
+        layer,
         mesh=mesh,
         in_specs=(
             P(("req", "head"), None),

time: 333 us -> 355 us (1.066); the launches traced: 333 us -> 350 us
  starting transfers between devices: 16.4 us -> 25.4 us
  local copies, waits for them, and re-layouts: 10.9 us -> 18.9 us
  other arithmetic: 9.1 us -> 13 us
    all_to_all x2 -> x3, waiting for transfers between devices: 94.3 us -> 32.6 us  [the longest x1 18.4 us: layer(): lax.all_to_all(out_rows.astype(jnp.bfloat16).reshape(columns, local_exper...]
    ppermute x0 -> x3, waiting for transfers between devices: none -> 58 us  [layer(): lax.ppermute(expert_down[0], 'req', [(i, (i + shift) % groups) for i in r...]
    squeeze x0 -> x2, local copies, waits for them, and re-layouts: none -> 8.59 us  [layer(): hidden = silu_mul(both_parts[:, 0], both_parts[:, 1]).astype(jnp.bfloat16)]
    all_to_all x2 -> x3, starting transfers between devices: 16.4 us -> 23.3 us  [the longest x1 12.7 us: layer(): lax.all_to_all(out_rows.astype(jnp.bfloat16).reshape(columns, local_exper...]
    convert_element_type x2 -> x3, other arithmetic: 1.17 us -> 5.97 us  [the longest x1 4.8 us: layer(): hidden = silu_mul(both_parts[:, 0], both_parts[:, 1]).astype(jnp.bfloat16)]
    dot_general x6 -> x9, matrix products: 33.5 us -> 32.6 us  [the longest x4 11 us: layer(): jnp.dot(hidden_part, down_parts[shift], preferred_element_type=jnp.float32)]
  transfers between devices with their start and end apart: 3 -> 7, of which waited for: 2 -> 6; matrix products, arithmetic and copies ran while one was open for 6% -> 7% of each run, Pallas kernels for 0% -> 0%
where the time goes in v6:
time: 355 us; the launch traced here: 350 us
  waiting for transfers between devices  124 us (35%)
  blocking collectives  112 us (32%)
  matrix products  32.6 us (9%)
  starting transfers between devices  25.4 us (7%)
  local copies, waits for them, and re-layouts  18.9 us (5%)
  between operations  13.6 us (4%)
  other arithmetic  13 us (4%)
  Pallas kernels  11.2 us (3%)
    all_to_all x1, blocking collectives, layer(): lax.all_to_all(copies, ('req', 'head'), split_axis=0, concat_axis=0, tile...  105 us
    ppermute x3, waiting for transfers between devices, layer(): lax.ppermute(expert_down[0], 'req', [(i, (i + shift) % groups) for i in r...  58 us
    all_gather x1, waiting for transfers between devices, layer(): kv_piece = lax.all_gather(key_value_rows, 'head', axis=0, tiled=True)  32.9 us
    all_to_all x1, waiting for transfers between devices, layer(): lax.all_to_all(out_rows.astype(jnp.bfloat16).reshape(columns, local_exper...  18.4 us
    all_to_all x1, waiting for transfers between devices, layer(): lax.all_to_all(hidden, 'req', split_axis=0, concat_axis=0, tiled=True)  13.8 us
    all_to_all x1, starting transfers between devices, layer(): lax.all_to_all(out_rows.astype(jnp.bfloat16).reshape(columns, local_exper...  12.7 us
    pallas_call x1, Pallas kernels, attention(): pl.pallas_call(functools.partial(attn_kernel, heads=16, kv_heads=4, size=...  11.2 us
    dot_general x4, matrix products, layer(): jnp.dot(hidden_part, down_parts[shift], preferred_element_type=jnp.float32)  11 us
  transfers between devices with their start and end apart: 7, of which 6 were waited for; matrix products, arithmetic and copies ran while one was open for 7% of the time, Pallas kernels for 0%

profile of v6, /device:TPU:53, one launch (start us, length us, event | category | flops | bytes accessed | tf_op | source)
XLA Modules:
  0.0 350.0 jit_solution(16709746167447836429)
XLA Ops:
  6.5 0.9 select_reduce_fusion
  7.5 1.5 gather_fusion.1
  9.1 6.5 %all_to_all.25 = bf16[4,16,1024]{2,1,0:T(8,128)(2,1)} all-to-all(bf16[4,16,1024]{2,1,0:T(8,128)(2,1)S(1)} %broadcast_select_fusion.1), channel_id=1, replica_groups=mesh['req'=4,'head'=32] {'req'}, dimensions={0} | all-to-all | bytes 262144 | tf_op jit(solution)/shard_map/all_to_all | solution.py:82
  15.6 1.1 pad_maximum_fusion
  16.7 1.4 gather_fusion
  18.1 1.9 broadcast_select_fusion
  20.0 5.9 %all-to-all-start = ((bf16[4,16,4096]{2,1,0:T(8,128)(2,1)}), bf16[4,16,4096]{2,1,0:T(8,128)(2,1)S(1)}, u32[]{:S(2)}, u32[]{:S(2)}) async-start(bf16[4,16,4096]{2,1,0:T(8,128)(2,1)} %broadcast_select_fusion), calls=%async_computation | async-start | bytes 1048576 | tf_op jit(solution)/shard_map/all_to_all | solution.py:87
  31.1 32.9 %all-gather.2.cloned.1.call-done.kv_ref = bf16[2048,1024]{1,0:T(8,128)(2,1)} async-done(((bf16[64,1024]{1,0:T(8,128)(2,1)}), bf16[2048,1024]{1,0:T(8,128)(2,1)}) %all-gather.2.cloned.1.call-update) | async-done | bytes 4194320 | tf_op jit(solution)/shard_map/all_gather | solution.py:84
  64.7 11.2 %shard_map.118 = f32[64,2048]{1,0:T(8,128)} custom-call(bf16[64,2048]{1,0:T(8,128)(2,1)} %slice.37.q_ref, bf16[2048,1024]{1,0:T(8,128)(2,1)} %all-gather.2.cloned.1.call-done.kv_ref, s32[64,1]{1,0:T(8,128)} %copy.39.segq_ref, s32[1,2048]{1,0:T(1,128)} %bitcast.100, s32[64,1]{1,0:T(8,128)} %iota_add_fusion.posq_ref, s32[1,2048]{1,0:T(1,128)} %iota.38.posk_ref), custom_call_target="tpu_custom_call" | custom-call | tf_op jit(solution)/shard_map/pallas_call | solution.py:42
  75.8 1.2 multiply_reduce_fusion.1
  77.1 1.2 multiply_convert_fusion
  79.0 1.1 broadcast_in_dim.42
  80.1 105.0 %all_to_all.26 = bf16[128,16,2048]{2,1,0:T(8,128)(2,1)S(1)} all-to-all(bf16[128,16,2048]{2,1,0:T(8,128)(2,1)S(1)} %bitcast.87), channel_id=1, replica_groups=mesh['req'=4,'head'=32] {'req','head'}, dimensions={0} | all-to-all | bytes 16777216 | tf_op jit(solution)/shard_map/all_to_all | solution.py:121
  185.1 6.3 %fusion.2 = f32[2048,2,352]{0,2,1:T(8,128)S(1)} fusion(bf16[2048,2048,1]{1,0,2:T(8,128)(2,1)S(1)} %bitcast.89, bf16[1,2,352,2048]{3,2,1,0:T(8,128)(2,1)S(1)} %copy-done), kind=kOutput, calls=%fused_computation.7 | convolution fusion | flops 5905580032 | bytes 17039360 | tf_op jit(solution)/shard_map/nd,kfd->nkf/dot_general | solution.py:123
  191.4 2.8 fusion.40
  194.2 3.7 %squeeze.37 = f32[4,512,352]{1,0,2:T(4,128)S(1)} reshape(f32[2048,1,352]{0,2,1:T(8,128)} %get-tuple-element.5) | data formatting | bytes 5767168 | tf_op jit(solution)/shard_map/squeeze | solution.py:126
  197.8 4.9 %squeeze.38 = f32[4,512,352]{1,0,2:T(4,128)} reshape(f32[2048,1,352]{0,2,1:T(8,128)} %get-tuple-element.6) | data formatting | bytes 5767168 | tf_op jit(solution)/shard_map/squeeze | solution.py:126
  202.8 4.8 %fusion.4 = bf16[4,512,352]{1,2,0:T(8,128)(2,1)} fusion(f32[4,512,352]{1,0,2:T(4,128)} %squeeze.38, f32[4,512,352]{1,0,2:T(4,128)S(1)} %squeeze.37), kind=kLoop, calls=%fused_computation.10 | loop fusion | flops 3604480 | bytes 7208960 | tf_op jit(solution)/shard_map/convert_element_type | solution.py:126
  207.6 4.7 %all-to-all-start.3 = ((bf16[4,512,352]{1,2,0:T(8,128)(2,1)}), bf16[4,512,352]{1,2,0:T(8,128)(2,1)S(1)}, u32[]{:S(2)}, u32[]{:S(2)}) async-start(bf16[4,512,352]{1,2,0:T(8,128)(2,1)} %fusion.4), calls=%async_computation.3 | async-start | bytes 2883584 | tf_op jit(solution)/shard_map/all_to_all | solution.py:128
  212.3 0.9 collective-permute-start
  214.4 13.8 %all-to-all-done.3 = bf16[4,512,352]{1,2,0:T(8,128)(2,1)S(1)} async-done(((bf16[4,512,352]{1,2,0:T(8,128)(2,1)}), bf16[4,512,352]{1,2,0:T(8,128)(2,1)S(1)}, u32[]{:S(2)}, u32[]{:S(2)}) %all-to-all-start.3) | async-done | bytes 1441824 | tf_op jit(solution)/shard_map/all_to_all | solution.py:128
  228.3 1.3 fusion.21
  229.6 29.7 %collective-permute-done = bf16[352,2048]{1,0:T(8,128)(2,1)} collective-permute-done((bf16[352,2048]{1,0:T(8,128)(2,1)S(1)}, bf16[352,2048]{1,0:T(8,128)(2,1)}, u32[]{:S(2)}, u32[]{:S(2)}) %collective-permute-start) | collective-permute-done | bytes 1441824 | tf_op jit(solution)/shard_map/ppermute | solution.py:76
  259.2 2.6 fusion.19
  261.9 28.4 %collective-permute-done.1 = bf16[352,2048]{1,0:T(8,128)(2,1)} collective-permute-done((bf16[352,2048]{1,0:T(8,128)(2,1)S(1)}, bf16[352,2048]{1,0:T(8,128)(2,1)}, u32[]{:S(2)}, u32[]{:S(2)}) %collective-permute-start.1) | collective-permute-done | bytes 1441824 | tf_op jit(solution)/shard_map/ppermute | solution.py:76
  290.2 2.6 fusion.17
  292.9 4.4 %add_convert_fusion = bf16[512,2048]{1,0:T(8,128)(2,1)} fusion(f32[512,2048]{1,0:T(8,128)S(1)} %fusion.17, f32[512,2048]{1,0:T(8,128)S(1)} %fusion.21, f32[512,2048]{1,0:T(8,128)S(1)} %fusion.19, bf16[352,2048]{1,0:T(8,128)(2,1)} %collective-permute-done.2, bf16[4,512,352]{1,2,0:T(8,128)(2,1)S(1)} %all-to-all-done.3, s32[]{:T(128)S(6)} %select_n.73), kind=kOutput, calls=%fused_computation.4 | convolution fusion | flops 742391808 | bytes 16482308 | tf_op jit(solution)/shard_map/dot_general | solution.py:133
  297.3 12.7 %all-to-all-start.4 = ((bf16[32,16,2048]{2,1,0:T(8,128)(2,1)}), bf16[32,16,2048]{2,1,0:T(8,128)(2,1)}, u32[]{:S(2)}, u32[]{:S(2)}) async-start(bf16[32,16,2048]{2,1,0:T(8,128)(2,1)} %bitcast.24), calls=%async_computation.4 | async-start | bytes 4194304 | tf_op jit(solution)/shard_map/all_to_all | solution.py:135
  310.0 7.3 %fusion = f32[64,2,1408]{2,0,1:T(8,128)} fusion(bf16[2048,2,1408]{2,1,0:T(2,128)(2,1)} %param.20, bf16[64,2048]{1,0:T(8,128)(2,1)S(1)} %copy-done.7), kind=kOutput, calls=%fused_computation.2 | convolution fusion | flops 738197504 | bytes 12517376 | tf_op jit(solution)/shard_map/td,dkf->tkf/dot_general | solution.py:113
  317.3 18.4 %all-to-all-done.4 = bf16[32,16,2048]{2,1,0:T(8,128)(2,1)} async-done(((bf16[32,16,2048]{2,1,0:T(8,128)(2,1)}), bf16[32,16,2048]{2,1,0:T(8,128)(2,1)}, u32[]{:S(2)}, u32[]{:S(2)}) %all-to-all-start.4) | async-done | bytes 2097184 | tf_op jit(solution)/shard_map/all_to_all | solution.py:135
  335.7 2.8 multiply_reduce_fusion
  338.6 4.5 %fusion.6 = bf16[64,2048]{1,0:T(8,128)(2,1)} fusion(f32[64,2048]{1,0:T(8,128)S(1)} %multiply_reduce_fusion, bf16[1408,2048]{1,0:T(8,128)(2,1)} %param.21, f32[64,2,1408]{2,0,1:T(8,128)S(1)} %copy-done.8, f32[64,2048]{1,0:T(8,128)S(1)} %copy-done.2, bf16[64,4096]{1,0:T(8,128)(2,1)S(1)} %bitcast.93), kind=kOutput, calls=%fused_computation.13 | convolution fusion | flops 370204672 | bytes 8060928 | tf_op jit(solution)/shard_map/dot_general | solution.py:117
  (53 shorter events, 8.1 us)
Async XLA Ops:
  6.5 178.6 %copy-start = (bf16[1,2,352,2048]{3,2,1,0:T(8,128)(2,1)S(1)}, bf16[1,2,352,2048]{3,2,1,0:T(8,128)(2,1)}, u32[]{:S(2)}) copy-start(bf16[1,2,352,2048]{3,2,1,0:T(8,128)(2,1)} %param.22) | copy-start | bytes 8650756
  6.5 19.3 %copy-start.9 = (s32[64,6]{0,1:T(8,128)S(1)}, s32[64,6]{0,1:T(8,128)}, u32[]{:S(2)}) copy-start(s32[64,6]{0,1:T(8,128)} %param.17) | copy-start | bytes 4612
  6.5 57.5 %all-gather.2.cloned.1.call-start = ((), (), s32[]{:S(2)}) async-start(), calls=%async_computation.5 | async-start | bytes 4325376 | tf_op jit(solution)/shard_map/all_gather | solution.py:84
  20.0 10.4 %all-to-all-start = ((bf16[4,16,4096]{2,1,0:T(8,128)(2,1)}), bf16[4,16,4096]{2,1,0:T(8,128)(2,1)S(1)}, u32[]{:S(2)}, u32[]{:S(2)}) async-start(bf16[4,16,4096]{2,1,0:T(8,128)(2,1)} %broadcast_select_fusion), calls=%async_computation | async-start | bytes 1048576 | tf_op jit(solution)/shard_map/all_to_all | solution.py:87
  30.4 46.7 %copy-start.3 = (bf16[4,16,4096]{2,1,0:T(8,128)(2,1)}, bf16[4,16,4096]{2,1,0:T(8,128)(2,1)S(1)}, u32[]{:S(2)}) copy-start(bf16[4,16,4096]{2,1,0:T(8,128)(2,1)S(1)} %all-to-all-done) | copy-start | bytes 1572868
  64.6 12.4 %copy-start.10 = (f32[2048]{0:T(1024)S(1)}, f32[2048]{0:T(1024)}, u32[]{:S(2)}) copy-start(f32[2048]{0:T(1024)} %param.19) | copy-start | bytes 24580
  78.2 1.9 copy-start.6
  207.6 4.7 %copy-start.5 = (bf16[1,352,2048]{2,1,0:T(8,128)(2,1)S(1)}, bf16[1,352,2048]{2,1,0:T(8,128)(2,1)}, u32[]{:S(2)}) copy-start(bf16[1,352,2048]{2,1,0:T(8,128)(2,1)} %param.23) | copy-start | bytes 4325380
  207.6 20.7 %all-to-all-start.3 = ((bf16[4,512,352]{1,2,0:T(8,128)(2,1)}), bf16[4,512,352]{1,2,0:T(8,128)(2,1)S(1)}, u32[]{:S(2)}, u32[]{:S(2)}) async-start(bf16[4,512,352]{1,2,0:T(8,128)(2,1)} %fusion.4), calls=%async_computation.3 | async-start | bytes 2883584 | tf_op jit(solution)/shard_map/all_to_all | solution.py:128
  212.3 47.0 %collective-permute-start = (bf16[352,2048]{1,0:T(8,128)(2,1)S(1)}, bf16[352,2048]{1,0:T(8,128)(2,1)}, u32[]{:S(2)}, u32[]{:S(2)}) collective-permute-start(bf16[352,2048]{1,0:T(8,128)(2,1)S(1)} %bitcast.95), channel_id=1, source_target_pairs={{0,32},{32,64},{64,96},{96,0},{1,33},{33,65},{65,97},{97,1},{2,34}... | collective-permute-start | bytes 4325384 | tf_op jit(solution)/shard_map/ppermute | solution.py:76
  213.2 77.1 %collective-permute-start.1 = (bf16[352,2048]{1,0:T(8,128)(2,1)S(1)}, bf16[352,2048]{1,0:T(8,128)(2,1)}, u32[]{:S(2)}, u32[]{:S(2)}) collective-permute-start(bf16[352,2048]{1,0:T(8,128)(2,1)S(1)} %bitcast.96), channel_id=1, source_target_pairs={{0,64},{32,96},{64,0},{96,32},{1,65},{33,97},{65,1},{97,33},{2,66}... | collective-permute-start | bytes 4325384 | tf_op jit(solution)/shard_map/ppermute | solution.py:76
  213.7 79.2 %collective-permute-start.2 = (bf16[352,2048]{1,0:T(8,128)(2,1)S(1)}, bf16[352,2048]{1,0:T(8,128)(2,1)}, u32[]{:S(2)}, u32[]{:S(2)}) collective-permute-start(bf16[352,2048]{1,0:T(8,128)(2,1)S(1)} %bitcast.97), channel_id=1, source_target_pairs={{0,96},{32,0},{64,32},{96,64},{1,97},{33,1},{65,33},{97,65},{2,98}... | collective-permute-start | bytes 4325384 | tf_op jit(solution)/shard_map/ppermute | solution.py:76
  297.3 12.7 %copy-start.7 = (bf16[64,2048]{1,0:T(8,128)(2,1)S(1)}, bf16[64,2048]{1,0:T(8,128)(2,1)}, u32[]{:S(2)}) copy-start(bf16[64,2048]{1,0:T(8,128)(2,1)} %copy-done.6) | copy-start | bytes 786436
  297.3 38.4 %all-to-all-start.4 = ((bf16[32,16,2048]{2,1,0:T(8,128)(2,1)}), bf16[32,16,2048]{2,1,0:T(8,128)(2,1)}, u32[]{:S(2)}, u32[]{:S(2)}) async-start(bf16[32,16,2048]{2,1,0:T(8,128)(2,1)} %bitcast.24), calls=%async_computation.4 | async-start | bytes 4194304 | tf_op jit(solution)/shard_map/all_to_all | solution.py:135
  310.0 25.7 %copy-start.11 = (f32[64,6]{0,1:T(8,128)S(1)}, f32[64,6]{0,1:T(8,128)}, u32[]{:S(2)}) copy-start(f32[64,6]{0,1:T(8,128)} %param.18) | copy-start | bytes 4612
  317.3 21.2 %copy-start.2 = (f32[64,2048]{1,0:T(8,128)S(1)}, f32[64,2048]{1,0:T(8,128)}, u32[]{:S(2)}) copy-start(f32[64,2048]{1,0:T(8,128)} %shard_map.118) | copy-start | bytes 1572868
  335.7 2.9 copy-start.4
  335.7 2.9 copy-start.8
  335.7 7.4 %copy-start.1 = (bf16[1,2,352,2048]{3,2,1,0:T(8,128)(2,1)S(1)}, bf16[1,2,352,2048]{3,2,1,0:T(8,128)(2,1)}, u32[]{:S(2)}) copy-start(bf16[1,2,352,2048]{3,2,1,0:T(8,128)(2,1)} %param.22) | copy-start | bytes 8650756
Sparse Core Ops, SparseCore 0:
  15.7 48.2 all-gather.1

commit v7 on v6

--- a/solution.py
+++ b/solution.py
@@ -70,12 +70,6 @@
     matches = (page_dest[None, :] == group_ids[:, None]).astype(jnp.int32)
     dest_order = jnp.sum(matches * group_ids[None, :], axis=1)
 
-    down_parts = [expert_down[0]]
-    for shift in range(1, groups):
-        down_parts.append(
-            lax.ppermute(expert_down[0], "req", [(i, (i + shift) % groups) for i in range(groups)])
-        )
-
     def by_dest(array_in):
         return jnp.take(array_in.reshape(groups, page_rows, array_in.shape[1]), dest_order, axis=0)
 
@@ -85,6 +79,15 @@
     widths = (hidden_in.shape[1], queries.shape[1])
     packed = jnp.concatenate((hidden_in, queries), axis=1)
     moved = lax.all_to_all(by_dest(packed), "req", split_axis=0, concat_axis=0, tiled=True)
+    down_own, moved = lax.optimization_barrier((expert_down[0], moved))
+    down_parts = [down_own]
+    for shift in range(1, groups):
+        down_parts.append(
+            lax.ppermute(
+                down_own, "req", [(i, (i + shift) % groups) for i in range(groups)]
+            )
+        )
+
     moved = moved.reshape(token_rows, sum(widths))
     resid = moved[:, : widths[0]]
     rows_of_queries = moved[:, widths[0] :]

time: 355 us -> 355 us (level)
  no operation moved by 1% of the time
where the time goes in v7:
time: 355 us; the launch traced here: 350 us
  waiting for transfers between devices  124 us (35%)
  blocking collectives  112 us (32%)
  matrix products  32.6 us (9%)
  starting transfers between devices  25.4 us (7%)
  local copies, waits for them, and re-layouts  18.9 us (5%)
  between operations  13.6 us (4%)
  other arithmetic  13 us (4%)
  Pallas kernels  11.2 us (3%)
    all_to_all x1, blocking collectives, layer(): lax.all_to_all(copies, ('req', 'head'), split_axis=0, concat_axis=0, tile...  105 us
    ppermute x3, waiting for transfers between devices, layer(): lax.ppermute(down_own, 'req', [(i, (i + shift) % groups) for i in range(g...  58 us
    all_gather x1, waiting for transfers between devices, layer(): kv_piece = lax.all_gather(key_value_rows, 'head', axis=0, tiled=True)  32.9 us
    all_to_all x1, waiting for transfers between devices, layer(): lax.all_to_all(out_rows.astype(jnp.bfloat16).reshape(columns, local_exper...  18.4 us
    all_to_all x1, waiting for transfers between devices, layer(): lax.all_to_all(hidden, 'req', split_axis=0, concat_axis=0, tiled=True)  13.8 us
    all_to_all x1, starting transfers between devices, layer(): lax.all_to_all(out_rows.astype(jnp.bfloat16).reshape(columns, local_exper...  12.7 us
    pallas_call x1, Pallas kernels, attention(): pl.pallas_call(functools.partial(attn_kernel, heads=16, kv_heads=4, size=...  11.2 us
    dot_general x4, matrix products, layer(): jnp.dot(hidden_part, down_parts[shift], preferred_element_type=jnp.float32)  11 us
  transfers between devices with their start and end apart: 7, of which 6 were waited for; matrix products, arithmetic and copies ran while one was open for 7% of the time, Pallas kernels for 0%

profile of v7, /device:TPU:53, one launch (start us, length us, event | category | flops | bytes accessed | tf_op | source)
XLA Modules:
  0.0 350.0 jit_solution(7529291611606073415)
XLA Ops:
  6.5 0.9 select_reduce_fusion
  7.5 1.5 gather_fusion.1
  9.1 6.5 %all_to_all.25 = bf16[4,16,1024]{2,1,0:T(8,128)(2,1)} all-to-all(bf16[4,16,1024]{2,1,0:T(8,128)(2,1)S(1)} %broadcast_select_fusion.1), channel_id=1, replica_groups=mesh['req'=4,'head'=32] {'req'}, dimensions={0} | all-to-all | bytes 262144 | tf_op jit(solution)/shard_map/all_to_all | solution.py:76
  15.6 1.1 pad_maximum_fusion
  16.7 1.4 gather_fusion
  18.1 1.9 broadcast_select_fusion
  20.0 5.9 %all-to-all-start = ((bf16[4,16,4096]{2,1,0:T(8,128)(2,1)}), bf16[4,16,4096]{2,1,0:T(8,128)(2,1)S(1)}, u32[]{:S(2)}, u32[]{:S(2)}) async-start(bf16[4,16,4096]{2,1,0:T(8,128)(2,1)} %broadcast_select_fusion), calls=%async_computation | async-start | bytes 1048576 | tf_op jit(solution)/shard_map/all_to_all | solution.py:81
  31.1 32.9 %all-gather.2.cloned.1.call-done.kv_ref = bf16[2048,1024]{1,0:T(8,128)(2,1)} async-done(((bf16[64,1024]{1,0:T(8,128)(2,1)}), bf16[2048,1024]{1,0:T(8,128)(2,1)}) %all-gather.2.cloned.1.call-update) | async-done | bytes 4194320 | tf_op jit(solution)/shard_map/all_gather | solution.py:78
  64.7 11.2 %shard_map.118 = f32[64,2048]{1,0:T(8,128)} custom-call(bf16[64,2048]{1,0:T(8,128)(2,1)} %slice.37.q_ref, bf16[2048,1024]{1,0:T(8,128)(2,1)} %all-gather.2.cloned.1.call-done.kv_ref, s32[64,1]{1,0:T(8,128)} %copy.39.segq_ref, s32[1,2048]{1,0:T(1,128)} %bitcast.100, s32[64,1]{1,0:T(8,128)} %iota_add_fusion.posq_ref, s32[1,2048]{1,0:T(1,128)} %iota.38.posk_ref), custom_call_target="tpu_custom_call" | custom-call | tf_op jit(solution)/shard_map/pallas_call | solution.py:42
  75.8 1.2 multiply_reduce_fusion.1
  77.1 1.2 multiply_convert_fusion
  79.0 1.1 broadcast_in_dim.42
  80.1 105.0 %all_to_all.26 = bf16[128,16,2048]{2,1,0:T(8,128)(2,1)S(1)} all-to-all(bf16[128,16,2048]{2,1,0:T(8,128)(2,1)S(1)} %bitcast.86), channel_id=1, replica_groups=mesh['req'=4,'head'=32] {'req','head'}, dimensions={0} | all-to-all | bytes 16777216 | tf_op jit(solution)/shard_map/all_to_all | solution.py:124
  185.1 6.3 %fusion.2 = f32[2048,2,352]{0,2,1:T(8,128)S(1)} fusion(bf16[2048,2048,1]{1,0,2:T(8,128)(2,1)S(1)} %bitcast.88, bf16[1,2,352,2048]{3,2,1,0:T(8,128)(2,1)S(1)} %copy-done), kind=kOutput, calls=%fused_computation.7 | convolution fusion | flops 5905580032 | bytes 17039360 | tf_op jit(solution)/shard_map/nd,kfd->nkf/dot_general | solution.py:126
  191.4 2.8 fusion.39
  194.2 3.7 %squeeze.35 = f32[4,512,352]{1,0,2:T(4,128)S(1)} reshape(f32[2048,1,352]{0,2,1:T(8,128)} %get-tuple-element.9) | data formatting | bytes 5767168 | tf_op jit(solution)/shard_map/squeeze | solution.py:129
  197.8 4.9 %squeeze.36 = f32[4,512,352]{1,0,2:T(4,128)} reshape(f32[2048,1,352]{0,2,1:T(8,128)} %get-tuple-element.10) | data formatting | bytes 5767168 | tf_op jit(solution)/shard_map/squeeze | solution.py:129
  202.8 4.8 %fusion.4 = bf16[4,512,352]{1,2,0:T(8,128)(2,1)} fusion(f32[4,512,352]{1,0,2:T(4,128)} %squeeze.36, f32[4,512,352]{1,0,2:T(4,128)S(1)} %squeeze.35), kind=kLoop, calls=%fused_computation.10 | loop fusion | flops 3604480 | bytes 7208960 | tf_op jit(solution)/shard_map/convert_element_type | solution.py:129
  207.6 4.7 %all-to-all-start.3 = ((bf16[4,512,352]{1,2,0:T(8,128)(2,1)}), bf16[4,512,352]{1,2,0:T(8,128)(2,1)S(1)}, u32[]{:S(2)}, u32[]{:S(2)}) async-start(bf16[4,512,352]{1,2,0:T(8,128)(2,1)} %fusion.4), calls=%async_computation.3 | async-start | bytes 2883584 | tf_op jit(solution)/shard_map/all_to_all | solution.py:131
  212.3 0.9 collective-permute-start
  214.4 13.8 %all-to-all-done.3 = bf16[4,512,352]{1,2,0:T(8,128)(2,1)S(1)} async-done(((bf16[4,512,352]{1,2,0:T(8,128)(2,1)}), bf16[4,512,352]{1,2,0:T(8,128)(2,1)S(1)}, u32[]{:S(2)}, u32[]{:S(2)}) %all-to-all-start.3) | async-done | bytes 1441824 | tf_op jit(solution)/shard_map/all_to_all | solution.py:131
  228.3 1.3 fusion.21
  229.6 29.7 %collective-permute-done = bf16[352,2048]{1,0:T(8,128)(2,1)} collective-permute-done((bf16[352,2048]{1,0:T(8,128)(2,1)S(1)}, bf16[352,2048]{1,0:T(8,128)(2,1)}, u32[]{:S(2)}, u32[]{:S(2)}) %collective-permute-start) | collective-permute-done | bytes 1441824 | tf_op jit(solution)/shard_map/ppermute | solution.py:86
  259.2 2.6 fusion.19
  261.9 28.4 %collective-permute-done.1 = bf16[352,2048]{1,0:T(8,128)(2,1)} collective-permute-done((bf16[352,2048]{1,0:T(8,128)(2,1)S(1)}, bf16[352,2048]{1,0:T(8,128)(2,1)}, u32[]{:S(2)}, u32[]{:S(2)}) %collective-permute-start.1) | collective-permute-done | bytes 1441824 | tf_op jit(solution)/shard_map/ppermute | solution.py:86
  290.2 2.6 fusion.17
  292.9 4.4 %add_convert_fusion = bf16[512,2048]{1,0:T(8,128)(2,1)} fusion(f32[512,2048]{1,0:T(8,128)S(1)} %fusion.17, f32[512,2048]{1,0:T(8,128)S(1)} %fusion.21, f32[512,2048]{1,0:T(8,128)S(1)} %fusion.19, bf16[352,2048]{1,0:T(8,128)(2,1)} %collective-permute-done.2, bf16[4,512,352]{1,2,0:T(8,128)(2,1)S(1)} %all-to-all-done.3, s32[]{:T(128)S(6)} %select_n.73), kind=kOutput, calls=%fused_computation.4 | convolution fusion | flops 742391808 | bytes 16482308 | tf_op jit(solution)/shard_map/dot_general | solution.py:136
  297.3 12.7 %all-to-all-start.4 = ((bf16[32,16,2048]{2,1,0:T(8,128)(2,1)}), bf16[32,16,2048]{2,1,0:T(8,128)(2,1)}, u32[]{:S(2)}, u32[]{:S(2)}) async-start(bf16[32,16,2048]{2,1,0:T(8,128)(2,1)} %bitcast.24), calls=%async_computation.4 | async-start | bytes 4194304 | tf_op jit(solution)/shard_map/all_to_all | solution.py:138
  310.0 7.3 %fusion = f32[64,2,1408]{2,0,1:T(8,128)} fusion(bf16[2048,2,1408]{2,1,0:T(2,128)(2,1)} %param.20, bf16[64,2048]{1,0:T(8,128)(2,1)S(1)} %copy-done.7), kind=kOutput, calls=%fused_computation.2 | convolution fusion | flops 738197504 | bytes 12517376 | tf_op jit(solution)/shard_map/td,dkf->tkf/dot_general | solution.py:116
  317.3 18.4 %all-to-all-done.4 = bf16[32,16,2048]{2,1,0:T(8,128)(2,1)} async-done(((bf16[32,16,2048]{2,1,0:T(8,128)(2,1)}), bf16[32,16,2048]{2,1,0:T(8,128)(2,1)}, u32[]{:S(2)}, u32[]{:S(2)}) %all-to-all-start.4) | async-done | bytes 2097184 | tf_op jit(solution)/shard_map/all_to_all | solution.py:138
  335.7 2.8 multiply_reduce_fusion
  338.6 4.5 %fusion.6 = bf16[64,2048]{1,0:T(8,128)(2,1)} fusion(f32[64,2048]{1,0:T(8,128)S(1)} %multiply_reduce_fusion, bf16[1408,2048]{1,0:T(8,128)(2,1)} %param.21, f32[64,2,1408]{2,0,1:T(8,128)S(1)} %copy-done.8, f32[64,2048]{1,0:T(8,128)S(1)} %copy-done.2, bf16[64,4096]{1,0:T(8,128)(2,1)S(1)} %bitcast.92), kind=kOutput, calls=%fused_computation.13 | convolution fusion | flops 370204672 | bytes 8060928 | tf_op jit(solution)/shard_map/dot_general | solution.py:120
  (53 shorter events, 8.1 us)
Async XLA Ops:
  6.5 178.6 %copy-start = (bf16[1,2,352,2048]{3,2,1,0:T(8,128)(2,1)S(1)}, bf16[1,2,352,2048]{3,2,1,0:T(8,128)(2,1)}, u32[]{:S(2)}) copy-start(bf16[1,2,352,2048]{3,2,1,0:T(8,128)(2,1)} %param.22) | copy-start | bytes 8650756
  6.5 19.3 %copy-start.9 = (s32[64,6]{0,1:T(8,128)S(1)}, s32[64,6]{0,1:T(8,128)}, u32[]{:S(2)}) copy-start(s32[64,6]{0,1:T(8,128)} %param.17) | copy-start | bytes 4612
  6.5 57.5 %all-gather.2.cloned.1.call-start = ((), (), s32[]{:S(2)}) async-start(), calls=%async_computation.5 | async-start | bytes 4325376 | tf_op jit(solution)/shard_map/all_gather | solution.py:78
  20.0 10.4 %all-to-all-start = ((bf16[4,16,4096]{2,1,0:T(8,128)(2,1)}), bf16[4,16,4096]{2,1,0:T(8,128)(2,1)S(1)}, u32[]{:S(2)}, u32[]{:S(2)}) async-start(bf16[4,16,4096]{2,1,0:T(8,128)(2,1)} %broadcast_select_fusion), calls=%async_computation | async-start | bytes 1048576 | tf_op jit(solution)/shard_map/all_to_all | solution.py:81
  30.4 46.7 %copy-start.3 = (bf16[4,16,4096]{2,1,0:T(8,128)(2,1)}, bf16[4,16,4096]{2,1,0:T(8,128)(2,1)S(1)}, u32[]{:S(2)}) copy-start(bf16[4,16,4096]{2,1,0:T(8,128)(2,1)S(1)} %all-to-all-done) | copy-start | bytes 1572868
  64.6 12.4 %copy-start.10 = (f32[2048]{0:T(1024)S(1)}, f32[2048]{0:T(1024)}, u32[]{:S(2)}) copy-start(f32[2048]{0:T(1024)} %param.19) | copy-start | bytes 24580
  78.2 1.9 copy-start.6
  207.6 4.7 %copy-start.5 = (bf16[1,352,2048]{2,1,0:T(8,128)(2,1)S(1)}, bf16[1,352,2048]{2,1,0:T(8,128)(2,1)}, u32[]{:S(2)}) copy-start(bf16[1,352,2048]{2,1,0:T(8,128)(2,1)} %param.23) | copy-start | bytes 4325380
  207.6 20.7 %all-to-all-start.3 = ((bf16[4,512,352]{1,2,0:T(8,128)(2,1)}), bf16[4,512,352]{1,2,0:T(8,128)(2,1)S(1)}, u32[]{:S(2)}, u32[]{:S(2)}) async-start(bf16[4,512,352]{1,2,0:T(8,128)(2,1)} %fusion.4), calls=%async_computation.3 | async-start | bytes 2883584 | tf_op jit(solution)/shard_map/all_to_all | solution.py:131
  212.3 47.0 %collective-permute-start = (bf16[352,2048]{1,0:T(8,128)(2,1)S(1)}, bf16[352,2048]{1,0:T(8,128)(2,1)}, u32[]{:S(2)}, u32[]{:S(2)}) collective-permute-start(bf16[352,2048]{1,0:T(8,128)(2,1)S(1)} %bitcast.94), channel_id=1, source_target_pairs={{0,32},{32,64},{64,96},{96,0},{1,33},{33,65},{65,97},{97,1},{2,34}... | collective-permute-start | bytes 4325384 | tf_op jit(solution)/shard_map/ppermute | solution.py:86
  213.2 77.1 %collective-permute-start.1 = (bf16[352,2048]{1,0:T(8,128)(2,1)S(1)}, bf16[352,2048]{1,0:T(8,128)(2,1)}, u32[]{:S(2)}, u32[]{:S(2)}) collective-permute-start(bf16[352,2048]{1,0:T(8,128)(2,1)S(1)} %bitcast.95), channel_id=1, source_target_pairs={{0,64},{32,96},{64,0},{96,32},{1,65},{33,97},{65,1},{97,33},{2,66}... | collective-permute-start | bytes 4325384 | tf_op jit(solution)/shard_map/ppermute | solution.py:86
  213.7 79.2 %collective-permute-start.2 = (bf16[352,2048]{1,0:T(8,128)(2,1)S(1)}, bf16[352,2048]{1,0:T(8,128)(2,1)}, u32[]{:S(2)}, u32[]{:S(2)}) collective-permute-start(bf16[352,2048]{1,0:T(8,128)(2,1)S(1)} %bitcast.96), channel_id=1, source_target_pairs={{0,96},{32,0},{64,32},{96,64},{1,97},{33,1},{65,33},{97,65},{2,98}... | collective-permute-start | bytes 4325384 | tf_op jit(solution)/shard_map/ppermute | solution.py:86
  297.3 12.7 %copy-start.7 = (bf16[64,2048]{1,0:T(8,128)(2,1)S(1)}, bf16[64,2048]{1,0:T(8,128)(2,1)}, u32[]{:S(2)}) copy-start(bf16[64,2048]{1,0:T(8,128)(2,1)} %copy-done.6) | copy-start | bytes 786436
  297.3 38.4 %all-to-all-start.4 = ((bf16[32,16,2048]{2,1,0:T(8,128)(2,1)}), bf16[32,16,2048]{2,1,0:T(8,128)(2,1)}, u32[]{:S(2)}, u32[]{:S(2)}) async-start(bf16[32,16,2048]{2,1,0:T(8,128)(2,1)} %bitcast.24), calls=%async_computation.4 | async-start | bytes 4194304 | tf_op jit(solution)/shard_map/all_to_all | solution.py:138
  310.0 25.7 %copy-start.11 = (f32[64,6]{0,1:T(8,128)S(1)}, f32[64,6]{0,1:T(8,128)}, u32[]{:S(2)}) copy-start(f32[64,6]{0,1:T(8,128)} %param.18) | copy-start | bytes 4612
  317.3 21.2 %copy-start.2 = (f32[64,2048]{1,0:T(8,128)S(1)}, f32[64,2048]{1,0:T(8,128)}, u32[]{:S(2)}) copy-start(f32[64,2048]{1,0:T(8,128)} %shard_map.118) | copy-start | bytes 1572868
  335.7 2.9 copy-start.4
  335.7 2.9 copy-start.8
  335.7 7.4 %copy-start.1 = (bf16[1,2,352,2048]{3,2,1,0:T(8,128)(2,1)S(1)}, bf16[1,2,352,2048]{3,2,1,0:T(8,128)(2,1)}, u32[]{:S(2)}) copy-start(bf16[1,2,352,2048]{3,2,1,0:T(8,128)(2,1)} %param.22) | copy-start | bytes 8650756
Sparse Core Ops, SparseCore 0:
  15.7 48.2 all-gather.1

commit v8 on v6

--- a/solution.py
+++ b/solution.py
@@ -70,12 +70,6 @@
     matches = (page_dest[None, :] == group_ids[:, None]).astype(jnp.int32)
     dest_order = jnp.sum(matches * group_ids[None, :], axis=1)
 
-    down_parts = [expert_down[0]]
-    for shift in range(1, groups):
-        down_parts.append(
-            lax.ppermute(expert_down[0], "req", [(i, (i + shift) % groups) for i in range(groups)])
-        )
-
     def by_dest(array_in):
         return jnp.take(array_in.reshape(groups, page_rows, array_in.shape[1]), dest_order, axis=0)
 
@@ -85,6 +79,14 @@
     widths = (hidden_in.shape[1], queries.shape[1])
     packed = jnp.concatenate((hidden_in, queries), axis=1)
     moved = lax.all_to_all(by_dest(packed), "req", split_axis=0, concat_axis=0, tiled=True)
+    gate_own, down_own, moved = lax.optimization_barrier(
+        (expert_gate_up[0], expert_down[0], moved)
+    )
+    gate_parts, down_parts = [gate_own], [down_own]
+    for shift in range(1, groups):
+        ring = [(i, (i + shift) % groups) for i in range(groups)]
+        gate_parts.append(lax.ppermute(gate_own, "req", ring))
+        down_parts.append(lax.ppermute(down_own, "req", ring))
     moved = moved.reshape(token_rows, sum(widths))
     resid = moved[:, : widths[0]]
     rows_of_queries = moved[:, widths[0] :]
@@ -115,21 +117,15 @@
     )
     shared_hidden = silu_mul(shared_both[:, 0], shared_both[:, 1]).astype(jnp.bfloat16)
     shared_out = jnp.dot(shared_hidden, shared_down, preferred_element_type=jnp.float32)
-    copies = jnp.broadcast_to(outgoing[None], (groups,) + outgoing.shape).reshape(
-        groups * columns, local_experts * SLOT, model_width
-    )
-    arrived = lax.all_to_all(copies, ("req", "head"), split_axis=0, concat_axis=0, tiled=True)
+    arrived = lax.all_to_all(outgoing, "head", split_axis=0, concat_axis=0, tiled=True)
     expert_rows = arrived.reshape(-1, model_width)
-    both_parts = jnp.einsum(
-        "nd,kfd->nkf", expert_rows, expert_gate_up[0], preferred_element_type=jnp.float32
-    )
-    hidden = silu_mul(both_parts[:, 0], both_parts[:, 1]).astype(jnp.bfloat16)
-    hidden = hidden.reshape(groups, columns * local_experts * SLOT, hidden.shape[-1])
-    hidden_parts = lax.all_to_all(hidden, "req", split_axis=0, concat_axis=0, tiled=True)
     out_rows = None
     for shift in range(groups):
-        part_index = (lax.axis_index("req") - shift) % groups
-        hidden_part = lax.dynamic_index_in_dim(hidden_parts, part_index, 0, keepdims=False)
+        gate_value = jnp.dot(
+            expert_rows, gate_parts[shift][0].T, preferred_element_type=jnp.float32
+        )
+        upward = jnp.dot(expert_rows, gate_parts[shift][1].T, preferred_element_type=jnp.float32)
+        hidden_part = silu_mul(gate_value, upward).astype(jnp.bfloat16)
         product = jnp.dot(hidden_part, down_parts[shift], preferred_element_type=jnp.float32)
         out_rows = product if out_rows is None else out_rows + product
     returned = lax.all_to_all(

time: 355 us -> 344 us (0.969)
  the two profiles are of different devices: /device:TPU:53 before, /device:TPU:1 now
where the time goes in v8:
time: 344 us; the launch traced here: 343 us
  waiting for transfers between devices  216 us (63%)
  matrix products  55.7 us (16%)
  starting transfers between devices  24.2 us (7%)
  between operations  13.6 us (4%)
  Pallas kernels  11.2 us (3%)
  blocking collectives  9.73 us (3%)
  other arithmetic  7.09 us (2%)
  local copies, waits for them, and re-layouts  5.02 us (1%)
    ppermute x3, waiting for transfers between devices, layer(): gate_parts.append(lax.ppermute(gate_own, 'req', ring))  86.2 us
    ppermute x3, waiting for transfers between devices, layer(): down_parts.append(lax.ppermute(down_own, 'req', ring))  49.2 us
    all_gather x1, waiting for transfers between devices, layer(): kv_piece = lax.all_gather(key_value_rows, 'head', axis=0, tiled=True)  34.7 us
    dot_general x4, matrix products, layer(): jnp.dot(hidden_part, down_parts[shift], preferred_element_type=jnp.float32)  28.1 us
    all_to_all x1, waiting for transfers between devices, layer(): lax.all_to_all(outgoing, 'head', split_axis=0, concat_axis=0, tiled=True)  22.3 us
    all_to_all x1, waiting for transfers between devices, layer(): lax.all_to_all(out_rows.astype(jnp.bfloat16).reshape(columns, local_exper...  21.1 us
    pallas_call x1, Pallas kernels, attention(): pl.pallas_call(functools.partial(attn_kernel, heads=16, kv_heads=4, size=...  11.2 us
    all_to_all x1, blocking collectives, layer(): lax.all_to_all(by_dest(keys_values), 'req', split_axis=0, concat_axis=0,...  9.73 us
  transfers between devices with their start and end apart: 10, of which 8 were waited for; matrix products, arithmetic and copies ran while one was open for 13% of the time, Pallas kernels for 0%

profile of v8, /device:TPU:1, one launch (start us, length us, event | category | flops | bytes accessed | tf_op | source)
XLA Modules:
  0.0 342.8 jit_solution(15890499365180484270)
XLA Ops:
  8.1 9.7 %all_to_all.20 = bf16[4,16,1024]{2,1,0:T(8,128)(2,1)} all-to-all(bf16[4,16,1024]{2,1,0:T(8,128)(2,1)S(1)} %broadcast_select_fusion.1), channel_id=1, replica_groups=mesh['req'=4,'head'=32] {'req'}, dimensions={0} | all-to-all | bytes 262144 | tf_op jit(solution)/shard_map/all_to_all | solution.py:76
  17.9 1.1 pad_maximum_fusion
  20.4 3.5 %all-to-all-start = ((bf16[4,16,4096]{2,1,0:T(8,128)(2,1)}), bf16[4,16,4096]{2,1,0:T(8,128)(2,1)S(1)}, u32[]{:S(2)}, u32[]{:S(2)}) async-start(bf16[4,16,4096]{2,1,0:T(8,128)(2,1)} %broadcast_select_fusion), calls=%async_computation | async-start | bytes 1048576 | tf_op jit(solution)/shard_map/all_to_all | solution.py:81
  28.1 3.0 all-to-all-done
  31.8 34.7 %all-gather.2.cloned.1.call-done.kv_ref = bf16[2048,1024]{1,0:T(8,128)(2,1)} async-done(((bf16[64,1024]{1,0:T(8,128)(2,1)}), bf16[2048,1024]{1,0:T(8,128)(2,1)}) %all-gather.2.cloned.1.call-update) | async-done | bytes 4194320 | tf_op jit(solution)/shard_map/all_gather | solution.py:78
  67.0 11.2 %shard_map.118 = f32[64,2048]{1,0:T(8,128)} custom-call(bf16[64,2048]{1,0:T(8,128)(2,1)} %slice.61.q_ref, bf16[2048,1024]{1,0:T(8,128)(2,1)} %all-gather.2.cloned.1.call-done.kv_ref, s32[64,1]{1,0:T(8,128)} %copy.33.segq_ref, s32[1,2048]{1,0:T(1,128)} %bitcast.130, s32[64,1]{1,0:T(8,128)} %iota_add_fusion.posq_ref, s32[1,2048]{1,0:T(1,128)} %iota.38.posk_ref), custom_call_target="tpu_custom_call" | custom-call | tf_op jit(solution)/shard_map/pallas_call | solution.py:42
  78.2 1.2 multiply_reduce_fusion.1
  79.5 1.2 multiply_convert_fusion.3
  80.6 2.1 convolution_convert_fusion
  82.7 5.3 %all-to-all-start.2 = ((bf16[32,16,2048]{2,1,0:T(8,128)(2,1)}), bf16[32,16,2048]{2,1,0:T(8,128)(2,1)S(1)}, u32[]{:S(2)}, u32[]{:S(2)}) async-start(bf16[32,16,2048]{2,1,0:T(8,128)(2,1)} %bitcast.122), calls=%async_computation.2 | async-start | bytes 4194304 | tf_op jit(solution)/shard_map/all_to_all | solution.py:120
  88.0 1.3 collective-permute-start
  89.3 2.4 collective-permute-start.2
  91.8 1.2 collective-permute-start.4
  94.1 22.3 %all-to-all-done.2 = bf16[32,16,2048]{2,1,0:T(8,128)(2,1)S(1)} async-done(((bf16[32,16,2048]{2,1,0:T(8,128)(2,1)}), bf16[32,16,2048]{2,1,0:T(8,128)(2,1)S(1)}, u32[]{:S(2)}, u32[]{:S(2)}) %all-to-all-start.2) | async-done | bytes 2097184 | tf_op jit(solution)/shard_map/all_to_all | solution.py:120
  116.4 3.2 fusion.12
  119.5 6.1 %fusion.23 = f32[512,2048]{1,0:T(8,128)} fusion(bf16[352,2048]{1,0:T(8,128)(2,1)} %bitcast.139, bf16[512,2048]{1,0:T(8,128)(2,1)S(1)} %bitcast.114, bf16[2,352,2048]{2,1,0:T(8,128)(2,1)} %bitcast.136, f32[512,352]{0,1:T(8,128)} %fusion.12), kind=kOutput, calls=%fused_computation.30 | convolution fusion | flops 1477296128 | bytes 9895936 | tf_op jit(solution)/shard_map/dot_general | solution.py:129
  125.7 27.8 %collective-permute-done = bf16[2,352,2048]{2,1,0:T(8,128)(2,1)} collective-permute-done((bf16[2,352,2048]{2,1,0:T(8,128)(2,1)}, bf16[2,352,2048]{2,1,0:T(8,128)(2,1)}, u32[]{:S(2)}, u32[]{:S(2)}) %collective-permute-start) | collective-permute-done | bytes 2883616 | tf_op jit(solution)/shard_map/ppermute | solution.py:88
  153.4 1.2 collective-permute-start.5
  154.7 3.2 fusion.8
  157.9 58.4 %collective-permute-done.2 = bf16[2,352,2048]{2,1,0:T(8,128)(2,1)} collective-permute-done((bf16[2,352,2048]{2,1,0:T(8,128)(2,1)}, bf16[2,352,2048]{2,1,0:T(8,128)(2,1)}, u32[]{:S(2)}, u32[]{:S(2)}) %collective-permute-start.2) | collective-permute-done | bytes 2883616 | tf_op jit(solution)/shard_map/ppermute | solution.py:88
  216.2 3.2 fusion.6
  219.4 3.2 fusion.4
  222.6 23.5 %collective-permute-done.1 = bf16[352,2048]{1,0:T(8,128)(2,1)} collective-permute-done((bf16[352,2048]{1,0:T(8,128)(2,1)}, bf16[352,2048]{1,0:T(8,128)(2,1)}, u32[]{:S(2)}, u32[]{:S(2)}) %collective-permute-start.1) | collective-permute-done | bytes 1441824 | tf_op jit(solution)/shard_map/ppermute | solution.py:89
  246.1 6.3 %fusion.33 = f32[512,2048]{1,0:T(8,128)} fusion(bf16[352,2048]{1,0:T(8,128)(2,1)} %collective-permute-done.1, f32[512,352]{0,1:T(8,128)} %fusion.8, bf16[512,2048]{1,0:T(8,128)(2,1)S(1)} %bitcast.118, bf16[2,352,2048]{2,1,0:T(8,128)(2,1)} %collective-permute-done), kind=kOutput, calls=%fused_computation.48 | convolution fusion | flops 1477296128 | bytes 9895936 | tf_op jit(solution)/shard_map/dot_general | solution.py:129
  252.4 25.6 %collective-permute-done.3 = bf16[352,2048]{1,0:T(8,128)(2,1)} collective-permute-done((bf16[352,2048]{1,0:T(8,128)(2,1)}, bf16[352,2048]{1,0:T(8,128)(2,1)}, u32[]{:S(2)}, u32[]{:S(2)}) %collective-permute-start.3) | collective-permute-done | bytes 1441824 | tf_op jit(solution)/shard_map/ppermute | solution.py:89
  278.0 6.3 %fusion.34 = f32[512,2048]{1,0:T(8,128)} fusion(bf16[352,2048]{1,0:T(8,128)(2,1)} %collective-permute-done.3, f32[512,352]{0,1:T(8,128)} %fusion.6, bf16[512,2048]{1,0:T(8,128)(2,1)S(1)} %bitcast.119, bf16[2,352,2048]{2,1,0:T(8,128)(2,1)} %collective-permute-done.2), kind=kOutput, calls=%fused_computation.49 | convolution fusion | flops 1477296128 | bytes 9895936 | tf_op jit(solution)/shard_map/dot_general | solution.py:129
  284.3 9.5 %add_convert_fusion = bf16[512,2048]{1,0:T(8,128)(2,1)} fusion(f32[512,2048]{1,0:T(8,128)} %fusion.34, f32[512,2048]{1,0:T(8,128)} %fusion.23, f32[512,2048]{1,0:T(8,128)} %fusion.33, bf16[352,2048]{1,0:T(8,128)(2,1)} %collective-permute-done.5, f32[512,352]{0,1:T(8,128)} %fusion.4, bf16[512,2048]{1,0:T(8,128)(2,1)S(1)} %bitcast.120, ...), kind=kOutput, calls=%fused_computation.4 | convolution fusion | flops 1481490432 | bytes 20381696 | tf_op jit(solution)/shard_map/dot_general | solution.py:129
  293.8 8.1 %all-to-all-start.3 = ((bf16[32,16,2048]{2,1,0:T(8,128)(2,1)}), bf16[32,16,2048]{2,1,0:T(8,128)(2,1)S(1)}, u32[]{:S(2)}, u32[]{:S(2)}) async-start(bf16[32,16,2048]{2,1,0:T(8,128)(2,1)} %bitcast.121), calls=%async_computation.3 | async-start | bytes 4194304 | tf_op jit(solution)/shard_map/all_to_all | solution.py:131
  301.9 7.3 %fusion = f32[64,2,1408]{2,0,1:T(8,128)} fusion(bf16[2048,2,1408]{2,1,0:T(2,128)(2,1)} %param.20, bf16[64,2048]{1,0:T(8,128)(2,1)S(1)} %multiply_convert_fusion.3), kind=kOutput, calls=%fused_computation.2 | convolution fusion | flops 738197504 | bytes 12517376 | tf_op jit(solution)/shard_map/td,dkf->tkf/dot_general | solution.py:115
  309.1 21.1 %all-to-all-done.3 = bf16[32,16,2048]{2,1,0:T(8,128)(2,1)S(1)} async-done(((bf16[32,16,2048]{2,1,0:T(8,128)(2,1)}), bf16[32,16,2048]{2,1,0:T(8,128)(2,1)S(1)}, u32[]{:S(2)}, u32[]{:S(2)}) %all-to-all-start.3) | async-done | bytes 2097184 | tf_op jit(solution)/shard_map/all_to_all | solution.py:131
  330.2 1.0 multiply_reduce_fusion
  331.5 4.5 %fusion.3 = bf16[64,2048]{1,0:T(8,128)(2,1)} fusion(f32[64,2048]{1,0:T(8,128)S(1)} %multiply_reduce_fusion, bf16[1408,2048]{1,0:T(8,128)(2,1)} %param.21, f32[64,2,1408]{2,0,1:T(8,128)S(1)} %copy-done.3, f32[64,2048]{1,0:T(8,128)S(1)} %copy-done.2, bf16[64,4096]{1,0:T(8,128)(2,1)S(1)} %bitcast.126), kind=kOutput, calls=%fused_computation.9 | convolution fusion | flops 370204672 | bytes 8060928 | tf_op jit(solution)/shard_map/dot_general | solution.py:119
  (46 shorter events, 9.9 us)
Async XLA Ops:
  6.5 0.9 copy-start
  6.5 59.9 %all-gather.2.cloned.1.call-start = ((), (), s32[]{:S(2)}) async-start(), calls=%async_computation.4 | async-start | bytes 4325376 | tf_op jit(solution)/shard_map/all_gather | solution.py:78
  17.9 6.1 %copy-start.4 = (s32[64,6]{0,1:T(8,128)S(1)}, s32[64,6]{0,1:T(8,128)}, u32[]{:S(2)}) copy-start(s32[64,6]{0,1:T(8,128)} %param.17) | copy-start | bytes 4612
  20.4 10.6 %all-to-all-start = ((bf16[4,16,4096]{2,1,0:T(8,128)(2,1)}), bf16[4,16,4096]{2,1,0:T(8,128)(2,1)S(1)}, u32[]{:S(2)}, u32[]{:S(2)}) async-start(bf16[4,16,4096]{2,1,0:T(8,128)(2,1)} %broadcast_select_fusion), calls=%async_computation | async-start | bytes 1048576 | tf_op jit(solution)/shard_map/all_to_all | solution.py:81
  67.0 12.4 %copy-start.5 = (f32[2048]{0:T(1024)S(1)}, f32[2048]{0:T(1024)}, u32[]{:S(2)}) copy-start(f32[2048]{0:T(1024)} %param.19) | copy-start | bytes 24580
  82.7 33.7 %all-to-all-start.2 = ((bf16[32,16,2048]{2,1,0:T(8,128)(2,1)}), bf16[32,16,2048]{2,1,0:T(8,128)(2,1)S(1)}, u32[]{:S(2)}, u32[]{:S(2)}) async-start(bf16[32,16,2048]{2,1,0:T(8,128)(2,1)} %bitcast.122), calls=%async_computation.2 | async-start | bytes 4194304 | tf_op jit(solution)/shard_map/all_to_all | solution.py:120
  88.0 65.4 %collective-permute-start = (bf16[2,352,2048]{2,1,0:T(8,128)(2,1)}, bf16[2,352,2048]{2,1,0:T(8,128)(2,1)}, u32[]{:S(2)}, u32[]{:S(2)}) collective-permute-start(bf16[2,352,2048]{2,1,0:T(8,128)(2,1)} %bitcast.132), channel_id=1, source_target_pairs={{0,32},{32,64},{64,96},{96,0},{1,33},{33,65},{65,97},{97,1},{2,34}... | collective-permute-start | bytes 8650760 | tf_op jit(solution)/shard_map/ppermute | solution.py:88
  89.3 126.9 %collective-permute-start.2 = (bf16[2,352,2048]{2,1,0:T(8,128)(2,1)}, bf16[2,352,2048]{2,1,0:T(8,128)(2,1)}, u32[]{:S(2)}, u32[]{:S(2)}) collective-permute-start(bf16[2,352,2048]{2,1,0:T(8,128)(2,1)} %bitcast.133), channel_id=1, source_target_pairs={{0,64},{32,96},{64,0},{96,32},{1,65},{33,97},{65,1},{97,33},{2,66}... | collective-permute-start | bytes 8650760 | tf_op jit(solution)/shard_map/ppermute | solution.py:88
  91.8 127.7 %collective-permute-start.4 = (bf16[2,352,2048]{2,1,0:T(8,128)(2,1)}, bf16[2,352,2048]{2,1,0:T(8,128)(2,1)}, u32[]{:S(2)}, u32[]{:S(2)}) collective-permute-start(bf16[2,352,2048]{2,1,0:T(8,128)(2,1)} %bitcast.134), channel_id=1, source_target_pairs={{0,96},{32,0},{64,32},{96,64},{1,97},{33,1},{65,33},{97,65},{2,98}... | collective-permute-start | bytes 8650760 | tf_op jit(solution)/shard_map/ppermute | solution.py:88
  92.9 153.2 %collective-permute-start.1 = (bf16[352,2048]{1,0:T(8,128)(2,1)}, bf16[352,2048]{1,0:T(8,128)(2,1)}, u32[]{:S(2)}, u32[]{:S(2)}) collective-permute-start(bf16[352,2048]{1,0:T(8,128)(2,1)} %bitcast.137), channel_id=1, source_target_pairs={{0,32},{32,64},{64,96},{96,0},{1,33},{33,65},{65,97},{97,1},{2,34}... | collective-permute-start | bytes 4325384 | tf_op jit(solution)/shard_map/ppermute | solution.py:89
  93.2 184.8 %collective-permute-start.3 = (bf16[352,2048]{1,0:T(8,128)(2,1)}, bf16[352,2048]{1,0:T(8,128)(2,1)}, u32[]{:S(2)}, u32[]{:S(2)}) collective-permute-start(bf16[352,2048]{1,0:T(8,128)(2,1)} %bitcast.138), channel_id=1, source_target_pairs={{0,64},{32,96},{64,0},{96,32},{1,65},{33,97},{65,1},{97,33},{2,66}... | collective-permute-start | bytes 4325384 | tf_op jit(solution)/shard_map/ppermute | solution.py:89
  153.4 130.9 %collective-permute-start.5 = (bf16[352,2048]{1,0:T(8,128)(2,1)}, bf16[352,2048]{1,0:T(8,128)(2,1)}, u32[]{:S(2)}, u32[]{:S(2)}) collective-permute-start(bf16[352,2048]{1,0:T(8,128)(2,1)} %bitcast.140), channel_id=1, source_target_pairs={{0,96},{32,0},{64,32},{96,64},{1,97},{33,1},{65,33},{97,65},{2,98}... | collective-permute-start | bytes 4325384 | tf_op jit(solution)/shard_map/ppermute | solution.py:89
  293.8 36.4 %all-to-all-start.3 = ((bf16[32,16,2048]{2,1,0:T(8,128)(2,1)}), bf16[32,16,2048]{2,1,0:T(8,128)(2,1)S(1)}, u32[]{:S(2)}, u32[]{:S(2)}) async-start(bf16[32,16,2048]{2,1,0:T(8,128)(2,1)} %bitcast.121), calls=%async_computation.3 | async-start | bytes 4194304 | tf_op jit(solution)/shard_map/all_to_all | solution.py:131
  301.9 28.3 %copy-start.6 = (f32[64,6]{0,1:T(8,128)S(1)}, f32[64,6]{0,1:T(8,128)}, u32[]{:S(2)}) copy-start(f32[64,6]{0,1:T(8,128)} %param.18) | copy-start | bytes 4612
  330.2 1.1 copy-start.2
  330.2 1.3 copy-start.3
  330.2 5.8 %copy-start.1 = (bf16[64,1024]{1,0:T(8,128)(2,1)S(1)}, bf16[64,1024]{1,0:T(8,128)(2,1)}, u32[]{:S(2)}) copy-start(bf16[64,1024]{1,0:T(8,128)(2,1)} %param.14) | copy-start | bytes 393220
Sparse Core Ops, SparseCore 0:
  18.0 48.4 all-gather.1

commit v9 on v8

--- a/solution.py
+++ b/solution.py
@@ -82,11 +82,24 @@
     gate_own, down_own, moved = lax.optimization_barrier(
         (expert_gate_up[0], expert_down[0], moved)
     )
-    gate_parts, down_parts = [gate_own], [down_own]
-    for shift in range(1, groups):
-        ring = [(i, (i + shift) % groups) for i in range(groups)]
-        gate_parts.append(lax.ppermute(gate_own, "req", ring))
-        down_parts.append(lax.ppermute(down_own, "req", ring))
+    upward_ring = [(i, (i + 1) % groups) for i in range(groups)]
+    downward_ring = [(i, (i - 1) % groups) for i in range(groups)]
+    half = gate_own.shape[1] // 2
+    gate_below = lax.ppermute(gate_own, "req", upward_ring)
+    down_below = lax.ppermute(down_own, "req", upward_ring)
+    gate_above = lax.ppermute(gate_own, "req", downward_ring)
+    down_above = lax.ppermute(down_own, "req", downward_ring)
+    gate_far_low = lax.ppermute(gate_below[:, :half], "req", upward_ring)
+    down_far_low = lax.ppermute(down_below[:half], "req", upward_ring)
+    gate_far_high = lax.ppermute(gate_above[:, half:], "req", downward_ring)
+    down_far_high = lax.ppermute(down_above[half:], "req", downward_ring)
+    weight_sets = (
+        (gate_own, down_own),
+        (gate_below, down_below),
+        (gate_above, down_above),
+        (gate_far_low, down_far_low),
+        (gate_far_high, down_far_high),
+    )
     moved = moved.reshape(token_rows, sum(widths))
     resid = moved[:, : widths[0]]
     rows_of_queries = moved[:, widths[0] :]
@@ -120,13 +133,11 @@
     arrived = lax.all_to_all(outgoing, "head", split_axis=0, concat_axis=0, tiled=True)
     expert_rows = arrived.reshape(-1, model_width)
     out_rows = None
-    for shift in range(groups):
-        gate_value = jnp.dot(
-            expert_rows, gate_parts[shift][0].T, preferred_element_type=jnp.float32
-        )
-        upward = jnp.dot(expert_rows, gate_parts[shift][1].T, preferred_element_type=jnp.float32)
+    for gate_weights, down_weights in weight_sets:
+        gate_value = jnp.dot(expert_rows, gate_weights[0].T, preferred_element_type=jnp.float32)
+        upward = jnp.dot(expert_rows, gate_weights[1].T, preferred_element_type=jnp.float32)
         hidden_part = silu_mul(gate_value, upward).astype(jnp.bfloat16)
-        product = jnp.dot(hidden_part, down_parts[shift], preferred_element_type=jnp.float32)
+        product = jnp.dot(hidden_part, down_weights, preferred_element_type=jnp.float32)
         out_rows = product if out_rows is None else out_rows + product
     returned = lax.all_to_all(
         out_rows.astype(jnp.bfloat16).reshape(columns, local_experts * SLOT, model_width),

time: 344 us -> 264 us (0.77)
  waiting for transfers between devices: 216 us -> 116 us
  blocking collectives: 9.73 us -> 19.3 us
  local copies, waits for them, and re-layouts: 5.02 us -> 11.2 us
  matrix products: 55.7 us -> 60.6 us
    ppermute x6 -> x8, waiting for transfers between devices: 135 us -> 65.3 us  [the longest x1 30 us: layer(): down_below = lax.ppermute(down_own, 'req', upward_ring)]
    all_to_all x1, waiting for transfers between devices: 22.3 us -> 0.01 us  [layer(): lax.all_to_all(outgoing, 'head', split_axis=0, concat_axis=0, tiled=True)]
    all_to_all x0 -> x1, blocking collectives: none -> 9.58 us  [layer(): lax.all_to_all(by_dest(packed), 'req', split_axis=0, concat_axis=0, tiled...]
    slice x1 -> x5, local copies, waits for them, and re-layouts: 0.22 us -> 6.32 us  [the longest x1 2.68 us: layer(): gate_far_high = lax.ppermute(gate_above[:, half:], 'req', downward_ring)]
    all_gather x1, waiting for transfers between devices: 34.7 us -> 29.6 us  [layer(): kv_piece = lax.all_gather(key_value_rows, 'head', axis=0, tiled=True)]
    dot_general x8 -> x10, matrix products: 40.8 us -> 45.7 us  [the longest x5 33.4 us: layer(): jnp.dot(hidden_part, down_weights, preferred_element_type=jnp.float32)]
    all_to_all x1 -> x0, starting transfers between devices: 3.47 us -> none  [layer(): lax.all_to_all(by_dest(packed), 'req', split_axis=0, concat_axis=0, tiled...]
    ppermute x6 -> x8, starting transfers between devices: 7.3 us -> 8.88 us  [the longest x1 3.31 us: layer(): down_far_high = lax.ppermute(down_above[half:], 'req', downward_ring)]
  transfers between devices with their start and end apart: 10 -> 11, of which waited for: 8 -> 7; matrix products, arithmetic and copies ran while one was open for 13% -> 23% of each run, Pallas kernels for 0% -> 4%
where the time goes in v9:
time: 264 us
  waiting for transfers between devices  116 us (44%)
  matrix products  60.6 us (23%)
  starting transfers between devices  25.5 us (10%)
  blocking collectives  19.3 us (7%)
  between operations  13.6 us (5%)
  local copies, waits for them, and re-layouts  11.2 us (4%)
  Pallas kernels  11.2 us (4%)
  other arithmetic  6.28 us (2%)
    dot_general x5, matrix products, layer(): jnp.dot(hidden_part, down_weights, preferred_element_type=jnp.float32)  33.4 us
    ppermute x1, waiting for transfers between devices, layer(): down_below = lax.ppermute(down_own, 'req', upward_ring)  30 us
    all_gather x1, waiting for transfers between devices, layer(): kv_piece = lax.all_gather(key_value_rows, 'head', axis=0, tiled=True)  29.6 us
    ppermute x1, waiting for transfers between devices, layer(): gate_far_low = lax.ppermute(gate_below[:, :half], 'req', upward_ring)  21.5 us
    all_to_all x1, waiting for transfers between devices, layer(): lax.all_to_all(out_rows.astype(jnp.bfloat16).reshape(columns, local_exper...  21.1 us
    ppermute x1, waiting for transfers between devices, layer(): down_far_low = lax.ppermute(down_below[:half], 'req', upward_ring)  11.5 us
    all_to_all x1, starting transfers between devices, layer(): lax.all_to_all(out_rows.astype(jnp.bfloat16).reshape(columns, local_exper...  11.3 us
    pallas_call x1, Pallas kernels, attention(): pl.pallas_call(functools.partial(attn_kernel, heads=16, kv_heads=4, size=...  11.2 us
  transfers between devices with their start and end apart: 11, of which 7 were waited for; matrix products, arithmetic and copies ran while one was open for 23% of the time, Pallas kernels for 4%

profile of v9, /device:TPU:1, one launch (start us, length us, event | category | flops | bytes accessed | tf_op | source)
XLA Modules:
  0.0 263.6 jit_solution(1742033959739358531)
XLA Ops:
  8.1 9.7 %all_to_all.20 = bf16[4,16,1024]{2,1,0:T(8,128)(2,1)} all-to-all(bf16[4,16,1024]{2,1,0:T(8,128)(2,1)S(1)} %broadcast_select_fusion.1), channel_id=1, replica_groups=mesh['req'=4,'head'=32] {'req'}, dimensions={0} | all-to-all | bytes 262144 | tf_op jit(solution)/shard_map/all_to_all | solution.py:76
  19.7 9.6 %all_to_all.21 = bf16[4,16,4096]{2,1,0:T(8,128)(2,1)S(1)} all-to-all(bf16[4,16,4096]{2,1,0:T(8,128)(2,1)S(1)} %broadcast_select_fusion), channel_id=1, replica_groups=mesh['req'=4,'head'=32] {'req'}, dimensions={0} | all-to-all | bytes 1048576 | tf_op jit(solution)/shard_map/all_to_all | solution.py:81
  33.6 2.5 collective-permute-start.2
  36.8 29.6 %all-gather.2.cloned.1.call-done.kv_ref = bf16[2048,1024]{1,0:T(8,128)(2,1)} async-done(((bf16[64,1024]{1,0:T(8,128)(2,1)}), bf16[2048,1024]{1,0:T(8,128)(2,1)}) %all-gather.2.cloned.1.call-update) | async-done | bytes 4194320 | tf_op jit(solution)/shard_map/all_gather | solution.py:78
  67.0 11.2 %shard_map.118 = f32[64,2048]{1,0:T(8,128)} custom-call(bf16[64,2048]{1,0:T(8,128)(2,1)} %slice.85.q_ref, bf16[2048,1024]{1,0:T(8,128)(2,1)} %all-gather.2.cloned.1.call-done.kv_ref, s32[64,1]{1,0:T(8,128)} %copy.33.segq_ref, s32[1,2048]{1,0:T(1,128)} %bitcast.145, s32[64,1]{1,0:T(8,128)} %iota_add_fusion.posq_ref, s32[1,2048]{1,0:T(1,128)} %iota.38.posk_ref), custom_call_target="tpu_custom_call" | custom-call | tf_op jit(solution)/shard_map/pallas_call | solution.py:42
  78.2 1.2 multiply_reduce_fusion.1
  79.4 1.2 multiply_convert_fusion.2
  80.6 2.1 convolution_convert_fusion
  82.7 5.3 %all-to-all-start.2 = ((bf16[32,16,2048]{2,1,0:T(8,128)(2,1)}), bf16[32,16,2048]{2,1,0:T(8,128)(2,1)S(1)}, u32[]{:S(2)}, u32[]{:S(2)}) async-start(bf16[32,16,2048]{2,1,0:T(8,128)(2,1)} %bitcast.136), calls=%async_computation.2 | async-start | bytes 4194304 | tf_op jit(solution)/shard_map/all_to_all | solution.py:133
  88.0 1.3 collective-permute-start.1
  89.3 1.5 collective-permute-start.3
  91.5 1.5 slice.93
  93.1 30.0 %collective-permute-done.1 = bf16[352,2048]{1,0:T(8,128)(2,1)S(1)} collective-permute-done((bf16[352,2048]{1,0:T(8,128)(2,1)}, bf16[352,2048]{1,0:T(8,128)(2,1)S(1)}, u32[]{:S(2)}, u32[]{:S(2)}) %collective-permute-start.1) | collective-permute-done | bytes 1441824 | tf_op jit(solution)/shard_map/ppermute | solution.py:89
  124.1 1.5 collective-permute-done.3
  126.6 3.3 %collective-permute-start.7 = (bf16[176,2048]{1,0:T(8,128)(2,1)}, bf16[176,2048]{1,0:T(8,128)(2,1)}, u32[]{:S(2)}, u32[]{:S(2)}) collective-permute-start(bf16[176,2048]{1,0:T(8,128)(2,1)} %slice.100), channel_id=1, source_target_pairs={{0,96},{32,0},{64,32},{96,64},{1,97},{33,1},{65,33},{97,65},{2,98}... | collective-permute-start | bytes 2162696 | tf_op jit(solution)/shard_map/ppermute | solution.py:95
  129.9 2.7 %slice.97 = bf16[2,176,2048]{2,1,0:T(8,128)(2,1)} slice(bf16[2,352,2048]{2,1,0:T(8,128)(2,1)} %collective-permute-done.2), slice={[0:2], [176:352], [0:2048]} | slice | bytes 2883584 | tf_op jit(solution)/shard_map/slice | solution.py:94
  132.6 21.5 %collective-permute-done.4 = bf16[2,176,2048]{2,1,0:T(8,128)(2,1)} collective-permute-done((bf16[2,176,2048]{2,1,0:T(8,128)(2,1)S(1)}, bf16[2,176,2048]{2,1,0:T(8,128)(2,1)}, u32[]{:S(2)}, u32[]{:S(2)}) %collective-permute-start.4) | collective-permute-done | bytes 1441824 | tf_op jit(solution)/shard_map/ppermute | solution.py:92
  154.1 2.1 fusion.28
  156.2 1.9 fusion.10
  158.1 11.5 %collective-permute-done.5 = bf16[176,2048]{1,0:T(8,128)(2,1)} collective-permute-done((bf16[176,2048]{1,0:T(8,128)(2,1)}, bf16[176,2048]{1,0:T(8,128)(2,1)}, u32[]{:S(2)}, u32[]{:S(2)}) %collective-permute-start.5) | collective-permute-done | bytes 720928 | tf_op jit(solution)/shard_map/ppermute | solution.py:93
  169.5 4.9 %fusion.43 = f32[512,2048]{1,0:T(8,128)} fusion(bf16[176,2048]{1,0:T(8,128)(2,1)} %collective-permute-done.5, f32[512,176]{0,1:T(8,128)S(1)} %fusion.28, bf16[512,2048]{1,0:T(8,128)(2,1)S(1)} %bitcast.128, bf16[2,176,2048]{2,1,0:T(8,128)(2,1)} %collective-permute-done.4), kind=kOutput, calls=%fused_computation.63 | convolution fusion | flops 738648064 | bytes 8093696 | tf_op jit(solution)/shard_map/dot_general | solution.py:140
  174.5 3.2 %fusion.4 = f32[512,352]{0,1:T(8,128)} fusion(bf16[512,2048]{1,0:T(8,128)(2,1)S(1)} %bitcast.129, bf16[2,352,2048]{2,1,0:T(8,128)(2,1)} %collective-permute-done.2), kind=kOutput, calls=%fused_computation.11 | convolution fusion | flops 738197504 | bytes 4259840 | tf_op jit(solution)/shard_map/dot_general | solution.py:138
  177.6 3.2 %fusion.6 = f32[512,352]{0,1:T(8,128)} fusion(bf16[512,2048]{1,0:T(8,128)(2,1)S(1)} %bitcast.130, bf16[2,352,2048]{2,1,0:T(8,128)(2,1)} %collective-permute-done), kind=kOutput, calls=%fused_computation.15 | convolution fusion | flops 738197504 | bytes 4259840 | tf_op jit(solution)/shard_map/dot_general | solution.py:138
  180.8 6.2 %fusion.21 = f32[512,2048]{1,0:T(8,128)} fusion(bf16[352,2048]{1,0:T(8,128)(2,1)} %bitcast.153, bf16[512,2048]{1,0:T(8,128)(2,1)S(1)} %bitcast.131, bf16[2,352,2048]{2,1,0:T(8,128)(2,1)} %bitcast.149, f32[512,352]{0,1:T(8,128)} %fusion.10), kind=kOutput, calls=%fused_computation.26 | convolution fusion | flops 1477296128 | bytes 9895936 | tf_op jit(solution)/shard_map/dot_general | solution.py:140
  187.0 6.2 %fusion.36 = f32[512,2048]{1,0:T(8,128)} fusion(bf16[352,2048]{1,0:T(8,128)(2,1)} %copy-done.4, f32[512,352]{0,1:T(8,128)} %fusion.4, bf16[512,2048]{1,0:T(8,128)(2,1)S(1)} %bitcast.132, bf16[2,352,2048]{2,1,0:T(8,128)(2,1)} %collective-permute-done.2), kind=kOutput, calls=%fused_computation.52 | convolution fusion | flops 1477296128 | bytes 9895936 | tf_op jit(solution)/shard_map/dot_general | solution.py:140
  193.2 2.0 fusion.26
  195.2 6.2 %fusion.35 = f32[512,2048]{1,0:T(8,128)} fusion(bf16[352,2048]{1,0:T(8,128)(2,1)} %copy-done.3, f32[512,352]{0,1:T(8,128)} %fusion.6, bf16[512,2048]{1,0:T(8,128)(2,1)S(1)} %bitcast.134, bf16[2,352,2048]{2,1,0:T(8,128)(2,1)} %collective-permute-done), kind=kOutput, calls=%fused_computation.51 | convolution fusion | flops 1477296128 | bytes 9895936 | tf_op jit(solution)/shard_map/dot_general | solution.py:140
  201.4 9.9 %add_convert_fusion = bf16[512,2048]{1,0:T(8,128)(2,1)} fusion(f32[512,2048]{1,0:T(8,128)} %fusion.43, f32[512,2048]{1,0:T(8,128)} %fusion.36, f32[512,2048]{1,0:T(8,128)} %fusion.21, f32[512,2048]{1,0:T(8,128)} %fusion.35, bf16[176,2048]{1,0:T(8,128)(2,1)} %collective-permute-done.7, f32[512,176]{0,1:T(8,128)S(1)} %fusion.26, ...), kind=kOutput, calls=%fused_computation.4 | convolution fusion | flops 743890944 | bytes 22773760 | tf_op jit(solution)/shard_map/dot_general | solution.py:140
  211.3 11.3 %all-to-all-start.3 = ((bf16[32,16,2048]{2,1,0:T(8,128)(2,1)}), bf16[32,16,2048]{2,1,0:T(8,128)(2,1)S(1)}, u32[]{:S(2)}, u32[]{:S(2)}) async-start(bf16[32,16,2048]{2,1,0:T(8,128)(2,1)} %bitcast.137), calls=%async_computation.3 | async-start | bytes 4194304 | tf_op jit(solution)/shard_map/all_to_all | solution.py:142
  222.6 7.3 %fusion = f32[64,2,1408]{2,0,1:T(8,128)} fusion(bf16[2048,2,1408]{2,1,0:T(2,128)(2,1)} %param.20, bf16[64,2048]{1,0:T(8,128)(2,1)S(1)} %multiply_convert_fusion.2), kind=kOutput, calls=%fused_computation.2 | convolution fusion | flops 738197504 | bytes 12517376 | tf_op jit(solution)/shard_map/td,dkf->tkf/dot_general | solution.py:128
  229.9 21.1 %all-to-all-done.3 = bf16[32,16,2048]{2,1,0:T(8,128)(2,1)S(1)} async-done(((bf16[32,16,2048]{2,1,0:T(8,128)(2,1)}), bf16[32,16,2048]{2,1,0:T(8,128)(2,1)S(1)}, u32[]{:S(2)}, u32[]{:S(2)}) %all-to-all-start.3) | async-done | bytes 2097184 | tf_op jit(solution)/shard_map/all_to_all | solution.py:142
  252.2 4.5 %fusion.3 = bf16[64,2048]{1,0:T(8,128)(2,1)} fusion(f32[64,2048]{1,0:T(8,128)S(1)} %multiply_reduce_fusion, bf16[1408,2048]{1,0:T(8,128)(2,1)} %param.21, f32[64,2,1408]{2,0,1:T(8,128)S(1)} %copy-done.5, f32[64,2048]{1,0:T(8,128)S(1)} %copy-done.2, bf16[64,4096]{1,0:T(8,128)(2,1)S(1)} %bitcast.141), kind=kOutput, calls=%fused_computation.9 | convolution fusion | flops 370204672 | bytes 8060928 | tf_op jit(solution)/shard_map/dot_general | solution.py:132
  (61 shorter events, 13.2 us)
Async XLA Ops:
  6.5 0.9 copy-start
  6.5 59.9 %all-gather.2.cloned.1.call-start = ((), (), s32[]{:S(2)}) async-start(), calls=%async_computation.4 | async-start | bytes 4325376 | tf_op jit(solution)/shard_map/all_gather | solution.py:78
  17.9 11.7 %copy-start.6 = (s32[64,6]{0,1:T(8,128)S(1)}, s32[64,6]{0,1:T(8,128)}, u32[]{:S(2)}) copy-start(s32[64,6]{0,1:T(8,128)} %param.17) | copy-start | bytes 4612
  29.2 62.3 %collective-permute-start = (bf16[2,352,2048]{2,1,0:T(8,128)(2,1)}, bf16[2,352,2048]{2,1,0:T(8,128)(2,1)}, u32[]{:S(2)}, u32[]{:S(2)}) collective-permute-start(bf16[2,352,2048]{2,1,0:T(8,128)(2,1)} %bitcast.147), channel_id=1, source_target_pairs={{0,32},{32,64},{64,96},{96,0},{1,33},{33,65},{65,97},{97,1},{2,34}... | collective-permute-start | bytes 8650760 | tf_op jit(solution)/shard_map/ppermute | solution.py:88
  33.6 96.3 %collective-permute-start.2 = (bf16[2,352,2048]{2,1,0:T(8,128)(2,1)}, bf16[2,352,2048]{2,1,0:T(8,128)(2,1)}, u32[]{:S(2)}, u32[]{:S(2)}) collective-permute-start(bf16[2,352,2048]{2,1,0:T(8,128)(2,1)} %bitcast.148), channel_id=1, source_target_pairs={{0,96},{32,0},{64,32},{96,64},{1,97},{33,1},{65,33},{97,65},{2,98}... | collective-permute-start | bytes 8650760 | tf_op jit(solution)/shard_map/ppermute | solution.py:90
  67.0 12.4 %copy-start.7 = (f32[2048]{0:T(1024)S(1)}, f32[2048]{0:T(1024)}, u32[]{:S(2)}) copy-start(f32[2048]{0:T(1024)} %param.19) | copy-start | bytes 24580
  82.7 71.4 %all-to-all-start.2 = ((bf16[32,16,2048]{2,1,0:T(8,128)(2,1)}), bf16[32,16,2048]{2,1,0:T(8,128)(2,1)S(1)}, u32[]{:S(2)}, u32[]{:S(2)}) async-start(bf16[32,16,2048]{2,1,0:T(8,128)(2,1)} %bitcast.136), calls=%async_computation.2 | async-start | bytes 4194304 | tf_op jit(solution)/shard_map/all_to_all | solution.py:133
  88.0 35.1 %collective-permute-start.1 = (bf16[352,2048]{1,0:T(8,128)(2,1)}, bf16[352,2048]{1,0:T(8,128)(2,1)S(1)}, u32[]{:S(2)}, u32[]{:S(2)}) collective-permute-start(bf16[352,2048]{1,0:T(8,128)(2,1)} %bitcast.151), channel_id=1, source_target_pairs={{0,32},{32,64},{64,96},{96,0},{1,33},{33,65},{65,97},{97,1},{2,34}... | collective-permute-start | bytes 4325384 | tf_op jit(solution)/shard_map/ppermute | solution.py:89
  89.3 36.3 %collective-permute-start.3 = (bf16[352,2048]{1,0:T(8,128)(2,1)}, bf16[352,2048]{1,0:T(8,128)(2,1)S(1)}, u32[]{:S(2)}, u32[]{:S(2)}) collective-permute-start(bf16[352,2048]{1,0:T(8,128)(2,1)} %bitcast.152), channel_id=1, source_target_pairs={{0,96},{32,0},{64,32},{96,64},{1,97},{33,1},{65,33},{97,65},{2,98}... | collective-permute-start | bytes 4325384 | tf_op jit(solution)/shard_map/ppermute | solution.py:91
  93.0 61.1 %collective-permute-start.4 = (bf16[2,176,2048]{2,1,0:T(8,128)(2,1)S(1)}, bf16[2,176,2048]{2,1,0:T(8,128)(2,1)}, u32[]{:S(2)}, u32[]{:S(2)}) collective-permute-start(bf16[2,176,2048]{2,1,0:T(8,128)(2,1)S(1)} %slice.93), channel_id=1, source_target_pairs={{0,32},{32,64},{64,96},{96,0},{1,33},{33,65},{65,97},{97,1},{2,34}... | collective-permute-start | bytes 4325384 | tf_op jit(solution)/shard_map/ppermute | solution.py:92
  123.1 9.5 %copy-start.3 = (bf16[352,2048]{1,0:T(8,128)(2,1)}, bf16[352,2048]{1,0:T(8,128)(2,1)S(1)}, u32[]{:S(2)}) copy-start(bf16[352,2048]{1,0:T(8,128)(2,1)S(1)} %collective-permute-done.1) | copy-start | bytes 4325380
  124.1 45.5 %collective-permute-start.5 = (bf16[176,2048]{1,0:T(8,128)(2,1)}, bf16[176,2048]{1,0:T(8,128)(2,1)}, u32[]{:S(2)}, u32[]{:S(2)}) collective-permute-start(bf16[176,2048]{1,0:T(8,128)(2,1)} %slice.96), channel_id=1, source_target_pairs={{0,32},{32,64},{64,96},{96,0},{1,33},{33,65},{65,97},{97,1},{2,34}... | collective-permute-start | bytes 2162696 | tf_op jit(solution)/shard_map/ppermute | solution.py:93
  125.6 7.0 %copy-start.4 = (bf16[352,2048]{1,0:T(8,128)(2,1)}, bf16[352,2048]{1,0:T(8,128)(2,1)S(1)}, u32[]{:S(2)}) copy-start(bf16[352,2048]{1,0:T(8,128)(2,1)S(1)} %collective-permute-done.3) | copy-start | bytes 4325380
  126.6 74.8 %collective-permute-start.7 = (bf16[176,2048]{1,0:T(8,128)(2,1)}, bf16[176,2048]{1,0:T(8,128)(2,1)}, u32[]{:S(2)}, u32[]{:S(2)}) collective-permute-start(bf16[176,2048]{1,0:T(8,128)(2,1)} %slice.100), channel_id=1, source_target_pairs={{0,96},{32,0},{64,32},{96,64},{1,97},{33,1},{65,33},{97,65},{2,98}... | collective-permute-start | bytes 2162696 | tf_op jit(solution)/shard_map/ppermute | solution.py:95
  132.6 60.6 %collective-permute-start.6 = (bf16[2,176,2048]{2,1,0:T(8,128)(2,1)}, bf16[2,176,2048]{2,1,0:T(8,128)(2,1)}, u32[]{:S(2)}, u32[]{:S(2)}) collective-permute-start(bf16[2,176,2048]{2,1,0:T(8,128)(2,1)} %slice.97), channel_id=1, source_target_pairs={{0,96},{32,0},{64,32},{96,64},{1,97},{33,1},{65,33},{97,65},{2,98}... | collective-permute-start | bytes 4325384 | tf_op jit(solution)/shard_map/ppermute | solution.py:94
  154.1 2.1 copy-start.8
  211.3 39.7 %all-to-all-start.3 = ((bf16[32,16,2048]{2,1,0:T(8,128)(2,1)}), bf16[32,16,2048]{2,1,0:T(8,128)(2,1)S(1)}, u32[]{:S(2)}, u32[]{:S(2)}) async-start(bf16[32,16,2048]{2,1,0:T(8,128)(2,1)} %bitcast.137), calls=%async_computation.3 | async-start | bytes 4194304 | tf_op jit(solution)/shard_map/all_to_all | solution.py:142
  222.6 28.3 %copy-start.9 = (f32[64,6]{0,1:T(8,128)S(1)}, f32[64,6]{0,1:T(8,128)}, u32[]{:S(2)}) copy-start(f32[64,6]{0,1:T(8,128)} %param.18) | copy-start | bytes 4612
  251.0 1.1 copy-start.2
  251.0 1.3 copy-start.5
  251.0 5.8 %copy-start.1 = (bf16[64,1024]{1,0:T(8,128)(2,1)S(1)}, bf16[64,1024]{1,0:T(8,128)(2,1)}, u32[]{:S(2)}) copy-start(bf16[64,1024]{1,0:T(8,128)(2,1)} %param.14) | copy-start | bytes 393220
Sparse Core Ops, SparseCore 0:
  18.0 48.3 all-gather.1

commit v10 on v9

--- a/solution.py
+++ b/solution.py
@@ -132,13 +132,16 @@
     shared_out = jnp.dot(shared_hidden, shared_down, preferred_element_type=jnp.float32)
     arrived = lax.all_to_all(outgoing, "head", split_axis=0, concat_axis=0, tiled=True)
     expert_rows = arrived.reshape(-1, model_width)
-    out_rows = None
-    for gate_weights, down_weights in weight_sets:
-        gate_value = jnp.dot(expert_rows, gate_weights[0].T, preferred_element_type=jnp.float32)
+    hidden_parts = []
+    for gate_weights, _ in weight_sets:
+        gate_value = jnp.dot(
+            expert_rows, gate_weights[0].T, preferred_element_type=jnp.float32
+        )
         upward = jnp.dot(expert_rows, gate_weights[1].T, preferred_element_type=jnp.float32)
-        hidden_part = silu_mul(gate_value, upward).astype(jnp.bfloat16)
-        product = jnp.dot(hidden_part, down_weights, preferred_element_type=jnp.float32)
-        out_rows = product if out_rows is None else out_rows + product
+        hidden_parts.append(silu_mul(gate_value, upward).astype(jnp.bfloat16))
+    hidden_all = jnp.concatenate(hidden_parts, axis=1)
+    down_all = jnp.concatenate([down_weights for _, down_weights in weight_sets], axis=0)
+    out_rows = jnp.dot(hidden_all, down_all, preferred_element_type=jnp.float32)
     returned = lax.all_to_all(
         out_rows.astype(jnp.bfloat16).reshape(columns, local_experts * SLOT, model_width),
         "head",

time: 264 us -> 255 us (0.966)
  matrix products: 60.6 us -> 47.4 us
  blocking collectives: 19.3 us -> 9.73 us
  starting transfers between devices: 25.5 us -> 33.9 us
  local copies, waits for them, and re-layouts: 11.2 us -> 14.2 us
    dot_general x5 -> x1, matrix products: 33.4 us -> 4.66 us  [layer(): out_rows = jnp.dot(hidden_all, down_all, preferred_element_type=jnp.float32)]
    dot_general x1 -> x5, matrix products: 1.85 us -> 14 us  [layer(): jnp.dot(expert_rows, gate_weights[0].T, preferred_element_type=jnp.float32)]
    all_to_all x1 -> x0, blocking collectives: 9.58 us -> none  [layer(): lax.all_to_all(by_dest(packed), 'req', split_axis=0, concat_axis=0, tiled...]
    all_to_all x0 -> x1, waiting for transfers between devices: none -> 6.74 us  [layer(): lax.all_to_all(by_dest(packed), 'req', split_axis=0, concat_axis=0, tiled...]
    ppermute x1, waiting for transfers between devices: 30 us -> 35.4 us  [layer(): down_below = lax.ppermute(down_own, 'req', upward_ring)]
    unnamed x21 -> x31, local copies, waits for them, and re-layouts: 0.42 us -> 5.27 us
    ppermute x1, waiting for transfers between devices: 21.5 us -> 17.1 us  [layer(): gate_far_low = lax.ppermute(gate_below[:, :half], 'req', upward_ring)]
    all_gather x1, waiting for transfers between devices: 29.6 us -> 25.5 us  [layer(): kv_piece = lax.all_gather(key_value_rows, 'head', axis=0, tiled=True)]
  transfers between devices with their start and end apart: 11 -> 12, of which waited for: 7 -> 7; matrix products, arithmetic and copies ran while one was open for 23% -> 16% of each run, Pallas kernels for 4% -> 4%
where the time goes in v10:
time: 255 us; the launch traced here: 254 us
  waiting for transfers between devices  117 us (46%)
  matrix products  47.4 us (19%)
  starting transfers between devices  33.9 us (13%)
  local copies, waits for them, and re-layouts  14.2 us (6%)
  between operations  13.8 us (5%)
  Pallas kernels  11.2 us (4%)
  blocking collectives  9.73 us (4%)
  other arithmetic  7.1 us (3%)
    ppermute x1, waiting for transfers between devices, layer(): down_below = lax.ppermute(down_own, 'req', upward_ring)  35.4 us
    all_gather x1, waiting for transfers between devices, layer(): kv_piece = lax.all_gather(key_value_rows, 'head', axis=0, tiled=True)  25.5 us
    all_to_all x1, waiting for transfers between devices, layer(): lax.all_to_all(out_rows.astype(jnp.bfloat16).reshape(columns, local_exper...  21 us
    ppermute x1, waiting for transfers between devices, layer(): gate_far_low = lax.ppermute(gate_below[:, :half], 'req', upward_ring)  17.1 us
    dot_general x5, matrix products, layer(): jnp.dot(expert_rows, gate_weights[0].T, preferred_element_type=jnp.float32)  14 us
    dot_general x5, matrix products, layer(): jnp.dot(expert_rows, gate_weights[1].T, preferred_element_type=jnp.float32)  13.9 us
    all_to_all x1, starting transfers between devices, layer(): lax.all_to_all(out_rows.astype(jnp.bfloat16).reshape(columns, local_exper...  13.1 us
    pallas_call x1, Pallas kernels, attention(): pl.pallas_call(functools.partial(attn_kernel, heads=16, kv_heads=4, size=...  11.2 us
  transfers between devices with their start and end apart: 12, of which 7 were waited for; matrix products, arithmetic and copies ran while one was open for 16% of the time, Pallas kernels for 4%

profile of v10, /device:TPU:1, one launch (start us, length us, event | category | flops | bytes accessed | tf_op | source)
XLA Modules:
  0.0 253.9 jit_solution(10523880224242801819)
XLA Ops:
  8.1 9.7 %all_to_all.20 = bf16[4,16,1024]{2,1,0:T(8,128)(2,1)} all-to-all(bf16[4,16,1024]{2,1,0:T(8,128)(2,1)S(1)} %broadcast_select_fusion.1), channel_id=1, replica_groups=mesh['req'=4,'head'=32] {'req'}, dimensions={0} | all-to-all | bytes 262144 | tf_op jit(solution)/shard_map/all_to_all | solution.py:76
  20.5 3.5 %all-to-all-start = ((bf16[4,16,4096]{2,1,0:T(8,128)(2,1)}), bf16[4,16,4096]{2,1,0:T(8,128)(2,1)S(1)}, u32[]{:S(2)}, u32[]{:S(2)}) async-start(bf16[4,16,4096]{2,1,0:T(8,128)(2,1)} %broadcast_select_fusion), calls=%async_computation | async-start | bytes 1048576 | tf_op jit(solution)/shard_map/all_to_all | solution.py:81
  24.3 6.7 %all-to-all-done = bf16[4,16,4096]{2,1,0:T(8,128)(2,1)S(1)} async-done(((bf16[4,16,4096]{2,1,0:T(8,128)(2,1)}), bf16[4,16,4096]{2,1,0:T(8,128)(2,1)S(1)}, u32[]{:S(2)}, u32[]{:S(2)}) %all-to-all-start) | async-done | bytes 524320 | tf_op jit(solution)/shard_map/all_to_all | solution.py:81
  35.1 2.5 collective-permute-start.1
  37.6 2.7 %collective-permute-start.5 = (bf16[352,2048]{1,0:T(8,128)(2,1)}, bf16[352,2048]{1,0:T(8,128)(2,1)S(1)}, u32[]{:S(2)}, u32[]{:S(2)}) collective-permute-start(bf16[352,2048]{1,0:T(8,128)(2,1)} %bitcast.1), channel_id=1, source_target_pairs={{0,96},{32,0},{64,32},{96,64},{1,97},{33,1},{65,33},{97,65},{2,98}... | collective-permute-start | bytes 4325384 | tf_op jit(solution)/shard_map/ppermute | solution.py:91
  41.0 25.5 %all-gather.2.cloned.1.call-done.kv_ref = bf16[2048,1024]{1,0:T(8,128)(2,1)} async-done(((bf16[64,1024]{1,0:T(8,128)(2,1)}), bf16[2048,1024]{1,0:T(8,128)(2,1)}) %all-gather.2.cloned.1.call-update) | async-done | bytes 4194320 | tf_op jit(solution)/shard_map/all_gather | solution.py:78
  67.1 11.2 %shard_map.118 = f32[64,2048]{1,0:T(8,128)} custom-call(bf16[64,2048]{1,0:T(8,128)(2,1)} %slice.85.q_ref, bf16[2048,1024]{1,0:T(8,128)(2,1)} %all-gather.2.cloned.1.call-done.kv_ref, s32[64,1]{1,0:T(8,128)} %copy.33.segq_ref, s32[1,2048]{1,0:T(1,128)} %bitcast.125, s32[64,1]{1,0:T(8,128)} %iota_add_fusion.posq_ref, s32[1,2048]{1,0:T(1,128)} %iota.38.posk_ref), custom_call_target="tpu_custom_call" | custom-call | tf_op jit(solution)/shard_map/pallas_call | solution.py:42
  81.4 2.1 convolution_convert_fusion
  83.4 5.4 %all-to-all-start.2 = ((bf16[32,16,2048]{2,1,0:T(8,128)(2,1)}), bf16[32,16,2048]{2,1,0:T(8,128)(2,1)}, u32[]{:S(2)}, u32[]{:S(2)}) async-start(bf16[32,16,2048]{2,1,0:T(8,128)(2,1)} %bitcast.16), calls=%async_computation.2 | async-start | bytes 4194304 | tf_op jit(solution)/shard_map/all_to_all | solution.py:133
  88.8 35.4 %collective-permute-done.4 = bf16[352,2048]{1,0:T(8,128)(2,1)S(1)} collective-permute-done((bf16[352,2048]{1,0:T(8,128)(2,1)}, bf16[352,2048]{1,0:T(8,128)(2,1)S(1)}, u32[]{:S(2)}, u32[]{:S(2)}) %collective-permute-start.4) | collective-permute-done | bytes 1441824 | tf_op jit(solution)/shard_map/ppermute | solution.py:89
  124.3 2.6 %slice.93 = bf16[2,176,2048]{2,1,0:T(8,128)(2,1)} slice(bf16[2,352,2048]{2,1,0:T(8,128)(2,1)} %collective-permute-done), slice={[0:2], [0:176], [0:2048]} | slice | bytes 2883584 | tf_op jit(solution)/shard_map/slice | solution.py:92
  128.5 2.9 %collective-permute-start.7 = (bf16[176,2048]{1,0:T(8,128)(2,1)S(1)}, bf16[176,2048]{1,0:T(8,128)(2,1)S(1)}, u32[]{:S(2)}, u32[]{:S(2)}) collective-permute-start(bf16[176,2048]{1,0:T(8,128)(2,1)S(1)} %slice.100), channel_id=1, source_target_pairs={{0,96},{32,0},{64,32},{96,64},{1,97},{33,1},{65,33},{97,65},{2,98}... | collective-permute-start | bytes 2162696 | tf_op jit(solution)/shard_map/ppermute | solution.py:95
  131.6 7.5 %collective-permute-done.6 = bf16[176,2048]{1,0:T(8,128)(2,1)S(1)} collective-permute-done((bf16[176,2048]{1,0:T(8,128)(2,1)S(1)}, bf16[176,2048]{1,0:T(8,128)(2,1)S(1)}, u32[]{:S(2)}, u32[]{:S(2)}) %collective-permute-start.6) | collective-permute-done | bytes 720928 | tf_op jit(solution)/shard_map/ppermute | solution.py:93
  139.2 3.4 %collective-permute-done.7 = bf16[176,2048]{1,0:T(8,128)(2,1)S(1)} collective-permute-done((bf16[176,2048]{1,0:T(8,128)(2,1)S(1)}, bf16[176,2048]{1,0:T(8,128)(2,1)S(1)}, u32[]{:S(2)}, u32[]{:S(2)}) %collective-permute-start.7) | collective-permute-done | bytes 720928 | tf_op jit(solution)/shard_map/ppermute | solution.py:95
  142.6 2.5 copy-done.5
  146.5 3.5 %collective-permute-start.3 = (bf16[2,176,2048]{2,1,0:T(8,128)(2,1)S(1)}, bf16[2,176,2048]{2,1,0:T(8,128)(2,1)S(1)}, u32[]{:S(2)}, u32[]{:S(2)}) collective-permute-start(bf16[2,176,2048]{2,1,0:T(8,128)(2,1)S(1)} %slice.96), channel_id=1, source_target_pairs={{0,96},{32,0},{64,32},{96,64},{1,97},{33,1},{65,33},{97,65},{2,98}... | collective-permute-start | bytes 4325384 | tf_op jit(solution)/shard_map/ppermute | solution.py:94
  150.0 2.9 %fusion.10 = f32[512,352]{0,1:T(8,128)S(1)} fusion(bf16[512,2048]{1,0:T(8,128)(2,1)} %bitcast.17, bf16[2,352,2048]{2,1,0:T(8,128)(2,1)} %bitcast.129), kind=kOutput, calls=%fused_computation.20 | convolution fusion | flops 738197504 | bytes 4259840 | tf_op jit(solution)/shard_map/dot_general | solution.py:137
  153.0 17.1 %collective-permute-done.2 = bf16[2,176,2048]{2,1,0:T(8,128)(2,1)} collective-permute-done((bf16[2,176,2048]{2,1,0:T(8,128)(2,1)}, bf16[2,176,2048]{2,1,0:T(8,128)(2,1)}, u32[]{:S(2)}, u32[]{:S(2)}) %collective-permute-start.2) | collective-permute-done | bytes 1441824 | tf_op jit(solution)/shard_map/ppermute | solution.py:92
  170.1 2.6 %fusion.29 = f32[512,176]{0,1:T(8,128)S(1)} fusion(bf16[512,2048]{1,0:T(8,128)(2,1)} %bitcast.17, bf16[2,176,2048]{2,1,0:T(8,128)(2,1)} %collective-permute-done.2), kind=kOutput, calls=%fused_computation.38 | convolution fusion | flops 369098752 | bytes 3178496 | tf_op jit(solution)/shard_map/dot_general | solution.py:137
  172.7 2.9 %fusion.7 = f32[512,352]{0,1:T(8,128)S(1)} fusion(bf16[512,2048]{1,0:T(8,128)(2,1)} %bitcast.17, bf16[2,352,2048]{2,1,0:T(8,128)(2,1)} %collective-permute-done), kind=kOutput, calls=%fused_computation.17 | convolution fusion | flops 738197504 | bytes 4259840 | tf_op jit(solution)/shard_map/dot_general | solution.py:137
  175.6 3.1 %fusion.5 = f32[512,352]{0,1:T(8,128)S(1)} fusion(bf16[512,2048]{1,0:T(8,128)(2,1)} %bitcast.17, bf16[2,352,2048]{2,1,0:T(8,128)(2,1)} %collective-permute-done.1), kind=kOutput, calls=%fused_computation.13 | convolution fusion | flops 738197504 | bytes 4259840 | tf_op jit(solution)/shard_map/dot_general | solution.py:137
  178.8 2.6 %fusion.20 = bf16[512,1408]{0,1:T(8,128)(2,1)S(1)} fusion(bf16[512,2048]{1,0:T(8,128)(2,1)} %bitcast.17, bf16[2,352,2048]{2,1,0:T(8,128)(2,1)S(1)} %bitcast.130, f32[512,352]{0,1:T(8,128)S(1)} %fusion.10), kind=kOutput, calls=%fused_computation.26 | convolution fusion | flops 739098624 | bytes 4620288 | tf_op jit(solution)/shard_map/dot_general | solution.py:140
  181.3 2.4 fusion.27
  183.8 3.0 %fusion.31 = bf16[512,1408]{0,1:T(8,128)(2,1)S(1)} fusion(bf16[512,1408]{0,1:T(8,128)(2,1)S(1)} %fusion.20, f32[512,352]{0,1:T(8,128)S(1)} %fusion.7, bf16[512,2048]{1,0:T(8,128)(2,1)} %bitcast.17, bf16[2,352,2048]{2,1,0:T(8,128)(2,1)} %collective-permute-done), kind=kOutput, calls=%fused_computation.47 | convolution fusion | flops 739098624 | bytes 4620288 | tf_op jit(solution)/shard_map/dot_general | solution.py:140
  186.8 3.1 %fusion.32 = bf16[512,1408]{0,1:T(8,128)(2,1)S(1)} fusion(bf16[512,1408]{0,1:T(8,128)(2,1)S(1)} %fusion.31, f32[512,352]{0,1:T(8,128)S(1)} %fusion.5, bf16[512,2048]{1,0:T(8,128)(2,1)} %bitcast.17, bf16[2,352,2048]{2,1,0:T(8,128)(2,1)} %collective-permute-done.1), kind=kOutput, calls=%fused_computation.48 | convolution fusion | flops 739098624 | bytes 4620288 | tf_op jit(solution)/shard_map/dot_general | solution.py:140
  189.9 2.7 %fusion.36 = bf16[512,1408]{0,1:T(8,128)(2,1)S(1)} fusion(bf16[512,1408]{0,1:T(8,128)(2,1)S(1)} %fusion.32, f32[512,176]{0,1:T(8,128)S(1)} %fusion.29, bf16[512,2048]{1,0:T(8,128)(2,1)} %bitcast.17, bf16[2,176,2048]{2,1,0:T(8,128)(2,1)} %collective-permute-done.2), kind=kOutput, calls=%fused_computation.56 | convolution fusion | flops 369549312 | bytes 3358720 | tf_op jit(solution)/shard_map/dot_general | solution.py:140
  192.7 2.5 fusion.37
  195.2 4.7 %convolution_convert_fusion.1 = bf16[512,2048]{1,0:T(8,128)(2,1)} fusion(bf16[512,1408]{0,1:T(8,128)(2,1)S(1)} %fusion.37, bf16[1408,2048]{1,0:T(8,128)(2,1)S(1)} %bitcast.124), kind=kOutput, calls=%fused_computation.6 | convolution fusion | flops 2953838592 | bytes 9306112 | tf_op jit(solution)/shard_map/dot_general | solution.py:144
  199.8 13.1 %all-to-all-start.3 = ((bf16[32,16,2048]{2,1,0:T(8,128)(2,1)}), bf16[32,16,2048]{2,1,0:T(8,128)(2,1)S(1)}, u32[]{:S(2)}, u32[]{:S(2)}) async-start(bf16[32,16,2048]{2,1,0:T(8,128)(2,1)} %bitcast.120), calls=%async_computation.3 | async-start | bytes 4194304 | tf_op jit(solution)/shard_map/all_to_all | solution.py:145
  213.0 7.3 %fusion = f32[64,2,1408]{2,0,1:T(8,128)} fusion(bf16[2048,2,1408]{2,1,0:T(2,128)(2,1)} %param.20, bf16[64,2048]{1,0:T(8,128)(2,1)S(1)} %copy-done.4), kind=kOutput, calls=%fused_computation.2 | convolution fusion | flops 738197504 | bytes 12517376 | tf_op jit(solution)/shard_map/td,dkf->tkf/dot_general | solution.py:128
  220.3 21.0 %all-to-all-done.3 = bf16[32,16,2048]{2,1,0:T(8,128)(2,1)S(1)} async-done(((bf16[32,16,2048]{2,1,0:T(8,128)(2,1)}), bf16[32,16,2048]{2,1,0:T(8,128)(2,1)S(1)}, u32[]{:S(2)}, u32[]{:S(2)}) %all-to-all-start.3) | async-done | bytes 2097184 | tf_op jit(solution)/shard_map/all_to_all | solution.py:145
  242.6 4.5 %fusion.3 = bf16[64,2048]{1,0:T(8,128)(2,1)} fusion(f32[64,2048]{1,0:T(8,128)S(1)} %multiply_reduce_fusion, bf16[1408,2048]{1,0:T(8,128)(2,1)} %param.21, f32[64,2,1408]{2,0,1:T(8,128)S(1)} %copy-done.6, f32[64,2048]{1,0:T(8,128)S(1)} %copy-done.2, bf16[64,4096]{1,0:T(8,128)(2,1)S(1)} %bitcast.118), kind=kOutput, calls=%fused_computation.9 | convolution fusion | flops 370204672 | bytes 8060928 | tf_op jit(solution)/shard_map/dot_general | solution.py:132
  (75 shorter events, 17.6 us)
Async XLA Ops:
  6.5 0.9 copy-start
  6.5 59.9 %all-gather.2.cloned.1.call-start = ((), (), s32[]{:S(2)}) async-start(), calls=%async_computation.4 | async-start | bytes 4325376 | tf_op jit(solution)/shard_map/all_gather | solution.py:78
  17.9 6.1 %copy-start.7 = (s32[64,6]{0,1:T(8,128)S(1)}, s32[64,6]{0,1:T(8,128)}, u32[]{:S(2)}) copy-start(s32[64,6]{0,1:T(8,128)} %param.17) | copy-start | bytes 4612
  20.5 10.6 %all-to-all-start = ((bf16[4,16,4096]{2,1,0:T(8,128)(2,1)}), bf16[4,16,4096]{2,1,0:T(8,128)(2,1)S(1)}, u32[]{:S(2)}, u32[]{:S(2)}) async-start(bf16[4,16,4096]{2,1,0:T(8,128)(2,1)} %broadcast_select_fusion), calls=%async_computation | async-start | bytes 1048576 | tf_op jit(solution)/shard_map/all_to_all | solution.py:81
  31.1 93.2 %collective-permute-start = (bf16[2,352,2048]{2,1,0:T(8,128)(2,1)}, bf16[2,352,2048]{2,1,0:T(8,128)(2,1)}, u32[]{:S(2)}, u32[]{:S(2)}) collective-permute-start(bf16[2,352,2048]{2,1,0:T(8,128)(2,1)} %bitcast.127), channel_id=1, source_target_pairs={{0,32},{32,64},{64,96},{96,0},{1,33},{33,65},{65,97},{97,1},{2,34}... | collective-permute-start | bytes 8650760 | tf_op jit(solution)/shard_map/ppermute | solution.py:88
  35.1 107.5 %collective-permute-start.1 = (bf16[2,352,2048]{2,1,0:T(8,128)(2,1)}, bf16[2,352,2048]{2,1,0:T(8,128)(2,1)}, u32[]{:S(2)}, u32[]{:S(2)}) collective-permute-start(bf16[2,352,2048]{2,1,0:T(8,128)(2,1)} %bitcast.128), channel_id=1, source_target_pairs={{0,96},{32,0},{64,32},{96,64},{1,97},{33,1},{65,33},{97,65},{2,98}... | collective-permute-start | bytes 8650760 | tf_op jit(solution)/shard_map/ppermute | solution.py:90
  37.6 86.6 %collective-permute-start.4 = (bf16[352,2048]{1,0:T(8,128)(2,1)}, bf16[352,2048]{1,0:T(8,128)(2,1)S(1)}, u32[]{:S(2)}, u32[]{:S(2)}) collective-permute-start(bf16[352,2048]{1,0:T(8,128)(2,1)} %bitcast.1), channel_id=1, source_target_pairs={{0,32},{32,64},{64,96},{96,0},{1,33},{33,65},{65,97},{97,1},{2,34}... | collective-permute-start | bytes 4325384 | tf_op jit(solution)/shard_map/ppermute | solution.py:89
  37.6 90.9 %collective-permute-start.5 = (bf16[352,2048]{1,0:T(8,128)(2,1)}, bf16[352,2048]{1,0:T(8,128)(2,1)S(1)}, u32[]{:S(2)}, u32[]{:S(2)}) collective-permute-start(bf16[352,2048]{1,0:T(8,128)(2,1)} %bitcast.1), channel_id=1, source_target_pairs={{0,96},{32,0},{64,32},{96,64},{1,97},{33,1},{65,33},{97,65},{2,98}... | collective-permute-start | bytes 4325384 | tf_op jit(solution)/shard_map/ppermute | solution.py:91
  67.1 12.4 %copy-start.8 = (f32[2048]{0:T(1024)S(1)}, f32[2048]{0:T(1024)}, u32[]{:S(2)}) copy-start(f32[2048]{0:T(1024)} %param.19) | copy-start | bytes 24580
  80.6 0.7 copy-start.3
  83.4 66.6 %all-to-all-start.2 = ((bf16[32,16,2048]{2,1,0:T(8,128)(2,1)}), bf16[32,16,2048]{2,1,0:T(8,128)(2,1)}, u32[]{:S(2)}, u32[]{:S(2)}) async-start(bf16[32,16,2048]{2,1,0:T(8,128)(2,1)} %bitcast.16), calls=%async_computation.2 | async-start | bytes 4194304 | tf_op jit(solution)/shard_map/all_to_all | solution.py:133
  124.2 14.9 %collective-permute-start.6 = (bf16[176,2048]{1,0:T(8,128)(2,1)S(1)}, bf16[176,2048]{1,0:T(8,128)(2,1)S(1)}, u32[]{:S(2)}, u32[]{:S(2)}) collective-permute-start(bf16[176,2048]{1,0:T(8,128)(2,1)S(1)} %slice.99), channel_id=1, source_target_pairs={{0,32},{32,64},{64,96},{96,0},{1,33},{33,65},{65,97},{97,1},{2,34}... | collective-permute-start | bytes 2162696 | tf_op jit(solution)/shard_map/ppermute | solution.py:93
  127.0 43.1 %collective-permute-start.2 = (bf16[2,176,2048]{2,1,0:T(8,128)(2,1)}, bf16[2,176,2048]{2,1,0:T(8,128)(2,1)}, u32[]{:S(2)}, u32[]{:S(2)}) collective-permute-start(bf16[2,176,2048]{2,1,0:T(8,128)(2,1)} %slice.93), channel_id=1, source_target_pairs={{0,32},{32,64},{64,96},{96,0},{1,33},{33,65},{65,97},{97,1},{2,34}... | collective-permute-start | bytes 4325384 | tf_op jit(solution)/shard_map/ppermute | solution.py:92
  128.5 14.0 %collective-permute-start.7 = (bf16[176,2048]{1,0:T(8,128)(2,1)S(1)}, bf16[176,2048]{1,0:T(8,128)(2,1)S(1)}, u32[]{:S(2)}, u32[]{:S(2)}) collective-permute-start(bf16[176,2048]{1,0:T(8,128)(2,1)S(1)} %slice.100), channel_id=1, source_target_pairs={{0,96},{32,0},{64,32},{96,64},{1,97},{33,1},{65,33},{97,65},{2,98}... | collective-permute-start | bytes 2162696 | tf_op jit(solution)/shard_map/ppermute | solution.py:95
  142.6 2.5 copy-start.5
  146.5 34.8 %collective-permute-start.3 = (bf16[2,176,2048]{2,1,0:T(8,128)(2,1)S(1)}, bf16[2,176,2048]{2,1,0:T(8,128)(2,1)S(1)}, u32[]{:S(2)}, u32[]{:S(2)}) collective-permute-start(bf16[2,176,2048]{2,1,0:T(8,128)(2,1)S(1)} %slice.96), channel_id=1, source_target_pairs={{0,96},{32,0},{64,32},{96,64},{1,97},{33,1},{65,33},{97,65},{2,98}... | collective-permute-start | bytes 4325384 | tf_op jit(solution)/shard_map/ppermute | solution.py:94
  175.6 3.1 %copy-start.9 = (bf16[1,2,352,2048]{3,2,1,0:T(8,128)(2,1)S(1)}, bf16[1,2,352,2048]{3,2,1,0:T(8,128)(2,1)}, u32[]{:S(2)}) copy-start(bf16[1,2,352,2048]{3,2,1,0:T(8,128)(2,1)} %param.22) | copy-start | bytes 8650756
  186.8 8.3 %slice-start = ((s8[5767168]{0:T(1024)(128)(4,1)}), s8[4194304]{0:T(1024)(128)(4,1)S(1)}, s32[]{:S(2)}) async-start(s8[5767168]{0:T(1024)(128)(4,1)} %bitcast.123), calls=%async_computation.5 | async-start | bytes 8388608
  189.9 5.2 %slice-start.1 = ((s8[5767168]{0:T(1024)(128)(4,1)}), s8[1572864]{0:T(1024)(128)(4,1)S(1)}, s32[]{:S(2)}) async-start(s8[5767168]{0:T(1024)(128)(4,1)} %bitcast.123), calls=%async_computation.6 | async-start | bytes 3145728
  199.8 13.2 %copy-start.4 = (bf16[64,2048]{1,0:T(8,128)(2,1)S(1)}, bf16[64,2048]{1,0:T(8,128)(2,1)}, u32[]{:S(2)}) copy-start(bf16[64,2048]{1,0:T(8,128)(2,1)} %copy-done.3) | copy-start | bytes 786436
  199.8 41.5 %all-to-all-start.3 = ((bf16[32,16,2048]{2,1,0:T(8,128)(2,1)}), bf16[32,16,2048]{2,1,0:T(8,128)(2,1)S(1)}, u32[]{:S(2)}, u32[]{:S(2)}) async-start(bf16[32,16,2048]{2,1,0:T(8,128)(2,1)} %bitcast.120), calls=%async_computation.3 | async-start | bytes 4194304 | tf_op jit(solution)/shard_map/all_to_all | solution.py:145
  213.0 28.3 %copy-start.10 = (f32[64,6]{0,1:T(8,128)S(1)}, f32[64,6]{0,1:T(8,128)}, u32[]{:S(2)}) copy-start(f32[64,6]{0,1:T(8,128)} %param.18) | copy-start | bytes 4612
  241.3 1.1 copy-start.2
  241.3 1.3 copy-start.6
  241.3 5.8 %copy-start.1 = (bf16[64,1024]{1,0:T(8,128)(2,1)S(1)}, bf16[64,1024]{1,0:T(8,128)(2,1)}, u32[]{:S(2)}) copy-start(bf16[64,1024]{1,0:T(8,128)(2,1)} %param.14) | copy-start | bytes 393220
Sparse Core Ops, SparseCore 0:
  18.0 48.4 all-gather.1

commit v11 on v10

--- a/solution.py
+++ b/solution.py
@@ -73,11 +73,8 @@
     def by_dest(array_in):
         return jnp.take(array_in.reshape(groups, page_rows, array_in.shape[1]), dest_order, axis=0)
 
-    moved_kv = lax.all_to_all(by_dest(keys_values), "req", split_axis=0, concat_axis=0, tiled=True)
-    key_value_rows = moved_kv.reshape(token_rows, keys_values.shape[1])
-    kv_piece = lax.all_gather(key_value_rows, "head", axis=0, tiled=True)
-    widths = (hidden_in.shape[1], queries.shape[1])
-    packed = jnp.concatenate((hidden_in, queries), axis=1)
+    widths = (hidden_in.shape[1], queries.shape[1], keys_values.shape[1])
+    packed = jnp.concatenate((hidden_in, queries, keys_values), axis=1)
     moved = lax.all_to_all(by_dest(packed), "req", split_axis=0, concat_axis=0, tiled=True)
     gate_own, down_own, moved = lax.optimization_barrier(
         (expert_gate_up[0], expert_down[0], moved)
@@ -102,7 +99,11 @@
     )
     moved = moved.reshape(token_rows, sum(widths))
     resid = moved[:, : widths[0]]
-    rows_of_queries = moved[:, widths[0] :]
+    rows_of_queries = moved[:, widths[0] : widths[0] + widths[1]]
+    key_value_rows = moved[:, widths[0] + widths[1] :]
+    kv_copies = jnp.broadcast_to(key_value_rows[None], (columns,) + key_value_rows.shape)
+    kv_piece = lax.all_to_all(kv_copies, "head", split_axis=0, concat_axis=0, tiled=True)
+    kv_piece = kv_piece.reshape(-1, key_value_rows.shape[1])
     query_start = lax.axis_index("head") * token_rows
     segment_query = lax.dynamic_slice_in_dim(request_of_row, query_start, token_rows)
     position_query = query_start + jnp.arange(token_rows, dtype=jnp.int32)

time: 255 us -> 249 us (0.976)
  between operations: 13.8 us -> 0.39 us
  blocking collectives: 9.73 us -> 14.8 us
  waiting for transfers between devices: 117 us -> 112 us
  starting transfers between devices: 33.9 us -> 38.2 us
    all_to_all x1, waiting for transfers between devices: 6.74 us -> 41.3 us  [layer(): lax.all_to_all(kv_copies, 'head', split_axis=0, concat_axis=0, tiled=True)]
    all_gather x1 -> x0, waiting for transfers between devices: 25.5 us -> none  [layer(): kv_piece = lax.all_gather(key_value_rows, 'head', axis=0, tiled=True)]
    ppermute x1, waiting for transfers between devices: 35.4 us -> 19.6 us  [layer(): down_below = lax.ppermute(down_own, 'req', upward_ring)]
    all_to_all x1, starting transfers between devices: 3.47 us -> 9.92 us  [layer(): lax.all_to_all(kv_copies, 'head', split_axis=0, concat_axis=0, tiled=True)]
    all_to_all x1, blocking collectives: 9.73 us -> 14.8 us  [layer(): lax.all_to_all(by_dest(packed), 'req', split_axis=0, concat_axis=0, tiled...]
    all_to_all x1, starting transfers between devices: 13.1 us -> 8.98 us  [layer(): lax.all_to_all(out_rows.astype(jnp.bfloat16).reshape(columns, local_exper...]
    ppermute x1, waiting for transfers between devices: 7.47 us -> 10.1 us  [layer(): down_far_low = lax.ppermute(down_below[:half], 'req', upward_ring)]
    unnamed x31 -> x27, local copies, waits for them, and re-layouts: 5.27 us -> 5.36 us
  transfers between devices with their start and end apart: 12 -> 11, of which waited for: 7 -> 6; matrix products, arithmetic and copies ran while one was open for 16% -> 16% of each run, Pallas kernels for 4% -> 5%
where the time goes in v11:
time: 249 us; the launch traced here: 248 us
  waiting for transfers between devices  112 us (45%)
  matrix products  48.1 us (19%)
  starting transfers between devices  38.2 us (15%)
  local copies, waits for them, and re-layouts  16.2 us (7%)
  blocking collectives  14.8 us (6%)
  Pallas kernels  11.2 us (4%)
  other arithmetic  6.87 us (3%)
    all_to_all x1, waiting for transfers between devices, layer(): lax.all_to_all(kv_copies, 'head', split_axis=0, concat_axis=0, tiled=True)  41.3 us
    all_to_all x1, waiting for transfers between devices, layer(): lax.all_to_all(out_rows.astype(jnp.bfloat16).reshape(columns, local_exper...  21 us
    ppermute x1, waiting for transfers between devices, layer(): down_below = lax.ppermute(down_own, 'req', upward_ring)  19.6 us
    ppermute x1, waiting for transfers between devices, layer(): gate_far_low = lax.ppermute(gate_below[:, :half], 'req', upward_ring)  16.8 us
    all_to_all x1, blocking collectives, layer(): lax.all_to_all(by_dest(packed), 'req', split_axis=0, concat_axis=0, tiled...  14.8 us
    dot_general x5, matrix products, layer(): jnp.dot(expert_rows, gate_weights[0].T, preferred_element_type=jnp.float32)  14 us
    dot_general x5, matrix products, layer(): jnp.dot(expert_rows, gate_weights[1].T, preferred_element_type=jnp.float32)  13.8 us
    pallas_call x1, Pallas kernels, attention(): pl.pallas_call(functools.partial(attn_kernel, heads=16, kv_heads=4, size=...  11.2 us
  transfers between devices with their start and end apart: 11, of which 6 were waited for; matrix products, arithmetic and copies ran while one was open for 16% of the time, Pallas kernels for 5%

profile of v11, /device:TPU:1, one launch (start us, length us, event | category | flops | bytes accessed | tf_op | source)
XLA Modules:
  0.0 248.4 jit_solution(6893322219838274836)
XLA Ops:
  2.7 14.8 %all_to_all.20 = bf16[4,16,5120]{2,1,0:T(8,128)(2,1)S(1)} all-to-all(bf16[4,16,5120]{2,1,0:T(8,128)(2,1)S(1)} %broadcast_select_fusion), channel_id=1, replica_groups=mesh['req'=4,'head'=32] {'req'}, dimensions={0} | all-to-all | bytes 1310720 | tf_op jit(solution)/shard_map/all_to_all | solution.py:78
  17.5 2.5 %broadcast_in_dim.14 = bf16[32,64,1024]{2,1,0:T(8,128)(2,1)} broadcast(bf16[64,1024]{1,0:T(8,128)(2,1)S(1)} %slice.88), dimensions={1,2} | broadcast | bytes 4325376 | tf_op jit(solution)/shard_map/broadcast_in_dim | solution.py:104
  20.0 9.9 %all-to-all-start.1 = ((bf16[32,64,1024]{2,1,0:T(8,128)(2,1)}), bf16[32,64,1024]{2,1,0:T(8,128)(2,1)}, u32[]{:S(2)}, u32[]{:S(2)}) async-start(bf16[32,64,1024]{2,1,0:T(8,128)(2,1)} %broadcast_in_dim.14), calls=%async_computation.1 | async-start | bytes 8388608 | tf_op jit(solution)/shard_map/all_to_all | solution.py:105
  35.8 2.4 collective-permute-start.1
  38.2 2.7 %collective-permute-start.5 = (bf16[352,2048]{1,0:T(8,128)(2,1)}, bf16[352,2048]{1,0:T(8,128)(2,1)S(1)}, u32[]{:S(2)}, u32[]{:S(2)}) collective-permute-start(bf16[352,2048]{1,0:T(8,128)(2,1)} %bitcast.1), channel_id=1, source_target_pairs={{0,96},{32,0},{64,32},{96,64},{1,97},{33,1},{65,33},{97,65},{2,98}... | collective-permute-start | bytes 4325384 | tf_op jit(solution)/shard_map/ppermute | solution.py:88
  40.8 41.3 %all-to-all-done.1 = bf16[32,64,1024]{2,1,0:T(8,128)(2,1)} async-done(((bf16[32,64,1024]{2,1,0:T(8,128)(2,1)}), bf16[32,64,1024]{2,1,0:T(8,128)(2,1)}, u32[]{:S(2)}, u32[]{:S(2)}) %all-to-all-start.1) | async-done | bytes 4194336 | tf_op jit(solution)/shard_map/all_to_all | solution.py:105
  82.7 11.2 %shard_map.118 = f32[64,2048]{1,0:T(8,128)} custom-call(bf16[64,2048]{1,0:T(8,128)(2,1)} %slice.87.q_ref, bf16[2048,1024]{1,0:T(8,128)(2,1)} %bitcast.7.kv_ref, s32[64,1]{1,0:T(8,128)} %copy.33.segq_ref, s32[1,2048]{1,0:T(1,128)} %bitcast.123, s32[64,1]{1,0:T(8,128)} %iota_add_fusion.posq_ref, s32[1,2048]{1,0:T(1,128)} %iota.38.posk_ref), custom_call_target="tpu_custom_call" | custom-call | tf_op jit(solution)/shard_map/pallas_call | solution.py:42
  97.0 2.8 %convolution_convert_fusion = bf16[512,2048]{1,0:T(8,128)(2,1)} fusion(pred[512,64]{0,1:T(8,128)(4,1)} %fusion.25, bf16[64,2048]{1,0:T(8,128)(2,1)S(1)} %multiply_convert_fusion.2), kind=kOutput, calls=%fused_computation.4 | convolution fusion | flops 135266304 | bytes 2392064 | tf_op jit(solution)/shard_map/dot_general | solution.py:126
  99.9 7.1 %all-to-all-start.2 = ((bf16[32,16,2048]{2,1,0:T(8,128)(2,1)}), bf16[32,16,2048]{2,1,0:T(8,128)(2,1)}, u32[]{:S(2)}, u32[]{:S(2)}) async-start(bf16[32,16,2048]{2,1,0:T(8,128)(2,1)} %bitcast.15), calls=%async_computation.2 | async-start | bytes 4194304 | tf_op jit(solution)/shard_map/all_to_all | solution.py:134
  107.0 19.6 %collective-permute-done.4 = bf16[352,2048]{1,0:T(8,128)(2,1)S(1)} collective-permute-done((bf16[352,2048]{1,0:T(8,128)(2,1)}, bf16[352,2048]{1,0:T(8,128)(2,1)S(1)}, u32[]{:S(2)}, u32[]{:S(2)}) %collective-permute-start.4) | collective-permute-done | bytes 1441824 | tf_op jit(solution)/shard_map/ppermute | solution.py:86
  126.7 2.7 %slice.96 = bf16[2,176,2048]{2,1,0:T(8,128)(2,1)} slice(bf16[2,352,2048]{2,1,0:T(8,128)(2,1)} %collective-permute-done), slice={[0:2], [0:176], [0:2048]} | slice | bytes 2883584 | tf_op jit(solution)/shard_map/slice | solution.py:89
  130.9 3.2 %collective-permute-start.7 = (bf16[176,2048]{1,0:T(8,128)(2,1)S(1)}, bf16[176,2048]{1,0:T(8,128)(2,1)S(1)}, u32[]{:S(2)}, u32[]{:S(2)}) collective-permute-start(bf16[176,2048]{1,0:T(8,128)(2,1)S(1)} %slice.103), channel_id=1, source_target_pairs={{0,96},{32,0},{64,32},{96,64},{1,97},{33,1},{65,33},{97,65},{2,98}... | collective-permute-start | bytes 2162696 | tf_op jit(solution)/shard_map/ppermute | solution.py:92
  134.5 10.1 %collective-permute-done.6 = bf16[176,2048]{1,0:T(8,128)(2,1)S(1)} collective-permute-done((bf16[176,2048]{1,0:T(8,128)(2,1)S(1)}, bf16[176,2048]{1,0:T(8,128)(2,1)S(1)}, u32[]{:S(2)}, u32[]{:S(2)}) %collective-permute-start.6) | collective-permute-done | bytes 720928 | tf_op jit(solution)/shard_map/ppermute | solution.py:90
  144.6 3.7 %collective-permute-done.7 = bf16[176,2048]{1,0:T(8,128)(2,1)S(1)} collective-permute-done((bf16[176,2048]{1,0:T(8,128)(2,1)S(1)}, bf16[176,2048]{1,0:T(8,128)(2,1)S(1)}, u32[]{:S(2)}, u32[]{:S(2)}) %collective-permute-start.7) | collective-permute-done | bytes 720928 | tf_op jit(solution)/shard_map/ppermute | solution.py:92
  148.4 2.5 copy-done.3
  152.3 3.5 %collective-permute-start.3 = (bf16[2,176,2048]{2,1,0:T(8,128)(2,1)S(1)}, bf16[2,176,2048]{2,1,0:T(8,128)(2,1)S(1)}, u32[]{:S(2)}, u32[]{:S(2)}) collective-permute-start(bf16[2,176,2048]{2,1,0:T(8,128)(2,1)S(1)} %slice.99), channel_id=1, source_target_pairs={{0,96},{32,0},{64,32},{96,64},{1,97},{33,1},{65,33},{97,65},{2,98}... | collective-permute-start | bytes 4325384 | tf_op jit(solution)/shard_map/ppermute | solution.py:91
  155.8 2.9 %fusion.10 = f32[512,352]{0,1:T(8,128)S(1)} fusion(bf16[512,2048]{1,0:T(8,128)(2,1)} %bitcast.16, bf16[2,352,2048]{2,1,0:T(8,128)(2,1)} %bitcast.127), kind=kOutput, calls=%fused_computation.19 | convolution fusion | flops 738197504 | bytes 4259840 | tf_op jit(solution)/shard_map/dot_general | solution.py:138
  158.8 16.8 %collective-permute-done.2 = bf16[2,176,2048]{2,1,0:T(8,128)(2,1)} collective-permute-done((bf16[2,176,2048]{2,1,0:T(8,128)(2,1)}, bf16[2,176,2048]{2,1,0:T(8,128)(2,1)}, u32[]{:S(2)}, u32[]{:S(2)}) %collective-permute-start.2) | collective-permute-done | bytes 1441824 | tf_op jit(solution)/shard_map/ppermute | solution.py:89
  175.6 2.6 %fusion.29 = f32[512,176]{0,1:T(8,128)S(1)} fusion(bf16[512,2048]{1,0:T(8,128)(2,1)} %bitcast.16, bf16[2,176,2048]{2,1,0:T(8,128)(2,1)} %collective-permute-done.2), kind=kOutput, calls=%fused_computation.37 | convolution fusion | flops 369098752 | bytes 3178496 | tf_op jit(solution)/shard_map/dot_general | solution.py:138
  178.2 2.9 %fusion.7 = f32[512,352]{0,1:T(8,128)S(1)} fusion(bf16[512,2048]{1,0:T(8,128)(2,1)} %bitcast.16, bf16[2,352,2048]{2,1,0:T(8,128)(2,1)} %collective-permute-done), kind=kOutput, calls=%fused_computation.16 | convolution fusion | flops 738197504 | bytes 4259840 | tf_op jit(solution)/shard_map/dot_general | solution.py:138
  181.1 3.1 %fusion.5 = f32[512,352]{0,1:T(8,128)S(1)} fusion(bf16[512,2048]{1,0:T(8,128)(2,1)} %bitcast.16, bf16[2,352,2048]{2,1,0:T(8,128)(2,1)} %collective-permute-done.1), kind=kOutput, calls=%fused_computation.12 | convolution fusion | flops 738197504 | bytes 4259840 | tf_op jit(solution)/shard_map/dot_general | solution.py:138
  184.2 2.6 %fusion.20 = bf16[512,1408]{0,1:T(8,128)(2,1)S(1)} fusion(bf16[512,2048]{1,0:T(8,128)(2,1)} %bitcast.16, bf16[2,352,2048]{2,1,0:T(8,128)(2,1)S(1)} %bitcast.128, f32[512,352]{0,1:T(8,128)S(1)} %fusion.10), kind=kOutput, calls=%fused_computation.25 | convolution fusion | flops 739098624 | bytes 4620288 | tf_op jit(solution)/shard_map/dot_general | solution.py:141
  186.8 2.4 fusion.27
  189.2 3.0 %fusion.31 = bf16[512,1408]{0,1:T(8,128)(2,1)S(1)} fusion(bf16[512,1408]{0,1:T(8,128)(2,1)S(1)} %fusion.20, f32[512,352]{0,1:T(8,128)S(1)} %fusion.7, bf16[512,2048]{1,0:T(8,128)(2,1)} %bitcast.16, bf16[2,352,2048]{2,1,0:T(8,128)(2,1)} %collective-permute-done), kind=kOutput, calls=%fused_computation.46 | convolution fusion | flops 739098624 | bytes 4620288 | tf_op jit(solution)/shard_map/dot_general | solution.py:141
  192.2 3.1 %fusion.32 = bf16[512,1408]{0,1:T(8,128)(2,1)S(1)} fusion(bf16[512,1408]{0,1:T(8,128)(2,1)S(1)} %fusion.31, f32[512,352]{0,1:T(8,128)S(1)} %fusion.5, bf16[512,2048]{1,0:T(8,128)(2,1)} %bitcast.16, bf16[2,352,2048]{2,1,0:T(8,128)(2,1)} %collective-permute-done.1), kind=kOutput, calls=%fused_computation.47 | convolution fusion | flops 739098624 | bytes 4620288 | tf_op jit(solution)/shard_map/dot_general | solution.py:141
  195.4 2.7 %fusion.36 = bf16[512,1408]{0,1:T(8,128)(2,1)S(1)} fusion(bf16[512,1408]{0,1:T(8,128)(2,1)S(1)} %fusion.32, f32[512,176]{0,1:T(8,128)S(1)} %fusion.29, bf16[512,2048]{1,0:T(8,128)(2,1)} %bitcast.16, bf16[2,176,2048]{2,1,0:T(8,128)(2,1)} %collective-permute-done.2), kind=kOutput, calls=%fused_computation.55 | convolution fusion | flops 369549312 | bytes 3358720 | tf_op jit(solution)/shard_map/dot_general | solution.py:141
  198.1 2.4 fusion.37
  200.6 4.7 %convolution_convert_fusion.1 = bf16[512,2048]{1,0:T(8,128)(2,1)} fusion(bf16[512,1408]{0,1:T(8,128)(2,1)S(1)} %fusion.37, bf16[1408,2048]{1,0:T(8,128)(2,1)S(1)} %bitcast.122), kind=kOutput, calls=%fused_computation.5 | convolution fusion | flops 2953838592 | bytes 9306112 | tf_op jit(solution)/shard_map/dot_general | solution.py:145
  205.3 9.0 %all-to-all-start.3 = ((bf16[32,16,2048]{2,1,0:T(8,128)(2,1)}), bf16[32,16,2048]{2,1,0:T(8,128)(2,1)S(1)}, u32[]{:S(2)}, u32[]{:S(2)}) async-start(bf16[32,16,2048]{2,1,0:T(8,128)(2,1)} %bitcast.120), calls=%async_computation.3 | async-start | bytes 4194304 | tf_op jit(solution)/shard_map/all_to_all | solution.py:146
  214.3 7.3 %fusion = f32[64,2,1408]{2,0,1:T(8,128)} fusion(bf16[2048,2,1408]{2,1,0:T(2,128)(2,1)} %param.20, bf16[64,2048]{1,0:T(8,128)(2,1)S(1)} %copy-done.2), kind=kOutput, calls=%fused_computation.1 | convolution fusion | flops 738197504 | bytes 12517376 | tf_op jit(solution)/shard_map/td,dkf->tkf/dot_general | solution.py:129
  221.5 21.0 %all-to-all-done.3 = bf16[32,16,2048]{2,1,0:T(8,128)(2,1)S(1)} async-done(((bf16[32,16,2048]{2,1,0:T(8,128)(2,1)}), bf16[32,16,2048]{2,1,0:T(8,128)(2,1)S(1)}, u32[]{:S(2)}, u32[]{:S(2)}) %all-to-all-start.3) | async-done | bytes 2097184 | tf_op jit(solution)/shard_map/all_to_all | solution.py:146
  243.8 4.5 %fusion.3 = bf16[64,2048]{1,0:T(8,128)(2,1)} fusion(f32[64,2048]{1,0:T(8,128)S(1)} %multiply_reduce_fusion, bf16[1408,2048]{1,0:T(8,128)(2,1)} %param.21, f32[64,2,1408]{2,0,1:T(8,128)S(1)} %copy-done.4, f32[64,2048]{1,0:T(8,128)S(1)} %copy-done, bf16[64,5120]{1,0:T(8,128)(2,1)S(1)} %bitcast.117), kind=kOutput, calls=%fused_computation.8 | convolution fusion | flops 370204672 | bytes 8060928 | tf_op jit(solution)/shard_map/dot_general | solution.py:133
  (68 shorter events, 16.9 us)
Async XLA Ops:
  20.0 9.9 %copy-start.5 = (s32[64,6]{0,1:T(8,128)S(1)}, s32[64,6]{0,1:T(8,128)}, u32[]{:S(2)}) copy-start(s32[64,6]{0,1:T(8,128)} %param.17) | copy-start | bytes 4612
  20.0 62.0 %all-to-all-start.1 = ((bf16[32,64,1024]{2,1,0:T(8,128)(2,1)}), bf16[32,64,1024]{2,1,0:T(8,128)(2,1)}, u32[]{:S(2)}, u32[]{:S(2)}) async-start(bf16[32,64,1024]{2,1,0:T(8,128)(2,1)} %broadcast_in_dim.14), calls=%async_computation.1 | async-start | bytes 8388608 | tf_op jit(solution)/shard_map/all_to_all | solution.py:105
  30.4 96.4 %collective-permute-start = (bf16[2,352,2048]{2,1,0:T(8,128)(2,1)}, bf16[2,352,2048]{2,1,0:T(8,128)(2,1)}, u32[]{:S(2)}, u32[]{:S(2)}) collective-permute-start(bf16[2,352,2048]{2,1,0:T(8,128)(2,1)} %bitcast.125), channel_id=1, source_target_pairs={{0,32},{32,64},{64,96},{96,0},{1,33},{33,65},{65,97},{97,1},{2,34}... | collective-permute-start | bytes 8650760 | tf_op jit(solution)/shard_map/ppermute | solution.py:85
  35.8 112.6 %collective-permute-start.1 = (bf16[2,352,2048]{2,1,0:T(8,128)(2,1)}, bf16[2,352,2048]{2,1,0:T(8,128)(2,1)}, u32[]{:S(2)}, u32[]{:S(2)}) collective-permute-start(bf16[2,352,2048]{2,1,0:T(8,128)(2,1)} %bitcast.126), channel_id=1, source_target_pairs={{0,96},{32,0},{64,32},{96,64},{1,97},{33,1},{65,33},{97,65},{2,98}... | collective-permute-start | bytes 8650760 | tf_op jit(solution)/shard_map/ppermute | solution.py:87
  38.1 88.4 %collective-permute-start.4 = (bf16[352,2048]{1,0:T(8,128)(2,1)}, bf16[352,2048]{1,0:T(8,128)(2,1)S(1)}, u32[]{:S(2)}, u32[]{:S(2)}) collective-permute-start(bf16[352,2048]{1,0:T(8,128)(2,1)} %bitcast.1), channel_id=1, source_target_pairs={{0,32},{32,64},{64,96},{96,0},{1,33},{33,65},{65,97},{97,1},{2,34}... | collective-permute-start | bytes 4325384 | tf_op jit(solution)/shard_map/ppermute | solution.py:86
  38.2 92.7 %collective-permute-start.5 = (bf16[352,2048]{1,0:T(8,128)(2,1)}, bf16[352,2048]{1,0:T(8,128)(2,1)S(1)}, u32[]{:S(2)}, u32[]{:S(2)}) collective-permute-start(bf16[352,2048]{1,0:T(8,128)(2,1)} %bitcast.1), channel_id=1, source_target_pairs={{0,96},{32,0},{64,32},{96,64},{1,97},{33,1},{65,33},{97,65},{2,98}... | collective-permute-start | bytes 4325384 | tf_op jit(solution)/shard_map/ppermute | solution.py:88
  82.7 12.5 %copy-start.6 = (f32[2048]{0:T(1024)S(1)}, f32[2048]{0:T(1024)}, u32[]{:S(2)}) copy-start(f32[2048]{0:T(1024)} %param.19) | copy-start | bytes 24580
  96.3 0.7 copy-start.1
  99.9 56.0 %all-to-all-start.2 = ((bf16[32,16,2048]{2,1,0:T(8,128)(2,1)}), bf16[32,16,2048]{2,1,0:T(8,128)(2,1)}, u32[]{:S(2)}, u32[]{:S(2)}) async-start(bf16[32,16,2048]{2,1,0:T(8,128)(2,1)} %bitcast.15), calls=%async_computation.2 | async-start | bytes 4194304 | tf_op jit(solution)/shard_map/all_to_all | solution.py:134
  126.6 17.9 %collective-permute-start.6 = (bf16[176,2048]{1,0:T(8,128)(2,1)S(1)}, bf16[176,2048]{1,0:T(8,128)(2,1)S(1)}, u32[]{:S(2)}, u32[]{:S(2)}) collective-permute-start(bf16[176,2048]{1,0:T(8,128)(2,1)S(1)} %slice.102), channel_id=1, source_target_pairs={{0,32},{32,64},{64,96},{96,0},{1,33},{33,65},{65,97},{97,1},{2,34}... | collective-permute-start | bytes 2162696 | tf_op jit(solution)/shard_map/ppermute | solution.py:90
  129.4 46.2 %collective-permute-start.2 = (bf16[2,176,2048]{2,1,0:T(8,128)(2,1)}, bf16[2,176,2048]{2,1,0:T(8,128)(2,1)}, u32[]{:S(2)}, u32[]{:S(2)}) collective-permute-start(bf16[2,176,2048]{2,1,0:T(8,128)(2,1)} %slice.96), channel_id=1, source_target_pairs={{0,32},{32,64},{64,96},{96,0},{1,33},{33,65},{65,97},{97,1},{2,34}... | collective-permute-start | bytes 4325384 | tf_op jit(solution)/shard_map/ppermute | solution.py:89
  130.9 17.4 %collective-permute-start.7 = (bf16[176,2048]{1,0:T(8,128)(2,1)S(1)}, bf16[176,2048]{1,0:T(8,128)(2,1)S(1)}, u32[]{:S(2)}, u32[]{:S(2)}) collective-permute-start(bf16[176,2048]{1,0:T(8,128)(2,1)S(1)} %slice.103), channel_id=1, source_target_pairs={{0,96},{32,0},{64,32},{96,64},{1,97},{33,1},{65,33},{97,65},{2,98}... | collective-permute-start | bytes 2162696 | tf_op jit(solution)/shard_map/ppermute | solution.py:92
  148.4 2.5 %copy-start.3 = (bf16[1408,2048]{1,0:T(8,128)(2,1)}, bf16[1408,2048]{1,0:T(8,128)(2,1)S(1)}, u32[]{:S(2)}) copy-start(bf16[1408,2048]{1,0:T(8,128)(2,1)S(1)} %constant_dynamic-update-slice_fusion) | copy-start | bytes 17301508
  152.3 34.5 %collective-permute-start.3 = (bf16[2,176,2048]{2,1,0:T(8,128)(2,1)S(1)}, bf16[2,176,2048]{2,1,0:T(8,128)(2,1)S(1)}, u32[]{:S(2)}, u32[]{:S(2)}) collective-permute-start(bf16[2,176,2048]{2,1,0:T(8,128)(2,1)S(1)} %slice.99), channel_id=1, source_target_pairs={{0,96},{32,0},{64,32},{96,64},{1,97},{33,1},{65,33},{97,65},{2,98}... | collective-permute-start | bytes 4325384 | tf_op jit(solution)/shard_map/ppermute | solution.py:91
  181.1 3.1 %copy-start.7 = (bf16[1,2,352,2048]{3,2,1,0:T(8,128)(2,1)S(1)}, bf16[1,2,352,2048]{3,2,1,0:T(8,128)(2,1)}, u32[]{:S(2)}) copy-start(bf16[1,2,352,2048]{3,2,1,0:T(8,128)(2,1)} %param.22) | copy-start | bytes 8650756
  192.2 8.3 %slice-start = ((s8[5767168]{0:T(1024)(128)(4,1)}), s8[4194304]{0:T(1024)(128)(4,1)S(1)}, s32[]{:S(2)}) async-start(s8[5767168]{0:T(1024)(128)(4,1)} %bitcast.121), calls=%async_computation.4 | async-start | bytes 8388608
  195.4 5.2 %slice-start.1 = ((s8[5767168]{0:T(1024)(128)(4,1)}), s8[1572864]{0:T(1024)(128)(4,1)S(1)}, s32[]{:S(2)}) async-start(s8[5767168]{0:T(1024)(128)(4,1)} %bitcast.121), calls=%async_computation.5 | async-start | bytes 3145728
  205.2 9.0 %copy-start.2 = (bf16[64,2048]{1,0:T(8,128)(2,1)S(1)}, bf16[64,2048]{1,0:T(8,128)(2,1)}, u32[]{:S(2)}) copy-start(bf16[64,2048]{1,0:T(8,128)(2,1)} %copy-done.1) | copy-start | bytes 786436
  205.3 37.3 %all-to-all-start.3 = ((bf16[32,16,2048]{2,1,0:T(8,128)(2,1)}), bf16[32,16,2048]{2,1,0:T(8,128)(2,1)S(1)}, u32[]{:S(2)}, u32[]{:S(2)}) async-start(bf16[32,16,2048]{2,1,0:T(8,128)(2,1)} %bitcast.120), calls=%async_computation.3 | async-start | bytes 4194304 | tf_op jit(solution)/shard_map/all_to_all | solution.py:146
  214.2 28.3 %copy-start.8 = (f32[64,6]{0,1:T(8,128)S(1)}, f32[64,6]{0,1:T(8,128)}, u32[]{:S(2)}) copy-start(f32[64,6]{0,1:T(8,128)} %param.18) | copy-start | bytes 4612
  242.6 1.0 copy-start
  242.6 1.3 copy-start.4

commit v12 on v11

--- a/solution.py
+++ b/solution.py
@@ -123,7 +123,9 @@
     slots_all = EXPERTS * SLOT
     placing = jnp.arange(slots_all, dtype=jnp.int32)[:, None] == slot_of[None, :]
     placing = jnp.any(placing.reshape(slots_all, token_rows, TOP), axis=2).astype(jnp.bfloat16)
-    outgoing = jnp.dot(placing, normed, preferred_element_type=jnp.float32).astype(jnp.bfloat16)
+    outgoing = jnp.dot(placing, normed, preferred_element_type=jnp.float32).astype(
+        jnp.bfloat16
+    )
     local_experts = expert_gate_up.shape[0]
     outgoing = outgoing.reshape(columns, local_experts * SLOT, model_width)
     shared_both = jnp.einsum(
@@ -134,11 +136,11 @@
     arrived = lax.all_to_all(outgoing, "head", split_axis=0, concat_axis=0, tiled=True)
     expert_rows = arrived.reshape(-1, model_width)
     hidden_parts = []
-    for gate_weights, _ in weight_sets:
-        gate_value = jnp.dot(
-            expert_rows, gate_weights[0].T, preferred_element_type=jnp.float32
-        )
-        upward = jnp.dot(expert_rows, gate_weights[1].T, preferred_element_type=jnp.float32)
+    for sets in (weight_sets[:3], weight_sets[3:]):
+        gate_matrix = jnp.concatenate([weights[0] for weights, _ in sets], axis=0)
+        up_matrix = jnp.concatenate([weights[1] for weights, _ in sets], axis=0)
+        gate_value = jnp.dot(expert_rows, gate_matrix.T, preferred_element_type=jnp.float32)
+        upward = jnp.dot(expert_rows, up_matrix.T, preferred_element_type=jnp.float32)
         hidden_parts.append(silu_mul(gate_value, upward).astype(jnp.bfloat16))
     hidden_all = jnp.concatenate(hidden_parts, axis=1)
     down_all = jnp.concatenate([down_weights for _, down_weights in weight_sets], axis=0)

time: 249 us -> 271 us (1.088)
  local copies, waits for them, and re-layouts: 16.2 us -> 36.7 us
  waiting for transfers between devices: 112 us -> 126 us
  matrix products: 48.1 us -> 34.8 us
  other arithmetic: 6.87 us -> 10 us
    ppermute x1, waiting for transfers between devices: 19.6 us -> 74.1 us  [layer(): down_below = lax.ppermute(down_own, 'req', upward_ring)]
    all_to_all x1, waiting for transfers between devices: 41.3 us -> 0.01 us  [layer(): lax.all_to_all(kv_copies, 'head', split_axis=0, concat_axis=0, tiled=True)]
    all_to_all x1, waiting for transfers between devices: 0.01 us -> 19.3 us  [layer(): lax.all_to_all(outgoing, 'head', split_axis=0, concat_axis=0, tiled=True)]
    ppermute x1, waiting for transfers between devices: 16.8 us -> 0.01 us  [layer(): gate_far_low = lax.ppermute(gate_below[:, :half], 'req', upward_ring)]
    dot_general x10 -> x4, matrix products: 27.8 us -> 14.4 us  [the longest x2 7.24 us: layer(): jnp.dot(expert_rows, up_matrix.T, preferred_element_type=jnp.float32)]
    squeeze x0 -> x5, local copies, waits for them, and re-layouts: none -> 12.7 us  [layer(): up_matrix = jnp.concatenate([weights[1] for weights, _ in sets], axis=0)]
    all_to_all x1, starting transfers between devices: 8.98 us -> 4.61 us  [layer(): lax.all_to_all(out_rows.astype(jnp.bfloat16).reshape(columns, local_exper...]
    ppermute x1, waiting for transfers between devices: 3.68 us -> 0.32 us  [layer(): down_far_high = lax.ppermute(down_above[half:], 'req', downward_ring)]
  transfers between devices with their start and end apart: 11 -> 11, of which waited for: 6 -> 5; matrix products, arithmetic and copies ran while one was open for 16% -> 18% of each run, Pallas kernels for 5% -> 4%
where the time goes in v12:
time: 271 us; the launch traced here: 269 us
  waiting for transfers between devices  126 us (46%)
  local copies, waits for them, and re-layouts  36.7 us (14%)
  starting transfers between devices  35.9 us (13%)
  matrix products  34.8 us (13%)
  blocking collectives  14.8 us (5%)
  Pallas kernels  11.2 us (4%)
  other arithmetic  10 us (4%)
    ppermute x1, waiting for transfers between devices, layer(): down_below = lax.ppermute(down_own, 'req', upward_ring)  74.1 us
    all_to_all x1, waiting for transfers between devices, layer(): lax.all_to_all(out_rows.astype(jnp.bfloat16).reshape(columns, local_exper...  21.1 us
    all_to_all x1, waiting for transfers between devices, layer(): lax.all_to_all(outgoing, 'head', split_axis=0, concat_axis=0, tiled=True)  19.3 us
    all_to_all x1, blocking collectives, layer(): lax.all_to_all(by_dest(packed), 'req', split_axis=0, concat_axis=0, tiled...  14.8 us
    squeeze x5, local copies, waits for them, and re-layouts, layer(): up_matrix = jnp.concatenate([weights[1] for weights, _ in sets], axis=0)  12.7 us
    pallas_call x1, Pallas kernels, attention(): pl.pallas_call(functools.partial(attn_kernel, heads=16, kv_heads=4, size=...  11.2 us
    ppermute x1, waiting for transfers between devices, layer(): down_far_low = lax.ppermute(down_below[:half], 'req', upward_ring)  10.7 us
    all_to_all x1, starting transfers between devices, layer(): lax.all_to_all(kv_copies, 'head', split_axis=0, concat_axis=0, tiled=True)  9.92 us
  transfers between devices with their start and end apart: 11, of which 5 were waited for; matrix products, arithmetic and copies ran while one was open for 18% of the time, Pallas kernels for 4%

profile of v12, /device:TPU:1, one launch (start us, length us, event | category | flops | bytes accessed | tf_op | source)
XLA Modules:
  0.0 269.4 jit_solution(17628155455498252677)
XLA Ops:
  2.7 14.8 %all_to_all.20 = bf16[4,16,5120]{2,1,0:T(8,128)(2,1)S(1)} all-to-all(bf16[4,16,5120]{2,1,0:T(8,128)(2,1)S(1)} %broadcast_select_fusion), channel_id=1, replica_groups=mesh['req'=4,'head'=32] {'req'}, dimensions={0} | all-to-all | bytes 1310720 | tf_op jit(solution)/shard_map/all_to_all | solution.py:78
  17.5 2.6 broadcast_in_dim.14
  20.1 9.9 %all-to-all-start.1 = ((bf16[32,64,1024]{2,1,0:T(8,128)(2,1)}), bf16[32,64,1024]{2,1,0:T(8,128)(2,1)}, u32[]{:S(2)}, u32[]{:S(2)}) async-start(bf16[32,64,1024]{2,1,0:T(8,128)(2,1)} %broadcast_in_dim.14), calls=%async_computation.1 | async-start | bytes 8388608 | tf_op jit(solution)/shard_map/all_to_all | solution.py:105
  30.4 2.4 collective-permute-start.1
  35.1 2.6 reduce-window.6
  38.7 2.7 %collective-permute-start.5 = (bf16[352,2048]{1,0:T(8,128)(2,1)}, bf16[352,2048]{1,0:T(8,128)(2,1)}, u32[]{:S(2)}, u32[]{:S(2)}) collective-permute-start(bf16[352,2048]{1,0:T(8,128)(2,1)} %bitcast.94), channel_id=1, source_target_pairs={{0,96},{32,0},{64,32},{96,64},{1,97},{33,1},{65,33},{97,65},{2,98}... | collective-permute-start | bytes 4325384 | tf_op jit(solution)/shard_map/ppermute | solution.py:88
  48.5 3.7 %slice_bitcast_fusion.4 = (bf16[352,2048]{1,0:T(8,128)(2,1)}, bf16[352,2048]{1,0:T(8,128)(2,1)}) fusion(bf16[2,352,2048]{2,1,0:T(8,128)(2,1)} %bitcast.89), kind=kLoop, calls=%fused_computation.37 | loop fusion | bytes 5767168 | tf_op jit(solution)/shard_map/squeeze | solution.py:141
  52.2 74.1 %collective-permute-done.4 = bf16[352,2048]{1,0:T(8,128)(2,1)} collective-permute-done((bf16[352,2048]{1,0:T(8,128)(2,1)}, bf16[352,2048]{1,0:T(8,128)(2,1)}, u32[]{:S(2)}, u32[]{:S(2)}) %collective-permute-start.4) | collective-permute-done | bytes 1441824 | tf_op jit(solution)/shard_map/ppermute | solution.py:86
  128.9 2.7 %collective-permute-start.7 = (bf16[176,2048]{1,0:T(8,128)(2,1)S(1)}, bf16[176,2048]{1,0:T(8,128)(2,1)S(1)}, u32[]{:S(2)}, u32[]{:S(2)}) collective-permute-start(bf16[176,2048]{1,0:T(8,128)(2,1)S(1)} %slice.103), channel_id=1, source_target_pairs={{0,96},{32,0},{64,32},{96,64},{1,97},{33,1},{65,33},{97,65},{2,98}... | collective-permute-start | bytes 2162696 | tf_op jit(solution)/shard_map/ppermute | solution.py:92
  131.6 1.5 constant_dynamic-update-slice_fusion.3
  133.0 1.5 constant_dynamic-update-slice_fusion.2
  134.5 10.7 %collective-permute-done.6 = bf16[176,2048]{1,0:T(8,128)(2,1)S(1)} collective-permute-done((bf16[176,2048]{1,0:T(8,128)(2,1)S(1)}, bf16[176,2048]{1,0:T(8,128)(2,1)S(1)}, u32[]{:S(2)}, u32[]{:S(2)}) %collective-permute-start.6) | collective-permute-done | bytes 720928 | tf_op jit(solution)/shard_map/ppermute | solution.py:90
  145.7 2.5 copy-done.10
  149.5 2.7 slice.98
  152.2 3.4 %collective-permute-start.3 = (bf16[2,176,2048]{2,1,0:T(8,128)(2,1)}, bf16[2,176,2048]{2,1,0:T(8,128)(2,1)}, u32[]{:S(2)}, u32[]{:S(2)}) collective-permute-start(bf16[2,176,2048]{2,1,0:T(8,128)(2,1)} %slice.98), channel_id=1, source_target_pairs={{0,96},{32,0},{64,32},{96,64},{1,97},{33,1},{65,33},{97,65},{2,98}... | collective-permute-start | bytes 4325384 | tf_op jit(solution)/shard_map/ppermute | solution.py:91
  156.2 11.2 %shard_map.118 = f32[64,2048]{1,0:T(8,128)} custom-call(bf16[64,2048]{1,0:T(8,128)(2,1)} %slice.87.q_ref, bf16[2048,1024]{1,0:T(8,128)(2,1)} %bitcast.7.kv_ref, s32[64,1]{1,0:T(8,128)} %copy.33.segq_ref, s32[1,2048]{1,0:T(1,128)} %bitcast.98, s32[64,1]{1,0:T(8,128)} %iota_add_fusion.posq_ref, s32[1,2048]{1,0:T(1,128)} %iota.38.posk_ref), custom_call_target="tpu_custom_call" | custom-call | tf_op jit(solution)/shard_map/pallas_call | solution.py:42
  170.5 2.9 %convolution_convert_fusion = bf16[512,2048]{1,0:T(8,128)(2,1)} fusion(pred[512,64]{0,1:T(8,128)(4,1)} %fusion.29, bf16[64,2048]{1,0:T(8,128)(2,1)S(1)} %multiply_convert_fusion.2), kind=kOutput, calls=%fused_computation.16 | convolution fusion | flops 135266304 | bytes 2392064 | tf_op jit(solution)/shard_map/dot_general | solution.py:126
  173.4 9.6 %all-to-all-start.2 = ((bf16[32,16,2048]{2,1,0:T(8,128)(2,1)}), bf16[32,16,2048]{2,1,0:T(8,128)(2,1)}, u32[]{:S(2)}, u32[]{:S(2)}) async-start(bf16[32,16,2048]{2,1,0:T(8,128)(2,1)} %bitcast.15), calls=%async_computation.2 | async-start | bytes 4194304 | tf_op jit(solution)/shard_map/all_to_all | solution.py:136
  183.0 1.8 slice_bitcast_fusion.1
  184.8 2.0 slice_bitcast_fusion
  186.8 2.6 slice_bitcast_fusion.7
  189.4 2.6 slice_bitcast_fusion.6
  192.0 19.3 %all-to-all-done.2 = bf16[32,16,2048]{2,1,0:T(8,128)(2,1)} async-done(((bf16[32,16,2048]{2,1,0:T(8,128)(2,1)}), bf16[32,16,2048]{2,1,0:T(8,128)(2,1)}, u32[]{:S(2)}, u32[]{:S(2)}) %all-to-all-start.2) | async-done | bytes 2097184 | tf_op jit(solution)/shard_map/all_to_all | solution.py:136
  211.4 3.0 %fusion.16 = f32[512,352]{0,1:T(8,128)S(1)} fusion(bf16[512,2048]{1,0:T(8,128)(2,1)} %bitcast.16, bf16[176,2048]{1,0:T(8,128)(2,1)} %get-tuple-element.20, bf16[176,2048]{1,0:T(8,128)(2,1)} %get-tuple-element.18), kind=kOutput, calls=%fused_computation.26 | convolution fusion | flops 741081088 | bytes 4259840 | tf_op jit(solution)/shard_map/dot_general | solution.py:142
  214.5 4.1 %fusion.2 = f32[512,1056]{0,1:T(8,128)S(1)} fusion(bf16[512,2048]{1,0:T(8,128)(2,1)} %bitcast.16, bf16[352,2048]{1,0:T(8,128)(2,1)S(1)} %get-tuple-element.16, bf16[352,2048]{1,0:T(8,128)(2,1)S(1)} %copy-done.5, bf16[352,2048]{1,0:T(8,128)(2,1)S(1)} %copy-done.3), kind=kOutput, calls=%fused_computation.3 | convolution fusion | flops 2227568640 | bytes 8585216 | tf_op jit(solution)/shard_map/dot_general | solution.py:142
  218.7 2.7 %multiply_convert_fusion.1 = bf16[512,352]{0,1:T(8,128)(2,1)S(1)} fusion(f32[512,352]{0,1:T(8,128)S(1)} %fusion.16, bf16[512,2048]{1,0:T(8,128)(2,1)} %bitcast.16, bf16[176,2048]{1,0:T(8,128)(2,1)S(1)} %copy-done.9, bf16[176,2048]{1,0:T(8,128)(2,1)S(1)} %copy-done.8), kind=kOutput, calls=%fused_computation.47 | convolution fusion | flops 741982208 | bytes 4620288 | tf_op jit(solution)/shard_map/dot_general | solution.py:143
  221.5 4.5 %multiply_convert_fusion = bf16[512,1056]{0,1:T(8,128)(2,1)S(1)} fusion(f32[512,1056]{0,1:T(8,128)S(1)} %fusion.2, bf16[512,2048]{1,0:T(8,128)(2,1)} %bitcast.16, bf16[352,2048]{1,0:T(8,128)(2,1)S(1)} %get-tuple-element.15, bf16[352,2048]{1,0:T(8,128)(2,1)S(1)} %copy-done.4, bf16[352,2048]{1,0:T(8,128)(2,1)S(1)} %copy-done.2), kind=kOutput, calls=%fused_computation.21 | convolution fusion | flops 2230272000 | bytes 9666560 | tf_op jit(solution)/shard_map/dot_general | solution.py:143
  226.0 4.6 %convolution_convert_fusion.1 = bf16[512,2048]{1,0:T(8,128)(2,1)} fusion(bf16[1408,2048]{1,0:T(8,128)(2,1)S(1)} %bitcast.97, bf16[512,352]{0,1:T(8,128)(2,1)S(1)} %multiply_convert_fusion.1, bf16[512,1056]{0,1:T(8,128)(2,1)S(1)} %multiply_convert_fusion), kind=kOutput, calls=%fused_computation.17 | convolution fusion | flops 2956722176 | bytes 9306112 | tf_op jit(solution)/shard_map/dot_general | solution.py:147
  230.6 4.6 %all-to-all-start.3 = ((bf16[32,16,2048]{2,1,0:T(8,128)(2,1)}), bf16[32,16,2048]{2,1,0:T(8,128)(2,1)S(1)}, u32[]{:S(2)}, u32[]{:S(2)}) async-start(bf16[32,16,2048]{2,1,0:T(8,128)(2,1)} %bitcast.92), calls=%async_computation.3 | async-start | bytes 4194304 | tf_op jit(solution)/shard_map/all_to_all | solution.py:148
  235.3 7.3 %fusion = f32[64,2,1408]{2,0,1:T(8,128)} fusion(bf16[2048,2,1408]{2,1,0:T(2,128)(2,1)} %param.20, bf16[64,2048]{1,0:T(8,128)(2,1)S(1)} %copy-done.7), kind=kOutput, calls=%fused_computation.1 | convolution fusion | flops 738197504 | bytes 12517376 | tf_op jit(solution)/shard_map/td,dkf->tkf/dot_general | solution.py:131
  242.5 21.1 %all-to-all-done.3 = bf16[32,16,2048]{2,1,0:T(8,128)(2,1)S(1)} async-done(((bf16[32,16,2048]{2,1,0:T(8,128)(2,1)}), bf16[32,16,2048]{2,1,0:T(8,128)(2,1)S(1)}, u32[]{:S(2)}, u32[]{:S(2)}) %all-to-all-start.3) | async-done | bytes 2097184 | tf_op jit(solution)/shard_map/all_to_all | solution.py:148
  264.9 4.5 %fusion.15 = bf16[64,2048]{1,0:T(8,128)(2,1)} fusion(f32[64,2048]{1,0:T(8,128)S(1)} %multiply_reduce_fusion, bf16[1408,2048]{1,0:T(8,128)(2,1)} %param.21, f32[64,2,1408]{2,0,1:T(8,128)S(1)} %copy-done.11, f32[64,2048]{1,0:T(8,128)S(1)} %copy-done, bf16[64,5120]{1,0:T(8,128)(2,1)S(1)} %bitcast.86), kind=kOutput, calls=%fused_computation.20 | convolution fusion | flops 370204672 | bytes 8060928 | tf_op jit(solution)/shard_map/dot_general | solution.py:135
  (79 shorter events, 22.6 us)
Async XLA Ops:
  20.1 12.7 %copy-start.12 = (s32[64,6]{0,1:T(8,128)S(1)}, s32[64,6]{0,1:T(8,128)}, u32[]{:S(2)}) copy-start(s32[64,6]{0,1:T(8,128)} %param.17) | copy-start | bytes 4612
  20.1 135.4 %all-to-all-start.1 = ((bf16[32,64,1024]{2,1,0:T(8,128)(2,1)}), bf16[32,64,1024]{2,1,0:T(8,128)(2,1)}, u32[]{:S(2)}, u32[]{:S(2)}) async-start(bf16[32,64,1024]{2,1,0:T(8,128)(2,1)} %broadcast_in_dim.14), calls=%async_computation.1 | async-start | bytes 8388608 | tf_op jit(solution)/shard_map/all_to_all | solution.py:105
  30.0 115.7 %collective-permute-start = (bf16[2,352,2048]{2,1,0:T(8,128)(2,1)}, bf16[2,352,2048]{2,1,0:T(8,128)(2,1)S(1)}, u32[]{:S(2)}, u32[]{:S(2)}) collective-permute-start(bf16[2,352,2048]{2,1,0:T(8,128)(2,1)} %bitcast.87), channel_id=1, source_target_pairs={{0,32},{32,64},{64,96},{96,0},{1,33},{33,65},{65,97},{97,1},{2,34}... | collective-permute-start | bytes 8650760 | tf_op jit(solution)/shard_map/ppermute | solution.py:85
  30.4 119.1 %collective-permute-start.1 = (bf16[2,352,2048]{2,1,0:T(8,128)(2,1)}, bf16[2,352,2048]{2,1,0:T(8,128)(2,1)}, u32[]{:S(2)}, u32[]{:S(2)}) collective-permute-start(bf16[2,352,2048]{2,1,0:T(8,128)(2,1)} %bitcast.88), channel_id=1, source_target_pairs={{0,96},{32,0},{64,32},{96,64},{1,97},{33,1},{65,33},{97,65},{2,98}... | collective-permute-start | bytes 8650760 | tf_op jit(solution)/shard_map/ppermute | solution.py:87
  34.4 91.9 %collective-permute-start.4 = (bf16[352,2048]{1,0:T(8,128)(2,1)}, bf16[352,2048]{1,0:T(8,128)(2,1)}, u32[]{:S(2)}, u32[]{:S(2)}) collective-permute-start(bf16[352,2048]{1,0:T(8,128)(2,1)} %bitcast.93), channel_id=1, source_target_pairs={{0,32},{32,64},{64,96},{96,0},{1,33},{33,65},{65,97},{97,1},{2,34}... | collective-permute-start | bytes 4325384 | tf_op jit(solution)/shard_map/ppermute | solution.py:86
  38.7 89.0 %collective-permute-start.5 = (bf16[352,2048]{1,0:T(8,128)(2,1)}, bf16[352,2048]{1,0:T(8,128)(2,1)}, u32[]{:S(2)}, u32[]{:S(2)}) collective-permute-start(bf16[352,2048]{1,0:T(8,128)(2,1)} %bitcast.94), channel_id=1, source_target_pairs={{0,96},{32,0},{64,32},{96,64},{1,97},{33,1},{65,33},{97,65},{2,98}... | collective-permute-start | bytes 4325384 | tf_op jit(solution)/shard_map/ppermute | solution.py:88
  52.2 75.3 %copy-start.1 = (bf16[1,352,2048]{2,1,0:T(8,128)(2,1)S(1)}, bf16[1,352,2048]{2,1,0:T(8,128)(2,1)}, u32[]{:S(2)}) copy-start(bf16[1,352,2048]{2,1,0:T(8,128)(2,1)} %param.23) | copy-start | bytes 4325380
  127.4 17.8 %collective-permute-start.6 = (bf16[176,2048]{1,0:T(8,128)(2,1)S(1)}, bf16[176,2048]{1,0:T(8,128)(2,1)S(1)}, u32[]{:S(2)}, u32[]{:S(2)}) collective-permute-start(bf16[176,2048]{1,0:T(8,128)(2,1)S(1)} %slice.102), channel_id=1, source_target_pairs={{0,32},{32,64},{64,96},{96,0},{1,33},{33,65},{65,97},{97,1},{2,34}... | collective-permute-start | bytes 2162696 | tf_op jit(solution)/shard_map/ppermute | solution.py:90
  128.9 16.8 %collective-permute-start.7 = (bf16[176,2048]{1,0:T(8,128)(2,1)S(1)}, bf16[176,2048]{1,0:T(8,128)(2,1)S(1)}, u32[]{:S(2)}, u32[]{:S(2)}) collective-permute-start(bf16[176,2048]{1,0:T(8,128)(2,1)S(1)} %slice.103), channel_id=1, source_target_pairs={{0,96},{32,0},{64,32},{96,64},{1,97},{33,1},{65,33},{97,65},{2,98}... | collective-permute-start | bytes 2162696 | tf_op jit(solution)/shard_map/ppermute | solution.py:92
  145.7 2.5 copy-start.10
  149.5 37.3 %collective-permute-start.2 = (bf16[2,176,2048]{2,1,0:T(8,128)(2,1)}, bf16[2,176,2048]{2,1,0:T(8,128)(2,1)}, u32[]{:S(2)}, u32[]{:S(2)}) collective-permute-start(bf16[2,176,2048]{2,1,0:T(8,128)(2,1)} %slice.96), channel_id=1, source_target_pairs={{0,32},{32,64},{64,96},{96,0},{1,33},{33,65},{65,97},{97,1},{2,34}... | collective-permute-start | bytes 4325384 | tf_op jit(solution)/shard_map/ppermute | solution.py:89
  152.2 37.3 %collective-permute-start.3 = (bf16[2,176,2048]{2,1,0:T(8,128)(2,1)}, bf16[2,176,2048]{2,1,0:T(8,128)(2,1)}, u32[]{:S(2)}, u32[]{:S(2)}) collective-permute-start(bf16[2,176,2048]{2,1,0:T(8,128)(2,1)} %slice.98), channel_id=1, source_target_pairs={{0,96},{32,0},{64,32},{96,64},{1,97},{33,1},{65,33},{97,65},{2,98}... | collective-permute-start | bytes 4325384 | tf_op jit(solution)/shard_map/ppermute | solution.py:91
  156.2 12.5 %copy-start.13 = (f32[2048]{0:T(1024)S(1)}, f32[2048]{0:T(1024)}, u32[]{:S(2)}) copy-start(f32[2048]{0:T(1024)} %param.19) | copy-start | bytes 24580
  169.8 0.7 copy-start.6
  173.4 38.0 %all-to-all-start.2 = ((bf16[32,16,2048]{2,1,0:T(8,128)(2,1)}), bf16[32,16,2048]{2,1,0:T(8,128)(2,1)}, u32[]{:S(2)}, u32[]{:S(2)}) async-start(bf16[32,16,2048]{2,1,0:T(8,128)(2,1)} %bitcast.15), calls=%async_computation.2 | async-start | bytes 4194304 | tf_op jit(solution)/shard_map/all_to_all | solution.py:136
  211.4 3.1 %copy-start.3 = (bf16[352,2048]{1,0:T(8,128)(2,1)S(1)}, bf16[352,2048]{1,0:T(8,128)(2,1)}, u32[]{:S(2)}) copy-start(bf16[352,2048]{1,0:T(8,128)(2,1)} %get-tuple-element.12) | copy-start | bytes 4325380
  211.4 3.1 %copy-start.5 = (bf16[352,2048]{1,0:T(8,128)(2,1)S(1)}, bf16[352,2048]{1,0:T(8,128)(2,1)}, u32[]{:S(2)}) copy-start(bf16[352,2048]{1,0:T(8,128)(2,1)} %get-tuple-element.14) | copy-start | bytes 4325380
  214.4 4.2 %copy-start.8 = (bf16[176,2048]{1,0:T(8,128)(2,1)S(1)}, bf16[176,2048]{1,0:T(8,128)(2,1)}, u32[]{:S(2)}) copy-start(bf16[176,2048]{1,0:T(8,128)(2,1)} %get-tuple-element.17) | copy-start | bytes 2162692
  214.5 4.2 %copy-start.9 = (bf16[176,2048]{1,0:T(8,128)(2,1)S(1)}, bf16[176,2048]{1,0:T(8,128)(2,1)}, u32[]{:S(2)}) copy-start(bf16[176,2048]{1,0:T(8,128)(2,1)} %get-tuple-element.19) | copy-start | bytes 2162692
  218.6 2.8 %copy-start.2 = (bf16[352,2048]{1,0:T(8,128)(2,1)S(1)}, bf16[352,2048]{1,0:T(8,128)(2,1)}, u32[]{:S(2)}) copy-start(bf16[352,2048]{1,0:T(8,128)(2,1)} %get-tuple-element.11) | copy-start | bytes 4325380
  218.6 2.8 %copy-start.4 = (bf16[352,2048]{1,0:T(8,128)(2,1)S(1)}, bf16[352,2048]{1,0:T(8,128)(2,1)}, u32[]{:S(2)}) copy-start(bf16[352,2048]{1,0:T(8,128)(2,1)} %get-tuple-element.13) | copy-start | bytes 4325380
  218.7 7.3 %slice-start = ((s8[5767168]{0:T(1024)(128)(4,1)}), s8[1572864]{0:T(1024)(128)(4,1)S(1)}, s32[]{:S(2)}) async-start(s8[5767168]{0:T(1024)(128)(4,1)} %bitcast.96), calls=%async_computation.4 | async-start | bytes 3145728
  221.4 4.5 %slice-start.1 = ((s8[5767168]{0:T(1024)(128)(4,1)}), s8[4194304]{0:T(1024)(128)(4,1)S(1)}, s32[]{:S(2)}) async-start(s8[5767168]{0:T(1024)(128)(4,1)} %bitcast.96), calls=%async_computation.5 | async-start | bytes 8388608
  230.6 4.6 %copy-start.7 = (bf16[64,2048]{1,0:T(8,128)(2,1)S(1)}, bf16[64,2048]{1,0:T(8,128)(2,1)}, u32[]{:S(2)}) copy-start(bf16[64,2048]{1,0:T(8,128)(2,1)} %copy-done.6) | copy-start | bytes 786436
  230.6 33.0 %all-to-all-start.3 = ((bf16[32,16,2048]{2,1,0:T(8,128)(2,1)}), bf16[32,16,2048]{2,1,0:T(8,128)(2,1)S(1)}, u32[]{:S(2)}, u32[]{:S(2)}) async-start(bf16[32,16,2048]{2,1,0:T(8,128)(2,1)} %bitcast.92), calls=%async_computation.3 | async-start | bytes 4194304 | tf_op jit(solution)/shard_map/all_to_all | solution.py:148
  235.3 28.4 %copy-start.14 = (f32[64,6]{0,1:T(8,128)S(1)}, f32[64,6]{0,1:T(8,128)}, u32[]{:S(2)}) copy-start(f32[64,6]{0,1:T(8,128)} %param.18) | copy-start | bytes 4612
  263.7 1.0 copy-start
  263.7 1.3 copy-start.11

commit v13 on v12

--- a/solution.py
+++ b/solution.py
@@ -82,21 +82,27 @@
     upward_ring = [(i, (i + 1) % groups) for i in range(groups)]
     downward_ring = [(i, (i - 1) % groups) for i in range(groups)]
     half = gate_own.shape[1] // 2
-    gate_below = lax.ppermute(gate_own, "req", upward_ring)
-    down_below = lax.ppermute(down_own, "req", upward_ring)
-    gate_above = lax.ppermute(gate_own, "req", downward_ring)
-    down_above = lax.ppermute(down_own, "req", downward_ring)
-    gate_far_low = lax.ppermute(gate_below[:, :half], "req", upward_ring)
-    down_far_low = lax.ppermute(down_below[:half], "req", upward_ring)
-    gate_far_high = lax.ppermute(gate_above[:, half:], "req", downward_ring)
-    down_far_high = lax.ppermute(down_above[half:], "req", downward_ring)
-    weight_sets = (
-        (gate_own, down_own),
-        (gate_below, down_below),
-        (gate_above, down_above),
-        (gate_far_low, down_far_low),
-        (gate_far_high, down_far_high),
+    halves = (
+        (gate_own[:, :half], down_own[:half]),
+        (gate_own[:, half:], down_own[half:]),
     )
+    below, above = [], []
+    for gate_half, down_half in halves:
+        below.append(
+            (
+                lax.ppermute(gate_half, "req", upward_ring),
+                lax.ppermute(down_half, "req", upward_ring),
+            )
+        )
+        above.append(
+            (
+                lax.ppermute(gate_half, "req", downward_ring),
+                lax.ppermute(down_half, "req", downward_ring),
+            )
+        )
+    far_low = tuple(lax.ppermute(w, "req", upward_ring) for w in below[0])
+    far_high = tuple(lax.ppermute(w, "req", downward_ring) for w in above[1])
+    weight_sets = ((gate_own, down_own), below[0], below[1], above[0], above[1], far_low, far_high)
     moved = moved.reshape(token_rows, sum(widths))
     resid = moved[:, : widths[0]]
     rows_of_queries = moved[:, widths[0] : widths[0] + widths[1]]
@@ -123,9 +129,7 @@
     slots_all = EXPERTS * SLOT
     placing = jnp.arange(slots_all, dtype=jnp.int32)[:, None] == slot_of[None, :]
     placing = jnp.any(placing.reshape(slots_all, token_rows, TOP), axis=2).astype(jnp.bfloat16)
-    outgoing = jnp.dot(placing, normed, preferred_element_type=jnp.float32).astype(
-        jnp.bfloat16
-    )
+    outgoing = jnp.dot(placing, normed, preferred_element_type=jnp.float32).astype(jnp.bfloat16)
     local_experts = expert_gate_up.shape[0]
     outgoing = outgoing.reshape(columns, local_experts * SLOT, model_width)
     shared_both = jnp.einsum(
@@ -136,7 +140,7 @@
     arrived = lax.all_to_all(outgoing, "head", split_axis=0, concat_axis=0, tiled=True)
     expert_rows = arrived.reshape(-1, model_width)
     hidden_parts = []
-    for sets in (weight_sets[:3], weight_sets[3:]):
+    for sets in (weight_sets[:5], weight_sets[5:]):
         gate_matrix = jnp.concatenate([weights[0] for weights, _ in sets], axis=0)
         up_matrix = jnp.concatenate([weights[1] for weights, _ in sets], axis=0)
         gate_value = jnp.dot(expert_rows, gate_matrix.T, preferred_element_type=jnp.float32)

time: 271 us -> 244 us (0.900)
  blocking collectives: 14.8 us -> 0 us
  local copies, waits for them, and re-layouts: 36.7 us -> 23.1 us
  starting transfers between devices: 35.9 us -> 44.8 us
  waiting for transfers between devices: 126 us -> 119 us
    all_to_all x1, waiting for transfers between devices: 19.3 us -> 0.01 us  [layer(): lax.all_to_all(outgoing, 'head', split_axis=0, concat_axis=0, tiled=True)]
    all_to_all x1 -> x0, blocking collectives: 14.8 us -> none  [layer(): lax.all_to_all(by_dest(packed), 'req', split_axis=0, concat_axis=0, tiled...]
    squeeze x5 -> x2, local copies, waits for them, and re-layouts: 12.7 us -> 2.84 us  [layer(): up_matrix = jnp.concatenate([weights[1] for weights, _ in sets], axis=0)]
    all_to_all x0 -> x1, waiting for transfers between devices: none -> 6.72 us  [layer(): lax.all_to_all(by_dest(packed), 'req', split_axis=0, concat_axis=0, tiled...]
    slice x5 -> x3, local copies, waits for them, and re-layouts: 7.27 us -> 2.12 us  [the longest x1 1.75 us: layer(): gate_own[:, :half]]
    ppermute x8 -> x12, waiting for transfers between devices: 85.1 us -> 90.2 us  [the longest x2 66 us: layer(): far_low = tuple((lax.ppermute(w, 'req', upward_ring) for w in below[0]))]
    all_to_all x0 -> x1, starting transfers between devices: none -> 5 us  [layer(): lax.all_to_all(by_dest(packed), 'req', split_axis=0, concat_axis=0, tiled...]
    all_to_all x1, starting transfers between devices: 4.61 us -> 8.99 us  [layer(): lax.all_to_all(out_rows.astype(jnp.bfloat16).reshape(columns, local_exper...]
  transfers between devices with their start and end apart: 11 -> 16, of which waited for: 5 -> 6; matrix products, arithmetic and copies ran while one was open for 18% -> 13% of each run, Pallas kernels for 4% -> 5%
where the time goes in v13:
time: 244 us; the launch traced here: 243 us
  waiting for transfers between devices  119 us (49%)
  starting transfers between devices  44.8 us (18%)
  matrix products  37.3 us (15%)
  local copies, waits for them, and re-layouts  23.1 us (9%)
  Pallas kernels  11.2 us (5%)
  other arithmetic  7.71 us (3%)
    ppermute x2, waiting for transfers between devices, layer(): far_low = tuple((lax.ppermute(w, 'req', upward_ring) for w in below[0]))  66 us
    ppermute x2, waiting for transfers between devices, layer(): lax.ppermute(down_half, 'req', upward_ring)  24.2 us
    all_to_all x1, waiting for transfers between devices, layer(): lax.all_to_all(out_rows.astype(jnp.bfloat16).reshape(columns, local_exper...  22 us
    pallas_call x1, Pallas kernels, attention(): pl.pallas_call(functools.partial(attn_kernel, heads=16, kv_heads=4, size=...  11.2 us
    unnamed x32, local copies, waits for them, and re-layouts  10.5 us
    all_to_all x1, starting transfers between devices, layer(): lax.all_to_all(kv_copies, 'head', split_axis=0, concat_axis=0, tiled=True)  9.93 us
    all_to_all x1, starting transfers between devices, layer(): lax.all_to_all(out_rows.astype(jnp.bfloat16).reshape(columns, local_exper...  8.99 us
    all_to_all x1, starting transfers between devices, layer(): lax.all_to_all(outgoing, 'head', split_axis=0, concat_axis=0, tiled=True)  8.79 us
  transfers between devices with their start and end apart: 16, of which 6 were waited for; matrix products, arithmetic and copies ran while one was open for 13% of the time, Pallas kernels for 5%

profile of v13, /device:TPU:1, one launch (start us, length us, event | category | flops | bytes accessed | tf_op | source)
XLA Modules:
  0.0 243.4 jit_solution(16921939391363597469)
XLA Ops:
  3.5 5.0 %all-to-all-start = ((bf16[4,16,5120]{2,1,0:T(8,128)(2,1)}), bf16[4,16,5120]{2,1,0:T(8,128)(2,1)S(1)}, u32[]{:S(2)}, u32[]{:S(2)}) async-start(bf16[4,16,5120]{2,1,0:T(8,128)(2,1)} %broadcast_select_fusion), calls=%async_computation | async-start | bytes 1310720 | tf_op jit(solution)/shard_map/all_to_all | solution.py:78
  11.8 6.7 %all-to-all-done = bf16[4,16,5120]{2,1,0:T(8,128)(2,1)S(1)} async-done(((bf16[4,16,5120]{2,1,0:T(8,128)(2,1)}), bf16[4,16,5120]{2,1,0:T(8,128)(2,1)S(1)}, u32[]{:S(2)}, u32[]{:S(2)}) %all-to-all-start) | async-done | bytes 655392 | tf_op jit(solution)/shard_map/all_to_all | solution.py:78
  18.6 2.5 %broadcast_in_dim.14 = bf16[32,64,1024]{2,1,0:T(8,128)(2,1)} broadcast(bf16[64,1024]{1,0:T(8,128)(2,1)S(1)} %slice.104), dimensions={1,2} | broadcast | bytes 4325376 | tf_op jit(solution)/shard_map/broadcast_in_dim | solution.py:110
  21.1 9.9 %all-to-all-start.1 = ((bf16[32,64,1024]{2,1,0:T(8,128)(2,1)}), bf16[32,64,1024]{2,1,0:T(8,128)(2,1)}, u32[]{:S(2)}, u32[]{:S(2)}) async-start(bf16[32,64,1024]{2,1,0:T(8,128)(2,1)} %broadcast_in_dim.14), calls=%async_computation.1 | async-start | bytes 8388608 | tf_op jit(solution)/shard_map/all_to_all | solution.py:111
  33.0 2.4 collective-permute-start.8
  35.4 2.7 %collective-permute-start.9 = (bf16[176,2048]{1,0:T(8,128)(2,1)S(1)}, bf16[176,2048]{1,0:T(8,128)(2,1)S(1)}, u32[]{:S(2)}, u32[]{:S(2)}) collective-permute-start(bf16[176,2048]{1,0:T(8,128)(2,1)S(1)} %get-tuple-element.27), channel_id=1, source_target_pairs={{0,96},{32,0},{64,32},{96,64},{1,97},{33,1},{65,33},{97,65},{2,98}... | collective-permute-start | bytes 2162696 | tf_op jit(solution)/shard_map/ppermute | solution.py:100
  38.1 2.0 bitcast_dynamic-update-slice_fusion.1
  40.1 1.8 fusion.42
  42.6 8.8 %collective-permute-done.6 = bf16[176,2048]{1,0:T(8,128)(2,1)S(1)} collective-permute-done((bf16[176,2048]{1,0:T(8,128)(2,1)S(1)}, bf16[176,2048]{1,0:T(8,128)(2,1)S(1)}, u32[]{:S(2)}, u32[]{:S(2)}) %collective-permute-start.6) | collective-permute-done | bytes 720928 | tf_op jit(solution)/shard_map/ppermute | solution.py:94
  51.5 15.4 %collective-permute-done.7 = bf16[176,2048]{1,0:T(8,128)(2,1)S(1)} collective-permute-done((bf16[176,2048]{1,0:T(8,128)(2,1)S(1)}, bf16[176,2048]{1,0:T(8,128)(2,1)S(1)}, u32[]{:S(2)}, u32[]{:S(2)}) %collective-permute-start.7) | collective-permute-done | bytes 720928 | tf_op jit(solution)/shard_map/ppermute | solution.py:94
  67.0 2.7 %collective-permute-start.11 = (bf16[176,2048]{1,0:T(8,128)(2,1)S(1)}, bf16[176,2048]{1,0:T(8,128)(2,1)S(1)}, u32[]{:S(2)}, u32[]{:S(2)}) collective-permute-start(bf16[176,2048]{1,0:T(8,128)(2,1)S(1)} %collective-permute-done.9), channel_id=1, source_target_pairs={{0,96},{32,0},{64,32},{96,64},{1,97},{33,1},{65,33},{97,65},{2,98}... | collective-permute-start | bytes 2162696 | tf_op jit(solution)/shard_map/ppermute | solution.py:104
  69.9 43.2 %collective-permute-done.10 = bf16[176,2048]{1,0:T(8,128)(2,1)S(1)} collective-permute-done((bf16[176,2048]{1,0:T(8,128)(2,1)S(1)}, bf16[176,2048]{1,0:T(8,128)(2,1)S(1)}, u32[]{:S(2)}, u32[]{:S(2)}) %collective-permute-start.10) | collective-permute-done | bytes 720928 | tf_op jit(solution)/shard_map/ppermute | solution.py:103
  113.2 1.5 collective-permute-start.4
  115.7 2.3 collective-permute-start.5
  119.9 11.2 %shard_map.118 = f32[64,2048]{1,0:T(8,128)} custom-call(bf16[64,2048]{1,0:T(8,128)(2,1)} %slice.103.q_ref, bf16[2048,1024]{1,0:T(8,128)(2,1)} %bitcast.7.kv_ref, s32[64,1]{1,0:T(8,128)} %copy.33.segq_ref, s32[1,2048]{1,0:T(1,128)} %bitcast.120, s32[64,1]{1,0:T(8,128)} %iota_add_fusion.posq_ref, s32[1,2048]{1,0:T(1,128)} %iota.38.posk_ref), custom_call_target="tpu_custom_call" | custom-call | tf_op jit(solution)/shard_map/pallas_call | solution.py:42
  134.2 2.8 %convolution_convert_fusion = bf16[512,2048]{1,0:T(8,128)(2,1)} fusion(pred[512,64]{0,1:T(8,128)(4,1)} %fusion.17, bf16[64,2048]{1,0:T(8,128)(2,1)S(1)} %multiply_convert_fusion.2), kind=kOutput, calls=%fused_computation.4 | convolution fusion | flops 135266304 | bytes 2392064 | tf_op jit(solution)/shard_map/dot_general | solution.py:132
  137.0 8.8 %all-to-all-start.2 = ((bf16[32,16,2048]{2,1,0:T(8,128)(2,1)}), bf16[32,16,2048]{2,1,0:T(8,128)(2,1)}, u32[]{:S(2)}, u32[]{:S(2)}) async-start(bf16[32,16,2048]{2,1,0:T(8,128)(2,1)} %bitcast.15), calls=%async_computation.2 | async-start | bytes 4194304 | tf_op jit(solution)/shard_map/all_to_all | solution.py:140
  145.8 2.6 %fusion.24 = (bf16[1056,2048]{1,0:T(8,128)(2,1)}, bf16[1056,2048]{1,0:T(8,128)(2,1)}) fusion(bf16[1056,2048]{1,0:T(8,128)(2,1)} %get-tuple-element.21, bf16[2,176,2048]{2,1,0:T(8,128)(2,1)} %collective-permute-done.1, bf16[1056,2048]{1,0:T(8,128)(2,1)} %get-tuple-element.22), kind=kLoop, calls=%fused_computation.44 | loop fusion | bytes 2883584
  148.4 2.6 %fusion.23 = (bf16[1056,2048]{1,0:T(8,128)(2,1)}, bf16[1056,2048]{1,0:T(8,128)(2,1)}) fusion(bf16[1056,2048]{1,0:T(8,128)(2,1)} %get-tuple-element.19, bf16[2,176,2048]{2,1,0:T(8,128)(2,1)} %collective-permute-done.2, bf16[1056,2048]{1,0:T(8,128)(2,1)} %get-tuple-element.20), kind=kLoop, calls=%fused_computation.42 | loop fusion | bytes 2883584
  152.2 22.8 %collective-permute-done.4 = bf16[2,176,2048]{2,1,0:T(8,128)(2,1)} collective-permute-done((bf16[2,176,2048]{2,1,0:T(8,128)(2,1)S(1)}, bf16[2,176,2048]{2,1,0:T(8,128)(2,1)}, u32[]{:S(2)}, u32[]{:S(2)}) %collective-permute-start.4) | collective-permute-done | bytes 1441824 | tf_op jit(solution)/shard_map/ppermute | solution.py:103
  175.0 1.4 slice_bitcast_fusion.1
  176.4 1.4 slice_bitcast_fusion
  177.9 5.3 %fusion.44 = f32[512,1056]{0,1:T(8,128)S(1)} fusion(bf16[512,2048]{1,0:T(8,128)(2,1)} %bitcast.16, bf16[1056,2048]{1,0:T(8,128)(2,1)} %get-tuple-element.15), kind=kOutput, calls=%fused_computation.92 | convolution fusion | flops 2214592512 | bytes 8585216 | tf_op jit(solution)/shard_map/dot_general | solution.py:146
  183.2 5.6 %multiply_convert_fusion = bf16[512,1056]{0,1:T(8,128)(2,1)S(1)} fusion(f32[512,1056]{0,1:T(8,128)S(1)} %fusion.44, bf16[512,2048]{1,0:T(8,128)(2,1)} %bitcast.16, bf16[1056,2048]{1,0:T(8,128)(2,1)} %get-tuple-element.16), kind=kOutput, calls=%fused_computation.9 | convolution fusion | flops 2217295872 | bytes 9666560 | tf_op jit(solution)/shard_map/dot_general | solution.py:147
  188.8 2.7 %fusion.4 = f32[512,352]{0,1:T(8,128)S(1)} fusion(bf16[512,2048]{1,0:T(8,128)(2,1)} %bitcast.16, bf16[176,2048]{1,0:T(8,128)(2,1)S(1)} %get-tuple-element.26, bf16[176,2048]{1,0:T(8,128)(2,1)S(1)} %get-tuple-element.24), kind=kOutput, calls=%fused_computation.10 | convolution fusion | flops 741081088 | bytes 4259840 | tf_op jit(solution)/shard_map/dot_general | solution.py:146
  191.5 2.7 %multiply_convert_fusion.1 = bf16[512,352]{0,1:T(8,128)(2,1)S(1)} fusion(f32[512,352]{0,1:T(8,128)S(1)} %fusion.4, bf16[512,2048]{1,0:T(8,128)(2,1)} %bitcast.16, bf16[176,2048]{1,0:T(8,128)(2,1)S(1)} %get-tuple-element.25, bf16[176,2048]{1,0:T(8,128)(2,1)S(1)} %get-tuple-element.23), kind=kOutput, calls=%fused_computation.47 | convolution fusion | flops 741982208 | bytes 4620288 | tf_op jit(solution)/shard_map/dot_general | solution.py:147
  194.2 4.6 %convolution_convert_fusion.1 = bf16[512,2048]{1,0:T(8,128)(2,1)} fusion(bf16[1408,2048]{1,0:T(8,128)(2,1)S(1)} %bitcast.119, bf16[512,352]{0,1:T(8,128)(2,1)S(1)} %multiply_convert_fusion.1, bf16[512,1056]{0,1:T(8,128)(2,1)S(1)} %multiply_convert_fusion), kind=kOutput, calls=%fused_computation.5 | convolution fusion | flops 2956722176 | bytes 9306112 | tf_op jit(solution)/shard_map/dot_general | solution.py:151
  198.8 9.0 %all-to-all-start.3 = ((bf16[32,16,2048]{2,1,0:T(8,128)(2,1)}), bf16[32,16,2048]{2,1,0:T(8,128)(2,1)}, u32[]{:S(2)}, u32[]{:S(2)}) async-start(bf16[32,16,2048]{2,1,0:T(8,128)(2,1)} %bitcast.31), calls=%async_computation.3 | async-start | bytes 4194304 | tf_op jit(solution)/shard_map/all_to_all | solution.py:152
  207.9 6.4 %fusion = f32[64,2,1408]{2,0,1:T(8,128)S(1)} fusion(bf16[2048,2,1408]{2,1,0:T(2,128)(2,1)} %param.20, bf16[64,2048]{1,0:T(8,128)(2,1)S(1)} %copy-done.4), kind=kOutput, calls=%fused_computation.1 | convolution fusion | flops 738197504 | bytes 12517376 | tf_op jit(solution)/shard_map/td,dkf->tkf/dot_general | solution.py:135
  214.3 22.0 %all-to-all-done.3 = bf16[32,16,2048]{2,1,0:T(8,128)(2,1)} async-done(((bf16[32,16,2048]{2,1,0:T(8,128)(2,1)}), bf16[32,16,2048]{2,1,0:T(8,128)(2,1)}, u32[]{:S(2)}, u32[]{:S(2)}) %all-to-all-start.3) | async-done | bytes 2097184 | tf_op jit(solution)/shard_map/all_to_all | solution.py:152
  236.2 2.7 %multiply_reduce_fusion = f32[64,2048]{1,0:T(8,128)S(1)} fusion(bf16[512,2048,1]{1,0,2:T(8,128)(2,1)} %bitcast.33, f32[64,6]{0,1:T(8,128)S(1)} %copy-done.8, s32[64,6]{0,1:T(8,128)S(1)} %multiply_add_fusion), kind=kOutput, calls=%fused_computation.3 | convolution fusion | flops 806944768 | bytes 2624512 | tf_op jit(solution)/shard_map/dot_general | solution.py:163
  238.9 4.5 %fusion.3 = bf16[64,2048]{1,0:T(8,128)(2,1)} fusion(f32[64,2048]{1,0:T(8,128)S(1)} %multiply_reduce_fusion, bf16[1408,2048]{1,0:T(8,128)(2,1)} %param.21, f32[64,2,1408]{2,0,1:T(8,128)S(1)} %fusion, f32[64,2048]{1,0:T(8,128)S(1)} %copy-done.1, bf16[64,5120]{1,0:T(8,128)(2,1)S(1)} %bitcast.116), kind=kOutput, calls=%fused_computation.8 | convolution fusion | flops 370204672 | bytes 8060928 | tf_op jit(solution)/shard_map/dot_general | solution.py:139
  (77 shorter events, 17.0 us)
Async XLA Ops:
  0.0 9.3 %copy-start.6 = (s32[64,6]{0,1:T(8,128)S(1)}, s32[64,6]{0,1:T(8,128)}, u32[]{:S(2)}) copy-start(s32[64,6]{0,1:T(8,128)} %param.17) | copy-start | bytes 4612
  3.5 15.0 %all-to-all-start = ((bf16[4,16,5120]{2,1,0:T(8,128)(2,1)}), bf16[4,16,5120]{2,1,0:T(8,128)(2,1)S(1)}, u32[]{:S(2)}, u32[]{:S(2)}) async-start(bf16[4,16,5120]{2,1,0:T(8,128)(2,1)} %broadcast_select_fusion), calls=%async_computation | async-start | bytes 1310720 | tf_op jit(solution)/shard_map/all_to_all | solution.py:78
  21.1 11.4 %copy-start.2 = (bf16[1,352,2048]{2,1,0:T(8,128)(2,1)S(1)}, bf16[1,352,2048]{2,1,0:T(8,128)(2,1)}, u32[]{:S(2)}) copy-start(bf16[1,352,2048]{2,1,0:T(8,128)(2,1)} %param.23) | copy-start | bytes 4325380
  21.1 98.1 %all-to-all-start.1 = ((bf16[32,64,1024]{2,1,0:T(8,128)(2,1)}), bf16[32,64,1024]{2,1,0:T(8,128)(2,1)}, u32[]{:S(2)}, u32[]{:S(2)}) async-start(bf16[32,64,1024]{2,1,0:T(8,128)(2,1)} %broadcast_in_dim.14), calls=%async_computation.1 | async-start | bytes 8388608 | tf_op jit(solution)/shard_map/all_to_all | solution.py:111
  31.1 7.0 %copy-start = (bf16[1,2,352,2048]{3,2,1,0:T(8,128)(2,1)S(1)}, bf16[1,2,352,2048]{3,2,1,0:T(8,128)(2,1)}, u32[]{:S(2)}) copy-start(bf16[1,2,352,2048]{3,2,1,0:T(8,128)(2,1)} %param.22) | copy-start | bytes 8650756
  32.6 18.8 %collective-permute-start.6 = (bf16[176,2048]{1,0:T(8,128)(2,1)S(1)}, bf16[176,2048]{1,0:T(8,128)(2,1)S(1)}, u32[]{:S(2)}, u32[]{:S(2)}) collective-permute-start(bf16[176,2048]{1,0:T(8,128)(2,1)S(1)} %get-tuple-element.28), channel_id=1, source_target_pairs={{0,32},{32,64},{64,96},{96,0},{1,33},{33,65},{65,97},{97,1},{2,34}... | collective-permute-start | bytes 2162696 | tf_op jit(solution)/shard_map/ppermute | solution.py:94
  33.0 33.9 %collective-permute-start.8 = (bf16[176,2048]{1,0:T(8,128)(2,1)S(1)}, bf16[176,2048]{1,0:T(8,128)(2,1)S(1)}, u32[]{:S(2)}, u32[]{:S(2)}) collective-permute-start(bf16[176,2048]{1,0:T(8,128)(2,1)S(1)} %get-tuple-element.28), channel_id=1, source_target_pairs={{0,96},{32,0},{64,32},{96,64},{1,97},{33,1},{65,33},{97,65},{2,98}... | collective-permute-start | bytes 2162696 | tf_op jit(solution)/shard_map/ppermute | solution.py:100
  35.4 31.5 %collective-permute-start.7 = (bf16[176,2048]{1,0:T(8,128)(2,1)S(1)}, bf16[176,2048]{1,0:T(8,128)(2,1)S(1)}, u32[]{:S(2)}, u32[]{:S(2)}) collective-permute-start(bf16[176,2048]{1,0:T(8,128)(2,1)S(1)} %get-tuple-element.27), channel_id=1, source_target_pairs={{0,32},{32,64},{64,96},{96,0},{1,33},{33,65},{65,97},{97,1},{2,34}... | collective-permute-start | bytes 2162696 | tf_op jit(solution)/shard_map/ppermute | solution.py:94
  35.4 31.6 %collective-permute-start.9 = (bf16[176,2048]{1,0:T(8,128)(2,1)S(1)}, bf16[176,2048]{1,0:T(8,128)(2,1)S(1)}, u32[]{:S(2)}, u32[]{:S(2)}) collective-permute-start(bf16[176,2048]{1,0:T(8,128)(2,1)S(1)} %get-tuple-element.27), channel_id=1, source_target_pairs={{0,96},{32,0},{64,32},{96,64},{1,97},{33,1},{65,33},{97,65},{2,98}... | collective-permute-start | bytes 2162696 | tf_op jit(solution)/shard_map/ppermute | solution.py:100
  42.6 70.7 %collective-permute-start = (bf16[2,176,2048]{2,1,0:T(8,128)(2,1)}, bf16[2,176,2048]{2,1,0:T(8,128)(2,1)S(1)}, u32[]{:S(2)}, u32[]{:S(2)}) collective-permute-start(bf16[2,176,2048]{2,1,0:T(8,128)(2,1)} %get-tuple-element.13), channel_id=1, source_target_pairs={{0,32},{32,64},{64,96},{96,0},{1,33},{33,65},{65,97},{97,1},{2,34}... | collective-permute-start | bytes 4325384 | tf_op jit(solution)/shard_map/ppermute | solution.py:93
  51.4 63.4 %collective-permute-start.3 = (bf16[2,176,2048]{2,1,0:T(8,128)(2,1)}, bf16[2,176,2048]{2,1,0:T(8,128)(2,1)S(1)}, u32[]{:S(2)}, u32[]{:S(2)}) collective-permute-start(bf16[2,176,2048]{2,1,0:T(8,128)(2,1)} %get-tuple-element.14), channel_id=1, source_target_pairs={{0,96},{32,0},{64,32},{96,64},{1,97},{33,1},{65,33},{97,65},{2,98}... | collective-permute-start | bytes 4325384 | tf_op jit(solution)/shard_map/ppermute | solution.py:99
  66.8 46.2 %collective-permute-start.10 = (bf16[176,2048]{1,0:T(8,128)(2,1)S(1)}, bf16[176,2048]{1,0:T(8,128)(2,1)S(1)}, u32[]{:S(2)}, u32[]{:S(2)}) collective-permute-start(bf16[176,2048]{1,0:T(8,128)(2,1)S(1)} %collective-permute-done.6), channel_id=1, source_target_pairs={{0,32},{32,64},{64,96},{96,0},{1,33},{33,65},{65,97},{97,1},{2,34}... | collective-permute-start | bytes 2162696 | tf_op jit(solution)/shard_map/ppermute | solution.py:103
  66.9 78.9 %collective-permute-start.1 = (bf16[2,176,2048]{2,1,0:T(8,128)(2,1)}, bf16[2,176,2048]{2,1,0:T(8,128)(2,1)}, u32[]{:S(2)}, u32[]{:S(2)}) collective-permute-start(bf16[2,176,2048]{2,1,0:T(8,128)(2,1)} %get-tuple-element.14), channel_id=1, source_target_pairs={{0,32},{32,64},{64,96},{96,0},{1,33},{33,65},{65,97},{97,1},{2,34}... | collective-permute-start | bytes 4325384 | tf_op jit(solution)/shard_map/ppermute | solution.py:93
  67.0 46.1 %collective-permute-start.11 = (bf16[176,2048]{1,0:T(8,128)(2,1)S(1)}, bf16[176,2048]{1,0:T(8,128)(2,1)S(1)}, u32[]{:S(2)}, u32[]{:S(2)}) collective-permute-start(bf16[176,2048]{1,0:T(8,128)(2,1)S(1)} %collective-permute-done.9), channel_id=1, source_target_pairs={{0,96},{32,0},{64,32},{96,64},{1,97},{33,1},{65,33},{97,65},{2,98}... | collective-permute-start | bytes 2162696 | tf_op jit(solution)/shard_map/ppermute | solution.py:104
  113.1 35.3 %collective-permute-start.2 = (bf16[2,176,2048]{2,1,0:T(8,128)(2,1)}, bf16[2,176,2048]{2,1,0:T(8,128)(2,1)}, u32[]{:S(2)}, u32[]{:S(2)}) collective-permute-start(bf16[2,176,2048]{2,1,0:T(8,128)(2,1)} %get-tuple-element.13), channel_id=1, source_target_pairs={{0,96},{32,0},{64,32},{96,64},{1,97},{33,1},{65,33},{97,65},{2,98}... | collective-permute-start | bytes 4325384 | tf_op jit(solution)/shard_map/ppermute | solution.py:99
  113.2 2.5 %copy-start.5 = (bf16[1408,2048]{1,0:T(8,128)(2,1)}, bf16[1408,2048]{1,0:T(8,128)(2,1)S(1)}, u32[]{:S(2)}) copy-start(bf16[1408,2048]{1,0:T(8,128)(2,1)S(1)} %constant_dynamic-update-slice_fusion) | copy-start | bytes 17301508
  113.2 61.8 %collective-permute-start.4 = (bf16[2,176,2048]{2,1,0:T(8,128)(2,1)S(1)}, bf16[2,176,2048]{2,1,0:T(8,128)(2,1)}, u32[]{:S(2)}, u32[]{:S(2)}) collective-permute-start(bf16[2,176,2048]{2,1,0:T(8,128)(2,1)S(1)} %collective-permute-done), channel_id=1, source_target_pairs={{0,32},{32,64},{64,96},{96,0},{1,33},{33,65},{65,97},{97,1},{2,34}... | collective-permute-start | bytes 4325384 | tf_op jit(solution)/shard_map/ppermute | solution.py:103
  115.7 60.7 %collective-permute-start.5 = (bf16[2,176,2048]{2,1,0:T(8,128)(2,1)S(1)}, bf16[2,176,2048]{2,1,0:T(8,128)(2,1)}, u32[]{:S(2)}, u32[]{:S(2)}) collective-permute-start(bf16[2,176,2048]{2,1,0:T(8,128)(2,1)S(1)} %collective-permute-done.3), channel_id=1, source_target_pairs={{0,96},{32,0},{64,32},{96,64},{1,97},{33,1},{65,33},{97,65},{2,98}... | collective-permute-start | bytes 4325384 | tf_op jit(solution)/shard_map/ppermute | solution.py:104
  119.9 12.4 %copy-start.7 = (f32[2048]{0:T(1024)S(1)}, f32[2048]{0:T(1024)}, u32[]{:S(2)}) copy-start(f32[2048]{0:T(1024)} %param.19) | copy-start | bytes 24580
  133.4 0.7 copy-start.3
  137.0 40.9 %all-to-all-start.2 = ((bf16[32,16,2048]{2,1,0:T(8,128)(2,1)}), bf16[32,16,2048]{2,1,0:T(8,128)(2,1)}, u32[]{:S(2)}, u32[]{:S(2)}) async-start(bf16[32,16,2048]{2,1,0:T(8,128)(2,1)} %bitcast.15), calls=%async_computation.2 | async-start | bytes 4194304 | tf_op jit(solution)/shard_map/all_to_all | solution.py:140
  188.8 5.4 %slice-start = ((s8[5767168]{0:T(1024)(128)(4,1)}), s8[4194304]{0:T(1024)(128)(4,1)S(1)}, s32[]{:S(2)}) async-start(s8[5767168]{0:T(1024)(128)(4,1)} %bitcast.118), calls=%async_computation.4 | async-start | bytes 8388608
  191.5 2.7 %slice-start.1 = ((s8[5767168]{0:T(1024)(128)(4,1)}), s8[1572864]{0:T(1024)(128)(4,1)S(1)}, s32[]{:S(2)}) async-start(s8[5767168]{0:T(1024)(128)(4,1)} %bitcast.118), calls=%async_computation.5 | async-start | bytes 3145728
  198.8 9.0 %copy-start.4 = (bf16[64,2048]{1,0:T(8,128)(2,1)S(1)}, bf16[64,2048]{1,0:T(8,128)(2,1)}, u32[]{:S(2)}) copy-start(bf16[64,2048]{1,0:T(8,128)(2,1)} %copy-done.3) | copy-start | bytes 786436
  198.8 37.4 %all-to-all-start.3 = ((bf16[32,16,2048]{2,1,0:T(8,128)(2,1)}), bf16[32,16,2048]{2,1,0:T(8,128)(2,1)}, u32[]{:S(2)}, u32[]{:S(2)}) async-start(bf16[32,16,2048]{2,1,0:T(8,128)(2,1)} %bitcast.31), calls=%async_computation.3 | async-start | bytes 4194304 | tf_op jit(solution)/shard_map/all_to_all | solution.py:152
  207.9 28.4 %copy-start.8 = (f32[64,6]{0,1:T(8,128)S(1)}, f32[64,6]{0,1:T(8,128)}, u32[]{:S(2)}) copy-start(f32[64,6]{0,1:T(8,128)} %param.18) | copy-start | bytes 4612
  214.3 24.7 %copy-start.1 = (f32[64,2048]{1,0:T(8,128)S(1)}, f32[64,2048]{1,0:T(8,128)}, u32[]{:S(2)}) copy-start(f32[64,2048]{1,0:T(8,128)} %shard_map.118) | copy-start | bytes 1572868
